TPU v7x, 512 devices: a whole 4x4x16 slice. The times are simulated.
512 devices in a mesh: dp: 4 (over x), ctx: 16 (over z), mp: 8 (over y, core).
Axes of the slice: x: 4, y: 4, z: 16, core: 2. Of those that a mesh axis runs over, the one named last changes fastest.
Arguments:
- tokens: bfloat16 [4, 2048, 4096], P('dp', 'ctx'), may hold values from -52 to 52
- x_weight: bfloat16 [4096, 8192], P(('dp', 'ctx'), 'mp'), may hold values from -0.09375 to 0.09375
- bc_weight: bfloat16 [4096, 1024], P(('dp', 'ctx'), 'mp'), may hold values from -0.09375 to 0.09375
- dt_weight: bfloat16 [4096, 128], P(('dp', 'ctx'), 'mp'), may hold values from -0.0234375 to 0.0234375
- conv_x: float32 [5, 8192], P(None, 'mp'), may hold values from -0.5 to 0.5
- conv_bc: float32 [5, 1024], P(None, 'mp'), may hold values from -0.5 to 0.5
- dt_bias: float32 [128], P('mp'), may hold values from -4.5 to -2.5
- a_log: float32 [128], P('mp')
- d_skip: float32 [128], P('mp'), may hold values from 0.5 to 1.5
- norm_gain: float32 [8192], P('mp'), may hold values from 0.5 to 1.5
Outputs:
- mixer_out: bfloat16 [4, 2048, 8192], P('dp', 'ctx', 'mp')
- kurtosis: float32 [4096], P('mp')
All inputs are finite; a program needn't handle non-finite values.
Results may differ from a plain program's by a relative error of at most 0.015.
Values may be sent and summed in bfloat16 or wider, within the bound.
No kernel may reach another device: no remote copies, remote signals or barrier semaphores. Data moves between devices by JAX's collectives and lax.ppermute only.
A program may use at most 64 MiB of HBM per device.

v0:
```python
import jax
import jax.numpy as jnp
from jax import lax
from jax.sharding import PartitionSpec as P

ROOT = 64
HEADS = 128
G = 4
NS = 128


HIGH = lax.Precision.HIGHEST


def passed_along(value, axis, steps):
    count = lax.axis_size(axis)
    first, last = (max(0, -steps), min(count, count - steps))
    return lax.ppermute(value, axis, [(source, source + steps) for source in range(first, last)])


def entering(array, axis, combine, identity):
    length, place = (lax.axis_size(axis), lax.axis_index(axis))
    everything = jax.tree.map(
        lambda part, kind: lax.all_gather(part.astype(kind), axis),
        array,
        (jnp.bfloat16, jnp.bfloat16),
    )
    start = jax.tree.map(
        lambda part, zero: jnp.broadcast_to(jnp.asarray(zero, part.dtype), part.shape),
        array,
        identity,
    )

    def step(k, before):
        reached = k < place
        new = combine(
            before, jax.tree.map(lambda part, own: part[k].astype(own.dtype), everything, array)
        )
        return jax.tree.map(lambda a, b: jnp.where(reached, a, b), new, before)

    return lax.fori_loop(0, length, step, start)


def hadamard_signs(sign_order):
    row_index = lax.broadcasted_iota(jnp.int32, (sign_order, sign_order), 0)
    col_index = lax.broadcasted_iota(jnp.int32, (sign_order, sign_order), 1)
    common = jnp.bitwise_and(row_index, col_index)
    parity = jnp.zeros((sign_order, sign_order), jnp.int32)
    for bit_index in range(sign_order.bit_length() - 1):
        parity = parity + jnp.bitwise_and(jnp.right_shift(common, bit_index), 1)
    return 1.0 - 2.0 * jnp.bitwise_and(parity, 1).astype(jnp.float32)


def kurtosis_from(powers, row_count):
    average = powers[0] / row_count
    second = powers[1] / row_count - average * average
    fourth = (
        powers[3] / row_count
        - 4.0 * average * powers[2] / row_count
        + 6.0 * average * average * powers[1] / row_count
        - 3.0 * average * average * average * average
    )
    return fourth / (second * second + 1e-06)


def chain_states(earlier, later):
    return (earlier[0] * later[0], later[0][:, :, None, None] * earlier[1] + later[1])


def shards(
    tokens, x_weight, bc_weight, dt_weight, conv_x, conv_bc, dt_bias, a_log, d_skip, norm_gain
):
    tok_rows = tokens.shape[1]
    model_width = tokens.shape[2]
    signs = hadamard_signs(ROOT)
    blocks = tokens.reshape(tok_rows, ROOT, ROOT)
    first_pass = jnp.einsum(
        "tab,ac->tcb", blocks, signs.astype(jnp.bfloat16), preferred_element_type=jnp.float32
    )
    second = jnp.einsum("tcb,bd->tcd", first_pass, signs, precision=HIGH)
    rotated = (second.reshape(tok_rows, model_width) / ROOT).astype(jnp.bfloat16)
    channel_share = model_width // lax.axis_size("mp")
    own_cols = lax.dynamic_slice_in_dim(
        rotated, lax.axis_index("mp") * channel_share, channel_share, 1
    ).astype(jnp.float32)
    square = own_cols * own_cols
    powers = jnp.stack(
        [
            jnp.sum(own_cols, 0),
            jnp.sum(square, 0),
            jnp.sum(square * own_cols, 0),
            jnp.sum(square * square, 0),
        ]
    )
    row_count = float(tok_rows * lax.axis_size("dp") * lax.axis_size("ctx"))
    totals = lax.psum(powers, ("dp", "ctx"))
    kurtosis = kurtosis_from(totals, row_count)
    panels = (
        lax.all_gather(x_weight, ("dp", "ctx"), axis=0, tiled=True),
        lax.all_gather(bc_weight, ("dp", "ctx"), axis=0, tiled=True),
        lax.all_gather(dt_weight, ("dp", "ctx"), axis=0, tiled=True),
    )
    projected = tuple(
        (jnp.dot(rotated, panel, preferred_element_type=jnp.float32) for panel in panels)
    )
    x_cols = x_weight.shape[1]
    joined = jnp.concatenate(
        [projected[0].astype(jnp.bfloat16), projected[1].astype(jnp.bfloat16)], 1
    )
    dt_proj = lax.optimization_barrier(projected[2].astype(jnp.bfloat16))
    conv_taps = jnp.concatenate([conv_x, conv_bc], 1)
    kernel = conv_taps.shape[0] - 1
    rim_rows = passed_along(joined[tok_rows - (kernel - 1) :], "ctx", 1)
    padded = jnp.concatenate([rim_rows, joined], 0)
    conv_sum = conv_taps[kernel]
    for tap_index in range(kernel):
        conv_sum = conv_sum + conv_taps[tap_index] * padded[tap_index : tap_index + tok_rows]
    convolved = jax.nn.silu(conv_sum).astype(jnp.bfloat16)
    x_conv = convolved[:, :x_cols]
    group_all = lax.all_gather(convolved[:, x_cols:], "mp", axis=1, tiled=True)
    heads_dev = dt_weight.shape[1]
    head_size = x_cols // heads_dev
    per_group = HEADS // G
    groups_here = max(1, heads_dev // per_group)
    heads_local = heads_dev // groups_here
    first_group = lax.axis_index("mp") * heads_dev // per_group
    write_all = group_all[:, : G * NS].reshape(tok_rows, G, NS)
    read_all = group_all[:, G * NS :].reshape(tok_rows, G, NS)
    write_here = lax.dynamic_slice_in_dim(write_all, first_group, groups_here, 1)
    read_here = lax.dynamic_slice_in_dim(read_all, first_group, groups_here, 1)
    step_size = jax.nn.softplus(dt_proj.astype(jnp.float32) + dt_bias)
    decay_rate = step_size * jnp.exp(a_log)
    cumulative = jnp.cumsum(decay_rate, 0)
    block_end = cumulative[-1]
    causal = lax.broadcasted_iota(jnp.int32, (tok_rows, tok_rows), 0) >= lax.broadcasted_iota(
        jnp.int32, (tok_rows, tok_rows), 1
    )
    spread = cumulative.T[:, :, None] - cumulative.T[:, None, :]
    decay_mask = jnp.where(causal, jnp.exp(-jnp.where(causal, spread, 0.0)), 0.0)
    scores = jnp.einsum("tgn,sgn->gts", read_here, write_here, preferred_element_type=jnp.float32)
    weights = (
        scores[:, None]
        * decay_mask.reshape(groups_here, heads_local, tok_rows, tok_rows)
        * step_size.T.reshape(groups_here, heads_local, 1, tok_rows)
    ).astype(jnp.bfloat16)
    x_heads = x_conv.reshape(tok_rows, groups_here, heads_local, head_size)
    within_block = jnp.einsum(
        "ghts,sghp->tghp", weights, x_heads, preferred_element_type=jnp.float32
    )
    update = (
        (jnp.exp(-(block_end - cumulative)) * step_size).reshape(
            tok_rows, groups_here, heads_local
        )[..., None]
        * x_heads
    ).astype(jnp.bfloat16)
    contrib = jnp.einsum("sghp,sgn->ghpn", update, write_here, preferred_element_type=jnp.float32)
    identity = (jnp.ones((groups_here, heads_local), jnp.float32), jnp.zeros_like(contrib))
    carried = entering(
        (jnp.exp(-block_end).reshape(groups_here, heads_local), contrib),
        "ctx",
        chain_states,
        identity,
    )
    from_before = jnp.exp(-cumulative).reshape(tok_rows, groups_here, heads_local)[
        ..., None
    ] * jnp.einsum("tgn,ghpn->tghp", read_here.astype(jnp.float32), carried[1], precision=HIGH)
    output_raw = (
        within_block
        + from_before
        + d_skip.reshape(groups_here, heads_local)[None, :, :, None] * x_heads.astype(jnp.float32)
    )
    mean_square = jnp.mean(output_raw * output_raw, -1, keepdims=True)
    normed = (
        output_raw
        * lax.rsqrt(mean_square + 1e-05)
        * norm_gain.reshape(groups_here, heads_local, head_size)
    )
    return (normed.reshape(1, tok_rows, x_cols).astype(jnp.bfloat16), kurtosis)


def solution(mesh):
    return jax.shard_map(
        shards,
        mesh=mesh,
        in_specs=(
            P("dp", "ctx", None),
            P(("dp", "ctx"), "mp"),
            P(("dp", "ctx"), "mp"),
            P(("dp", "ctx"), "mp"),
            P(None, "mp"),
            P(None, "mp"),
            P("mp"),
            P("mp"),
            P("mp"),
            P("mp"),
        ),
        out_specs=(P("dp", "ctx", "mp"), P("mp")),
        check_vma=False,
    )
```

profile of v0, /device:TPU:40, one launch (start us, length us, event | category | flops | bytes accessed | tf_op | source)
XLA Modules:
  0.0 531.7 jit_solution(13258673937758941600)
XLA Ops:
  8.7 1.6 copy.40
  10.3 87.8 %all-gather.2 = bf16[64,64,16]{1,2,0:T(8,128)(2,1)S(1)} all-gather(bf16[1,64,16]{1,2,0:T(8,128)(2,1)S(1)} %bitcast.105), channel_id=1, replica_groups=mesh['dp'=4,'ctx'=16,'mp'=8] {'dp','ctx'}, dimensions={0}, use_global_device_ids=true | all-gather | bytes 133120 | tf_op jit(solution)/shard_map/all_gather | solution.py:101
  99.4 3.3 multiply_convert_fusion
  103.6 49.5 %all-gather.10.cloned.1.call-done = bf16[4096,128]{1,0:T(8,128)(2,1)} async-done(((bf16[64,128]{1,0:T(8,128)(2,1)}), bf16[4096,128]{1,0:T(8,128)(2,1)}) %all-gather.10.cloned.1.call-update) | async-done | bytes 1048592 | tf_op jit(solution)/shard_map/all_gather | solution.py:100
  153.1 1.7 convolution_convert_fusion.2
  154.8 155.7 %all-gather.8.cloned.1.call-done = bf16[4096,1024]{1,0:T(8,128)(2,1)} async-done(((bf16[64,1024]{1,0:T(8,128)(2,1)}), bf16[4096,1024]{1,0:T(8,128)(2,1)}) %all-gather.8.cloned.1.call-update) | async-done | bytes 8388624 | tf_op jit(solution)/shard_map/all_gather | solution.py:99
  310.5 4.7 convolution_convert_fusion.1
  315.2 2.2 collective-permute-start
  317.7 3.0 collective-permute-done
  321.2 11.9 %all_gather.26 = bf16[128,1024]{1,0:T(8,128)(2,1)S(1)} all-gather(bf16[128,128]{1,0:T(8,128)(2,1)S(1)} %slice.84), channel_id=1, replica_groups=mesh['dp'=4,'ctx'=16,'mp'=8] {'mp'}, dimensions={1}, use_global_device_ids=true | all-gather | bytes 294912 | tf_op jit(solution)/shard_map/all_gather | solution.py:120
  334.7 25.9 %all-gather.3 = bf16[16,1,16]{2,1,0:T(2,128)(2,1)S(1)} all-gather(bf16[1,1,16]{2,1,0:T(2,128)(2,1)S(1)} %get-tuple-element.160), channel_id=2, replica_groups=mesh['dp'=4,'ctx'=16,'mp'=8] {'ctx'}, dimensions={0}, use_global_device_ids=true | all-gather | bytes 544 | tf_op jit(solution)/shard_map/all_gather | solution.py:24
  361.0 142.6 %psum.7 = f32[4,512]{1,0:T(4,128)S(1)} all-reduce(f32[4,512]{1,0:T(4,128)S(1)} %pad_maximum_fusion.1), channel_id=1, replica_groups=mesh['dp'=4,'ctx'=16,'mp'=8] {'dp','ctx'}, use_global_device_ids=true, to_apply=%region_8.9 | all-reduce | flops 2048 | bytes 16384 | tf_op jit(solution)/shard_map/psum | solution.py:96
  505.0 18.1 %while.14 = (s32[]{:T(128)}, f32[1,16,64,128]{3,2,1,0:T(8,128)S(1)}, s32[]{:T(128)}, bf16[16,1,16]{2,1,0:T(2,128)(2,1)S(1)}, bf16[16,1,16,64,128]{4,3,2,1,0:T(8,128)(2,1)}, /*index=5*/s32[]{:T(128)}, s32[]{:T(128)}) while((s32[]{:T(128)}, f32[1,16,64,128]{3,2,1,0:T(8,128)S(1)}, s32[]{:T(128)}, bf16[16,1,16]{2,1,0:T(2,128)(2,1)S(1)}, ...), condition=%wide.region_2.0_spmd.clone, body=%wide.region_1.0_spmd.clone.sunk | while | flops 655380 | bytes 1310985 | solution.py:41
  505.0 1.1 fusion.65
  506.2 1.1 fusion.65
  507.3 1.1 fusion.65
  508.4 1.1 fusion.65
  509.6 1.1 fusion.65
  510.7 1.1 fusion.65
  511.8 1.1 fusion.65
  513.0 1.1 fusion.65
  515.2 1.1 fusion.65
  516.3 1.1 fusion.65
  517.5 1.1 fusion.65
  (89 shorter events, 15.1 us)
Async XLA Ops:
  7.2 3.2 copy-start.1
  7.2 145.9 %all-gather.10.cloned.1.call-start = ((), (), s32[]{:S(2)}) async-start(), calls=%async_computation.1 | async-start | bytes 1064960 | tf_op jit(solution)/shard_map/all_gather | solution.py:100
  7.9 302.6 %all-gather.8.cloned.1.call-start = ((), (), s32[]{:S(2)}) async-start(), calls=%async_computation | async-start | bytes 8519680 | tf_op jit(solution)/shard_map/all_gather | solution.py:99
  8.7 496.3 %all-gather.12.cloned.1.call-start = ((), (), s32[]{:S(2)}) async-start(), calls=%async_computation.2 | async-start | bytes 4456448 | tf_op jit(solution)/shard_map/all_gather | solution.py:24
  99.4 3.6 copy-start.5
  99.4 3.6 copy-start.4
  99.4 4.0 copy-start
  99.4 4.1 copy-start.3
  315.2 5.6 %collective-permute-start = (bf16[3,1152]{1,0:T(4,128)(2,1)S(1)}, bf16[3,1152]{1,0:T(4,128)(2,1)S(1)}, u32[]{:S(2)}, u32[]{:S(2)}) collective-permute-start(bf16[3,1152]{1,0:T(4,128)(2,1)S(1)} %fusion.32), channel_id=1, source_target_pairs={{0,8},{8,16},{16,24},{24,32},{32,40},{40,48},{48,56},{56,64},{64,7... | collective-permute-start | bytes 20744 | tf_op jit(solution)/shard_map/ppermute | solution.py:18
  321.2 13.4 %copy-start.2 = (f32[1024]{0:T(1024)S(1)}, f32[1024]{0:T(1024)}, u32[]{:S(2)}) copy-start(f32[1024]{0:T(1024)} %param.21) | copy-start | bytes 12292
  505.0 18.5 %copy-start.6 = (f32[16]{0:T(128)S(1)}, f32[16]{0:T(128)}, u32[]{:S(2)}) copy-start(f32[16]{0:T(128)} %param.20) | copy-start | bytes 196
Sparse Core Ops, SparseCore 0:
  10.9 142.0 all-gather.9
  156.0 154.4 all-gather.7
  334.6 73.4 all-gather.11
where the time goes:
time: 533 us; the launch traced here: 532 us
  blocking collectives  268 us (50%)
  waiting for transfers between devices  210 us (39%)
  other arithmetic  19.7 us (4%)
  between operations  14.1 us (3%)
  matrix products  12.8 us (2%)
    all_gather x1, waiting for transfers between devices, shards(): lax.all_gather(x_weight, ('dp', 'ctx'), axis=0, tiled=True)  156 us
    psum x1, blocking collectives, shards(): totals = lax.psum(powers, ('dp', 'ctx'))  143 us
    all_gather x1, blocking collectives, shards(): lax.all_gather(dt_weight, ('dp', 'ctx'), axis=0, tiled=True)  87.8 us
    all_gather x1, waiting for transfers between devices, shards(): lax.all_gather(bc_weight, ('dp', 'ctx'), axis=0, tiled=True)  49.5 us
    all_gather x1, blocking collectives, entering(): lax.all_gather(part.astype(kind), axis)  25.9 us
    select_n x16, other arithmetic, step(): return jax.tree.map(lambda a, b: jnp.where(reached, a, b), new, before)  17.5 us
    all_gather x1, blocking collectives, shards(): group_all = lax.all_gather(convolved[:, x_cols:], 'mp', axis=1, tiled=True)  11.9 us
  transfers between devices with their start and end apart: 4, of which 3 were waited for; matrix products, arithmetic and copies ran while one was open for 2% of the time, Pallas kernels for 0%

commit v1 on v0

--- a/solution.py
+++ b/solution.py
@@ -18,27 +18,22 @@
     return lax.ppermute(value, axis, [(source, source + steps) for source in range(first, last)])
 
 
-def entering(array, axis, combine, identity):
+def entering(decay, contrib, axis):
     length, place = (lax.axis_size(axis), lax.axis_index(axis))
-    everything = jax.tree.map(
-        lambda part, kind: lax.all_gather(part.astype(kind), axis),
-        array,
-        (jnp.bfloat16, jnp.bfloat16),
-    )
-    start = jax.tree.map(
-        lambda part, zero: jnp.broadcast_to(jnp.asarray(zero, part.dtype), part.shape),
-        array,
-        identity,
-    )
-
-    def step(k, before):
-        reached = k < place
-        new = combine(
-            before, jax.tree.map(lambda part, own: part[k].astype(own.dtype), everything, array)
-        )
-        return jax.tree.map(lambda a, b: jnp.where(reached, a, b), new, before)
-
-    return lax.fori_loop(0, length, step, start)
+    lanes = contrib.shape[-1]
+    rows = contrib.size // lanes
+    tail = jnp.zeros((8, lanes), jnp.float32).at[0, : decay.size].set(decay.reshape(-1))
+    flat = jnp.concatenate([contrib.reshape(rows, lanes), tail]).astype(jnp.bfloat16)
+    everything = lax.all_gather(flat, axis).astype(jnp.float32)
+    states = everything[:, :rows].reshape((length,) + contrib.shape)
+    decays = everything[:, rows, : decay.size].reshape((length,) + decay.shape)
+    source = lax.broadcasted_iota(jnp.int32, (length, length), 0)
+    between = lax.broadcasted_iota(jnp.int32, (length, length), 1)
+    inside = jnp.logical_and(between > source, between < place)
+    factors = jnp.where(inside[:, :, None, None], decays[None], 1.0)
+    weights = jnp.prod(factors, 1)
+    weights = jnp.where((source[:, 0] < place)[:, None, None], weights, 0.0)
+    return jnp.einsum("jgh,jghpn->ghpn", weights, states, precision=HIGH)
 
 
 def hadamard_signs(sign_order):
@@ -61,10 +56,6 @@
         - 3.0 * average * average * average * average
     )
     return fourth / (second * second + 1e-06)
-
-
-def chain_states(earlier, later):
-    return (earlier[0] * later[0], later[0][:, :, None, None] * earlier[1] + later[1])
 
 
 def shards(
@@ -93,16 +84,15 @@
         ]
     )
     row_count = float(tok_rows * lax.axis_size("dp") * lax.axis_size("ctx"))
-    totals = lax.psum(powers, ("dp", "ctx"))
+    totals = lax.psum(lax.psum(powers, "ctx"), "dp")
+    totals, rotated = lax.optimization_barrier((totals, rotated))
     kurtosis = kurtosis_from(totals, row_count)
-    panels = (
-        lax.all_gather(x_weight, ("dp", "ctx"), axis=0, tiled=True),
-        lax.all_gather(bc_weight, ("dp", "ctx"), axis=0, tiled=True),
-        lax.all_gather(dt_weight, ("dp", "ctx"), axis=0, tiled=True),
-    )
-    projected = tuple(
-        (jnp.dot(rotated, panel, preferred_element_type=jnp.float32) for panel in panels)
-    )
+    local_panel = jnp.concatenate([x_weight, bc_weight, dt_weight], 1)
+    panel = lax.all_gather(local_panel, ("dp", "ctx"), axis=0, tiled=True)
+    both = jnp.dot(rotated, panel, preferred_element_type=jnp.float32)
+    x_end = x_weight.shape[1]
+    bc_end = x_end + bc_weight.shape[1]
+    projected = (both[:, :x_end], both[:, x_end:bc_end], both[:, bc_end:])
     x_cols = x_weight.shape[1]
     joined = jnp.concatenate(
         [projected[0].astype(jnp.bfloat16), projected[1].astype(jnp.bfloat16)], 1
@@ -154,16 +144,10 @@
         * x_heads
     ).astype(jnp.bfloat16)
     contrib = jnp.einsum("sghp,sgn->ghpn", update, write_here, preferred_element_type=jnp.float32)
-    identity = (jnp.ones((groups_here, heads_local), jnp.float32), jnp.zeros_like(contrib))
-    carried = entering(
-        (jnp.exp(-block_end).reshape(groups_here, heads_local), contrib),
-        "ctx",
-        chain_states,
-        identity,
-    )
+    carried = entering(jnp.exp(-block_end).reshape(groups_here, heads_local), contrib, "ctx")
     from_before = jnp.exp(-cumulative).reshape(tok_rows, groups_here, heads_local)[
         ..., None
-    ] * jnp.einsum("tgn,ghpn->tghp", read_here.astype(jnp.float32), carried[1], precision=HIGH)
+    ] * jnp.einsum("tgn,ghpn->tghp", read_here.astype(jnp.float32), carried, precision=HIGH)
     output_raw = (
         within_block
         + from_before

time: 533 us -> 302 us (0.57)
  the two profiles are of different devices: /device:TPU:40 before, /device:TPU:6 now
where the time goes in v1:
time: 302 us
  waiting for transfers between devices  196 us (65%)
  blocking collectives  58.1 us (19%)
  matrix products  17.2 us (6%)
  between operations  14.4 us (5%)
  other arithmetic  6.37 us (2%)
  local copies, waits for them, and re-layouts  6.17 us (2%)
  starting transfers between devices  3.7 us (1%)
    all_gather x1, waiting for transfers between devices, shards(): panel = lax.all_gather(local_panel, ('dp', 'ctx'), axis=0, tiled=True)  117 us
    all_gather x1, waiting for transfers between devices, entering(): everything = lax.all_gather(flat, axis).astype(jnp.float32)  75.5 us
    psum x2, blocking collectives, shards(): totals = lax.psum(lax.psum(powers, 'ctx'), 'dp')  44.7 us
    all_gather x1, blocking collectives, shards(): group_all = lax.all_gather(convolved[:, x_cols:], 'mp', axis=1, tiled=True)  13.4 us
    dot_general x1, matrix products, shards(): both = jnp.dot(rotated, panel, preferred_element_type=jnp.float32)  8.01 us
  transfers between devices with their start and end apart: 3, of which 3 were waited for; matrix products, arithmetic and copies ran while one was open for 2% of the time, Pallas kernels for 0%

profile of v1, /device:TPU:6, one launch (start us, length us, event | category | flops | bytes accessed | tf_op | source)
XLA Modules:
  0.0 302.0 jit_solution(1857820000837005802)
XLA Ops:
  7.2 0.8 copy.43
  8.0 1.6 pad_maximum_fusion.1
  9.7 1.6 copy.40
  11.3 0.9 convolution_bitcast_fusion
  12.2 3.3 %multiply_convert_fusion = bf16[128,64,64]{0,2,1:T(8,128)(2,1)S(1)} fusion(f32[128,64,64]{0,1,2:T(8,128)S(1)} %convolution_bitcast_fusion), kind=kOutput, calls=%fused_computation.5 | convolution fusion | flops 403791872 | bytes 3145728 | tf_op jit(solution)/shard_map/tcb,bd->tcd/dot_general | solution.py:71
  15.6 0.3 convert_reduce_fusion
  15.9 37.1 %psum.14 = f32[4,512]{1,0:T(4,128)S(1)} all-reduce(f32[4,512]{1,0:T(4,128)S(1)} %pad_maximum_fusion.2), channel_id=1, replica_groups=mesh['dp'=4,'ctx'=16,'mp'=8] {'ctx'}, use_global_device_ids=true, to_apply=%region_4.0 | all-reduce | flops 2048 | bytes 16384 | tf_op jit(solution)/shard_map/psum | solution.py:87
  53.1 7.6 %psum.15 = f32[4,512]{1,0:T(4,128)S(1)} all-reduce(f32[4,512]{1,0:T(4,128)S(1)} %psum.14), channel_id=1, replica_groups=mesh['dp'=4,'ctx'=16,'mp'=8] {'dp'}, use_global_device_ids=true, to_apply=%region_5.0 | all-reduce | flops 2048 | bytes 16384 | tf_op jit(solution)/shard_map/psum | solution.py:87
  60.8 116.5 %all-gather.3.cloned.1.call-done = bf16[4096,1168]{1,0:T(8,128)(2,1)} async-done(((bf16[64,1168]{1,0:T(8,128)(2,1)}), bf16[4096,1168]{1,0:T(8,128)(2,1)}) %all-gather.3.cloned.1.call-update) | async-done | bytes 9568272 | tf_op jit(solution)/shard_map/all_gather | solution.py:91
  177.4 8.0 %convolution_convert_fusion = bf16[128,1168]{0,1:T(8,128)(2,1)S(1)} fusion(bf16[128,4096]{0,1:T(8,128)(2,1)S(1)} %bitcast.81, bf16[4096,1168]{1,0:T(8,128)(2,1)} %all-gather.3.cloned.1.call-done), kind=kOutput, calls=%fused_computation.2 | convolution fusion | flops 1224886272 | bytes 10915840 | tf_op jit(solution)/shard_map/dot_general | solution.py:92
  186.0 3.6 %collective-permute-start = (bf16[3,1152]{0,1:T(8,128)(2,1)S(1)}, bf16[3,1152]{0,1:T(8,128)(2,1)S(1)}, u32[]{:S(2)}, u32[]{:S(2)}) collective-permute-start(bf16[3,1152]{0,1:T(8,128)(2,1)S(1)} %slice.121), channel_id=1, source_target_pairs={{0,8},{8,16},{16,24},{24,32},{32,40},{40,48},{48,56},{56,64},{64,7... | collective-permute-start | bytes 20744 | tf_op jit(solution)/shard_map/ppermute | solution.py:18
  189.7 4.1 %collective-permute-done = bf16[3,1152]{0,1:T(8,128)(2,1)S(1)} collective-permute-done((bf16[3,1152]{0,1:T(8,128)(2,1)S(1)}, bf16[3,1152]{0,1:T(8,128)(2,1)S(1)}, u32[]{:S(2)}, u32[]{:S(2)}) %collective-permute-start) | collective-permute-done | bytes 6944 | tf_op jit(solution)/shard_map/ppermute | solution.py:18
  193.8 1.4 multiply_convert_fusion.2
  195.3 13.4 %all_gather.11 = bf16[128,1024]{0,1:T(8,128)(2,1)S(1)} all-gather(bf16[128,128]{0,1:T(8,128)(2,1)S(1)} %slice.131), channel_id=1, replica_groups=mesh['dp'=4,'ctx'=16,'mp'=8] {'mp'}, dimensions={1}, use_global_device_ids=true | all-gather | bytes 294912 | tf_op jit(solution)/shard_map/all_gather | solution.py:110
  208.7 0.2 fusion.9
  209.0 0.7 fusion.22
  209.9 0.6 fusion.39
  210.8 75.5 %all-gather.5.cloned.1.call-done = bf16[16,1032,128]{2,1,0:T(8,128)(2,1)} async-done(((bf16[1,1032,128]{2,1,0:T(8,128)(2,1)}), bf16[16,1032,128]{2,1,0:T(8,128)(2,1)}) %all-gather.5.cloned.1.call-update) | async-done | bytes 4227088 | tf_op jit(solution)/shard_map/all_gather | solution.py:27
  286.3 0.8 slice_convert_fusion
  287.4 2.2 slice-done
  289.5 3.5 %fusion = f32[16,1,64,128]{3,1,2,0:T(1,128)S(1)} fusion(f32[16,16,1,1]{0,2,3,1:T(1,128)S(1)} %copy.51, bf16[16,16,64,128]{3,2,1,0:T(8,128)(2,1)S(1)} %bitcast.79), kind=kOutput, calls=%fused_computation | convolution fusion | flops 25165824 | bytes 4719616 | tf_op jit(solution)/shard_map/jgh,jghpn->ghpn/dot_general | solution.py:36
  293.1 0.4 fusion.8
  293.5 0.6 multiply_reduce_fusion
  294.3 0.9 copy.50
  (53 shorter events, 1.9 us)
Async XLA Ops:
  7.2 170.2 %all-gather.3.cloned.1.call-start = ((), (), s32[]{:S(2)}) async-start(), calls=%async_computation | async-start | bytes 10649600 | tf_op jit(solution)/shard_map/all_gather | solution.py:91
  9.6 276.7 %all-gather.5.cloned.1.call-start = ((), (), s32[]{:S(2)}) async-start(), calls=%async_computation.1 | async-start | bytes 4491264 | tf_op jit(solution)/shard_map/all_gather | solution.py:27
  9.7 51.0 %copy-start.5 = (f32[16]{0:T(128)S(1)}, f32[16]{0:T(128)}, u32[]{:S(2)}) copy-start(f32[16]{0:T(128)} %param.19) | copy-start | bytes 196
  9.7 51.0 %copy-start.1 = (f32[5,1024]{1,0:T(8,128)S(1)}, f32[5,1024]{1,0:T(8,128)}, u32[]{:S(2)}) copy-start(f32[5,1024]{1,0:T(8,128)} %param.16) | copy-start | bytes 61444
  9.7 51.0 %copy-start.3 = (f32[5,128]{1,0:T(8,128)S(1)}, f32[5,128]{1,0:T(8,128)}, u32[]{:S(2)}) copy-start(f32[5,128]{1,0:T(8,128)} %param.17) | copy-start | bytes 7684
  60.8 124.7 %copy-start.4 = (f32[16]{0:T(128)S(1)}, f32[16]{0:T(128)}, u32[]{:S(2)}) copy-start(f32[16]{0:T(128)} %param.18) | copy-start | bytes 196
  185.4 24.4 %copy-start.2 = (f32[1024]{0:T(1024)S(1)}, f32[1024]{0:T(1024)}, u32[]{:S(2)}) copy-start(f32[1024]{0:T(1024)} %param.21) | copy-start | bytes 12292
  186.0 7.8 %collective-permute-start = (bf16[3,1152]{0,1:T(8,128)(2,1)S(1)}, bf16[3,1152]{0,1:T(8,128)(2,1)S(1)}, u32[]{:S(2)}, u32[]{:S(2)}) collective-permute-start(bf16[3,1152]{0,1:T(8,128)(2,1)S(1)} %slice.121), channel_id=1, source_target_pairs={{0,8},{8,16},{16,24},{24,32},{32,40},{40,48},{48,56},{56,64},{64,7... | collective-permute-start | bytes 20744 | tf_op jit(solution)/shard_map/ppermute | solution.py:18
  195.3 92.1 %copy-start = (bf16[128,1152]{0,1:T(8,128)(2,1)}, bf16[128,1152]{0,1:T(8,128)(2,1)S(1)}, u32[]{:S(2)}) copy-start(bf16[128,1152]{0,1:T(8,128)(2,1)S(1)} %multiply_convert_fusion.2) | copy-start | bytes 884740
  287.4 2.2 slice-start
  287.4 6.1 %copy-start.6 = (f32[16]{0:T(128)S(1)}, f32[16]{0:T(128)}, u32[]{:S(2)}) copy-start(f32[16]{0:T(128)} %param.20) | copy-start | bytes 196
  289.5 3.9 %slice-start.1 = ((bf16[128,1152]{0,1:T(8,128)(2,1)}), bf16[128,1024]{0,1:T(8,128)(2,1)S(1)}, s32[]{:S(2)}) async-start(bf16[128,1152]{0,1:T(8,128)(2,1)} %copy-done), calls=%async_computation.3 | async-start | bytes 524288 | tf_op jit(solution)/shard_map/slice | solution.py:109
Sparse Core Ops, SparseCore 0:
  11.5 165.7 all-gather.2
  209.9 76.4 all-gather.4

commit v2 on v1

--- a/solution.py
+++ b/solution.py
@@ -88,8 +88,13 @@
     totals, rotated = lax.optimization_barrier((totals, rotated))
     kurtosis = kurtosis_from(totals, row_count)
     local_panel = jnp.concatenate([x_weight, bc_weight, dt_weight], 1)
-    panel = lax.all_gather(local_panel, ("dp", "ctx"), axis=0, tiled=True)
-    both = jnp.dot(rotated, panel, preferred_element_type=jnp.float32)
+    panel = lax.all_gather(local_panel, "ctx", axis=0, tiled=True)
+    seqs = lax.axis_size("dp")
+    share = model_width // seqs
+    outgoing = rotated.reshape(tok_rows, seqs, share).transpose(1, 0, 2)
+    incoming = lax.all_to_all(outgoing, "dp", 0, 0)
+    partials = jnp.einsum("kti,io->kto", incoming, panel, preferred_element_type=jnp.float32)
+    both = lax.psum_scatter(partials, "dp", scatter_dimension=0, tiled=False)
     x_end = x_weight.shape[1]
     bc_end = x_end + bc_weight.shape[1]
     projected = (both[:, :x_end], both[:, x_end:bc_end], both[:, bc_end:])

time: 302 us -> 255 us (0.84)
  waiting for transfers between devices: 196 us -> 136 us
  blocking collectives: 58.1 us -> 72.9 us
  matrix products: 17.2 us -> 13.8 us
    all_gather x1, waiting for transfers between devices: 117 us -> 14.1 us  [shards(): panel = lax.all_gather(local_panel, 'ctx', axis=0, tiled=True)]
    reduce_scatter x0 -> x1, waiting for transfers between devices: none -> 34.5 us  [shards(): both = lax.psum_scatter(partials, 'dp', scatter_dimension=0, tiled=False)]
    all_to_all x0 -> x1, blocking collectives: none -> 14.8 us  [shards(): incoming = lax.all_to_all(outgoing, 'dp', 0, 0)]
    all_gather x1, waiting for transfers between devices: 75.5 us -> 81.1 us  [entering(): everything = lax.all_gather(flat, axis).astype(jnp.float32)]
    dot_general x1, matrix products: 8.01 us -> 4.6 us  [shards(): jnp.einsum('kti,io->kto', incoming, panel, preferred_element_type=jnp.flo...]
  transfers between devices with their start and end apart: 3 -> 4, of which waited for: 3 -> 4; matrix products, arithmetic and copies ran while one was open for 2% -> 3% of each run, Pallas kernels for 0% -> 0%
where the time goes in v2:
time: 255 us; the launch traced here: 254 us
  waiting for transfers between devices  136 us (53%)
  blocking collectives  72.9 us (29%)
  between operations  14.1 us (6%)
  matrix products  13.8 us (5%)
  other arithmetic  7.49 us (3%)
  local copies, waits for them, and re-layouts  6.69 us (3%)
  starting transfers between devices  3.6 us (1%)
    all_gather x1, waiting for transfers between devices, entering(): everything = lax.all_gather(flat, axis).astype(jnp.float32)  81.1 us
    psum x2, blocking collectives, shards(): totals = lax.psum(lax.psum(powers, 'ctx'), 'dp')  44.7 us
    reduce_scatter x1, waiting for transfers between devices, shards(): both = lax.psum_scatter(partials, 'dp', scatter_dimension=0, tiled=False)  34.5 us
    all_to_all x1, blocking collectives, shards(): incoming = lax.all_to_all(outgoing, 'dp', 0, 0)  14.8 us
    all_gather x1, waiting for transfers between devices, shards(): panel = lax.all_gather(local_panel, 'ctx', axis=0, tiled=True)  14.1 us
    all_gather x1, blocking collectives, shards(): group_all = lax.all_gather(convolved[:, x_cols:], 'mp', axis=1, tiled=True)  13.4 us
    ppermute x1, waiting for transfers between devices, passed_along(): lax.ppermute(value, axis, [(source, source + steps) for source in range(f...  6.15 us
  transfers between devices with their start and end apart: 4, of which 4 were waited for; matrix products, arithmetic and copies ran while one was open for 3% of the time, Pallas kernels for 0%

profile of v2, /device:TPU:6, one launch (start us, length us, event | category | flops | bytes accessed | tf_op | source)
XLA Modules:
  0.0 254.4 jit_solution(2780219498483063899)
XLA Ops:
  7.2 0.8 copy.46
  8.0 1.6 pad_maximum_fusion.1
  9.7 1.6 copy.42
  11.3 0.9 convolution_bitcast_fusion
  12.2 3.3 %multiply_convert_fusion = bf16[128,64,64]{0,2,1:T(8,128)(2,1)S(1)} fusion(f32[128,64,64]{0,1,2:T(8,128)S(1)} %convolution_bitcast_fusion), kind=kOutput, calls=%fused_computation.6 | convolution fusion | flops 403791872 | bytes 3145728 | tf_op jit(solution)/shard_map/tcb,bd->tcd/dot_general | solution.py:71
  15.9 37.1 %psum.14 = f32[4,512]{1,0:T(4,128)S(1)} all-reduce(f32[4,512]{1,0:T(4,128)S(1)} %pad_maximum_fusion.2), channel_id=1, replica_groups=mesh['dp'=4,'ctx'=16,'mp'=8] {'ctx'}, use_global_device_ids=true, to_apply=%region_4.0 | all-reduce | flops 2048 | bytes 16384 | tf_op jit(solution)/shard_map/psum | solution.py:87
  53.0 7.6 %psum.15 = f32[4,512]{1,0:T(4,128)S(1)} all-reduce(f32[4,512]{1,0:T(4,128)S(1)} %psum.14), channel_id=1, replica_groups=mesh['dp'=4,'ctx'=16,'mp'=8] {'dp'}, use_global_device_ids=true, to_apply=%region_5.0 | all-reduce | flops 2048 | bytes 16384 | tf_op jit(solution)/shard_map/psum | solution.py:87
  61.2 14.8 %all_to_all.5 = bf16[4,128,1024]{2,1,0:T(8,128)(2,1)S(1)} all-to-all(bf16[4,128,1024]{2,1,0:T(8,128)(2,1)S(1)} %bitcast.89), channel_id=1, replica_groups=mesh['dp'=4,'ctx'=16,'mp'=8] {'dp'}, dimensions={0} | all-to-all | bytes 2097152 | tf_op jit(solution)/shard_map/all_to_all | solution.py:95
  75.9 14.1 %all-gather.3.cloned.1.call-done = bf16[1024,1168]{1,0:T(8,128)(2,1)} async-done(((bf16[64,1168]{1,0:T(8,128)(2,1)}), bf16[1024,1168]{1,0:T(8,128)(2,1)}) %all-gather.3.cloned.1.call-update) | async-done | bytes 2392080 | tf_op jit(solution)/shard_map/all_gather | solution.py:91
  90.1 4.6 %fusion.2 = f32[4,128,1168]{1,2,0:T(8,128)} fusion(bf16[4,128,1024]{2,1,0:T(8,128)(2,1)S(1)} %all_to_all.5, bf16[1024,1168]{1,0:T(8,128)(2,1)} %all-gather.3.cloned.1.call-done), kind=kOutput, calls=%fused_computation.2 | convolution fusion | flops 1224736768 | bytes 5832704 | tf_op jit(solution)/shard_map/kti,io->kto/dot_general | solution.py:96
  94.9 34.5 %reduce-scatter.2.cloned.1.call-done = f32[1,128,1168]{1,2,0:T(8,128)} async-done(((f32[4,128,1168]{1,2,0:T(8,128)}), f32[1,128,1168]{1,2,0:T(8,128)}) %reduce-scatter.2.cloned.1.call-update) | async-done | bytes 598032 | tf_op jit(solution)/shard_map/reduce_scatter | solution.py:97
  129.4 1.1 convert_bitcast_fusion
  131.2 3.5 %collective-permute-start = (bf16[3,1152]{0,1:T(8,128)(2,1)S(1)}, bf16[3,1152]{0,1:T(8,128)(2,1)S(1)}, u32[]{:S(2)}, u32[]{:S(2)}) collective-permute-start(bf16[3,1152]{0,1:T(8,128)(2,1)S(1)} %slice.121), channel_id=1, source_target_pairs={{0,8},{8,16},{16,24},{24,32},{32,40},{40,48},{48,56},{56,64},{64,7... | collective-permute-start | bytes 20744 | tf_op jit(solution)/shard_map/ppermute | solution.py:18
  134.8 6.2 %collective-permute-done = bf16[3,1152]{0,1:T(8,128)(2,1)S(1)} collective-permute-done((bf16[3,1152]{0,1:T(8,128)(2,1)S(1)}, bf16[3,1152]{0,1:T(8,128)(2,1)S(1)}, u32[]{:S(2)}, u32[]{:S(2)}) %collective-permute-start) | collective-permute-done | bytes 6944 | tf_op jit(solution)/shard_map/ppermute | solution.py:18
  140.9 1.4 multiply_convert_fusion.2
  142.4 13.4 %all_gather.11 = bf16[128,1024]{0,1:T(8,128)(2,1)S(1)} all-gather(bf16[128,128]{0,1:T(8,128)(2,1)S(1)} %slice.131), channel_id=1, replica_groups=mesh['dp'=4,'ctx'=16,'mp'=8] {'mp'}, dimensions={1}, use_global_device_ids=true | all-gather | bytes 294912 | tf_op jit(solution)/shard_map/all_gather | solution.py:115
  156.1 0.7 fusion.24
  157.0 0.6 fusion.41
  158.0 81.1 %all-gather.5.cloned.1.call-done = bf16[16,1032,128]{2,1,0:T(8,128)(2,1)} async-done(((bf16[1,1032,128]{2,1,0:T(8,128)(2,1)}), bf16[16,1032,128]{2,1,0:T(8,128)(2,1)}) %all-gather.5.cloned.1.call-update) | async-done | bytes 4227088 | tf_op jit(solution)/shard_map/all_gather | solution.py:27
  239.0 0.8 slice_convert_fusion
  240.1 2.2 slice-done
  242.3 3.6 %fusion = f32[16,1,64,128]{3,1,2,0:T(1,128)S(1)} fusion(f32[16,16,1,1]{0,2,3,1:T(1,128)S(1)} %copy.54, bf16[16,16,64,128]{3,2,1,0:T(8,128)(2,1)S(1)} %bitcast.85), kind=kOutput, calls=%fused_computation | convolution fusion | flops 25165824 | bytes 4719616 | tf_op jit(solution)/shard_map/jgh,jghpn->ghpn/dot_general | solution.py:36
  246.2 0.6 multiply_reduce_fusion
  247.1 0.9 copy.53
  (59 shorter events, 3.5 us)
Async XLA Ops:
  7.2 82.9 %all-gather.3.cloned.1.call-start = ((), (), s32[]{:S(2)}) async-start(), calls=%async_computation.2 | async-start | bytes 2785280 | tf_op jit(solution)/shard_map/all_gather | solution.py:91
  9.6 119.8 %reduce-scatter.2.cloned.1.call-start = ((), (), s32[]{:S(2)}) async-start(), calls=%async_computation.3 | async-start | bytes 2990080 | tf_op jit(solution)/shard_map/reduce_scatter | solution.py:97
  75.9 18.9 %copy-start.5 = (f32[16]{0:T(128)S(1)}, f32[16]{0:T(128)}, u32[]{:S(2)}) copy-start(f32[16]{0:T(128)} %param.19) | copy-start | bytes 196
  75.9 18.9 %copy-start.1 = (f32[5,1024]{1,0:T(8,128)S(1)}, f32[5,1024]{1,0:T(8,128)}, u32[]{:S(2)}) copy-start(f32[5,1024]{1,0:T(8,128)} %param.16) | copy-start | bytes 61444
  75.9 18.9 %copy-start.3 = (f32[5,128]{1,0:T(8,128)S(1)}, f32[5,128]{1,0:T(8,128)}, u32[]{:S(2)}) copy-start(f32[5,128]{1,0:T(8,128)} %param.17) | copy-start | bytes 7684
  94.7 35.9 %copy-start.4 = (f32[16]{0:T(128)S(1)}, f32[16]{0:T(128)}, u32[]{:S(2)}) copy-start(f32[16]{0:T(128)} %param.18) | copy-start | bytes 196
  94.7 144.3 %all-gather.5.cloned.1.call-start = ((), (), s32[]{:S(2)}) async-start(), calls=%async_computation.4 | async-start | bytes 4491264 | tf_op jit(solution)/shard_map/all_gather | solution.py:27
  130.5 26.3 %copy-start.2 = (f32[1024]{0:T(1024)S(1)}, f32[1024]{0:T(1024)}, u32[]{:S(2)}) copy-start(f32[1024]{0:T(1024)} %param.21) | copy-start | bytes 12292
  131.2 9.8 %collective-permute-start = (bf16[3,1152]{0,1:T(8,128)(2,1)S(1)}, bf16[3,1152]{0,1:T(8,128)(2,1)S(1)}, u32[]{:S(2)}, u32[]{:S(2)}) collective-permute-start(bf16[3,1152]{0,1:T(8,128)(2,1)S(1)} %slice.121), channel_id=1, source_target_pairs={{0,8},{8,16},{16,24},{24,32},{32,40},{40,48},{48,56},{56,64},{64,7... | collective-permute-start | bytes 20744 | tf_op jit(solution)/shard_map/ppermute | solution.py:18
  142.4 97.7 %copy-start = (bf16[128,1152]{0,1:T(8,128)(2,1)}, bf16[128,1152]{0,1:T(8,128)(2,1)S(1)}, u32[]{:S(2)}) copy-start(bf16[128,1152]{0,1:T(8,128)(2,1)S(1)} %multiply_convert_fusion.2) | copy-start | bytes 884740
  240.1 2.2 slice-start
  242.3 3.9 %slice-start.1 = ((bf16[128,1152]{0,1:T(8,128)(2,1)}), bf16[128,1024]{0,1:T(8,128)(2,1)S(1)}, s32[]{:S(2)}) async-start(bf16[128,1152]{0,1:T(8,128)(2,1)} %copy-done), calls=%async_computation.6 | async-start | bytes 524288 | tf_op jit(solution)/shard_map/slice | solution.py:114
  242.3 3.9 %copy-start.6 = (f32[16]{0:T(128)S(1)}, f32[16]{0:T(128)}, u32[]{:S(2)}) copy-start(f32[16]{0:T(128)} %param.20) | copy-start | bytes 196
Sparse Core Ops, SparseCore 0:
  10.7 79.3 all-gather.2
  94.8 34.5 reduce-scatter.1
  157.0 82.0 all-gather.4

commit v3 on v2

--- a/solution.py
+++ b/solution.py
@@ -19,21 +19,31 @@
 
 
 def entering(decay, contrib, axis):
-    length, place = (lax.axis_size(axis), lax.axis_index(axis))
+    count, place = (lax.axis_size(axis), lax.axis_index(axis))
     lanes = contrib.shape[-1]
-    rows = contrib.size // lanes
-    tail = jnp.zeros((8, lanes), jnp.float32).at[0, : decay.size].set(decay.reshape(-1))
-    flat = jnp.concatenate([contrib.reshape(rows, lanes), tail]).astype(jnp.bfloat16)
-    everything = lax.all_gather(flat, axis).astype(jnp.float32)
-    states = everything[:, :rows].reshape((length,) + contrib.shape)
-    decays = everything[:, rows, : decay.size].reshape((length,) + decay.shape)
-    source = lax.broadcasted_iota(jnp.int32, (length, length), 0)
-    between = lax.broadcasted_iota(jnp.int32, (length, length), 1)
-    inside = jnp.logical_and(between > source, between < place)
-    factors = jnp.where(inside[:, :, None, None], decays[None], 1.0)
-    weights = jnp.prod(factors, 1)
-    weights = jnp.where((source[:, 0] < place)[:, None, None], weights, 0.0)
-    return jnp.einsum("jgh,jghpn->ghpn", weights, states, precision=HIGH)
+    head_rows = contrib.shape[-2]
+    heads = decay.size
+    chunk = contrib.size // lanes // count
+    pieces = contrib.reshape(count, chunk, lanes)
+    tail = jnp.zeros((count, 8, lanes), jnp.float32)
+    tail = tail.at[:, 0, :heads].set(jnp.broadcast_to(decay.reshape(1, heads), (count, heads)))
+    outgoing = jnp.concatenate([pieces, tail], 1).astype(jnp.bfloat16)
+    incoming = lax.all_to_all(outgoing, axis, 0, 0).astype(jnp.float32)
+    states = incoming[:, :chunk]
+    decays = incoming[:, chunk, :heads]
+    row_head = (place * chunk + lax.broadcasted_iota(jnp.int32, (chunk, heads), 0)) // head_rows
+    pick = row_head == lax.broadcasted_iota(jnp.int32, (chunk, heads), 1)
+    row_decay = jnp.sum(jnp.where(pick[None], decays[:, None, :], 0.0), -1)
+    target = lax.broadcasted_iota(jnp.int32, (count, count, count), 0)
+    source = lax.broadcasted_iota(jnp.int32, (count, count, count), 1)
+    between = lax.broadcasted_iota(jnp.int32, (count, count, count), 2)
+    inside = jnp.logical_and(between > source, between < target)
+    factors = jnp.where(inside[..., None], row_decay[None, None], 1.0)
+    weights = jnp.prod(factors, 2)
+    weights = jnp.where((source[:, :, 0] < target[:, :, 0])[..., None], weights, 0.0)
+    carried = jnp.einsum("kjr,jrl->krl", weights, states, precision=HIGH)
+    returned = lax.all_to_all(carried, axis, 0, 0)
+    return returned.reshape(contrib.shape)
 
 
 def hadamard_signs(sign_order):
@@ -91,38 +101,51 @@
     panel = lax.all_gather(local_panel, "ctx", axis=0, tiled=True)
     seqs = lax.axis_size("dp")
     share = model_width // seqs
-    outgoing = rotated.reshape(tok_rows, seqs, share).transpose(1, 0, 2)
+    rim = 8
+    earlier = passed_along(rotated[tok_rows - rim :], "ctx", 1)
+    extended = jnp.concatenate([earlier, rotated], 0)
+    outgoing = extended.reshape(tok_rows + rim, seqs, share).transpose(1, 0, 2)
     incoming = lax.all_to_all(outgoing, "dp", 0, 0)
     partials = jnp.einsum("kti,io->kto", incoming, panel, preferred_element_type=jnp.float32)
-    both = lax.psum_scatter(partials, "dp", scatter_dimension=0, tiled=False)
+    both_ext = lax.psum_scatter(partials, "dp", scatter_dimension=0, tiled=False)
+    both = both_ext[rim:]
     x_end = x_weight.shape[1]
     bc_end = x_end + bc_weight.shape[1]
     projected = (both[:, :x_end], both[:, x_end:bc_end], both[:, bc_end:])
     x_cols = x_weight.shape[1]
-    joined = jnp.concatenate(
-        [projected[0].astype(jnp.bfloat16), projected[1].astype(jnp.bfloat16)], 1
-    )
+    joined_ext = both_ext[:, :bc_end].astype(jnp.bfloat16)
     dt_proj = lax.optimization_barrier(projected[2].astype(jnp.bfloat16))
     conv_taps = jnp.concatenate([conv_x, conv_bc], 1)
     kernel = conv_taps.shape[0] - 1
-    rim_rows = passed_along(joined[tok_rows - (kernel - 1) :], "ctx", 1)
-    padded = jnp.concatenate([rim_rows, joined], 0)
+    padded = joined_ext[rim - (kernel - 1) :]
     conv_sum = conv_taps[kernel]
     for tap_index in range(kernel):
         conv_sum = conv_sum + conv_taps[tap_index] * padded[tap_index : tap_index + tok_rows]
     convolved = jax.nn.silu(conv_sum).astype(jnp.bfloat16)
     x_conv = convolved[:, :x_cols]
-    group_all = lax.all_gather(convolved[:, x_cols:], "mp", axis=1, tiled=True)
     heads_dev = dt_weight.shape[1]
     head_size = x_cols // heads_dev
     per_group = HEADS // G
     groups_here = max(1, heads_dev // per_group)
     heads_local = heads_dev // groups_here
     first_group = lax.axis_index("mp") * heads_dev // per_group
-    write_all = group_all[:, : G * NS].reshape(tok_rows, G, NS)
-    read_all = group_all[:, G * NS :].reshape(tok_rows, G, NS)
-    write_here = lax.dynamic_slice_in_dim(write_all, first_group, groups_here, 1)
-    read_here = lax.dynamic_slice_in_dim(read_all, first_group, groups_here, 1)
+    bc_own = convolved[:, x_cols:]
+    mp_count = lax.axis_size("mp")
+    if bc_own.shape[1] == NS and mp_count == 2 * G and groups_here == 1:
+        owner = [m * heads_dev // per_group for m in range(mp_count)]
+        odd_first = [(owner[m] if m % 2 == 0 else G + owner[m], m) for m in range(mp_count)]
+        even_first = [(G + owner[m] if m % 2 == 0 else owner[m], m) for m in range(mp_count)]
+        got_a = lax.ppermute(bc_own, "mp", odd_first)
+        got_b = lax.ppermute(bc_own, "mp", even_first)
+        even = lax.axis_index("mp") % 2 == 0
+        write_here = jnp.where(even, got_a, got_b).reshape(tok_rows, 1, NS)
+        read_here = jnp.where(even, got_b, got_a).reshape(tok_rows, 1, NS)
+    else:
+        group_all = lax.all_gather(bc_own, "mp", axis=1, tiled=True)
+        write_all = group_all[:, : G * NS].reshape(tok_rows, G, NS)
+        read_all = group_all[:, G * NS :].reshape(tok_rows, G, NS)
+        write_here = lax.dynamic_slice_in_dim(write_all, first_group, groups_here, 1)
+        read_here = lax.dynamic_slice_in_dim(read_all, first_group, groups_here, 1)
     step_size = jax.nn.softplus(dt_proj.astype(jnp.float32) + dt_bias)
     decay_rate = step_size * jnp.exp(a_log)
     cumulative = jnp.cumsum(decay_rate, 0)

time: 255 us -> 244 us (0.957)
  starting transfers between devices: 3.6 us -> 27.7 us
  waiting for transfers between devices: 136 us -> 113 us
  blocking collectives: 72.9 us -> 60 us
    all_gather x1 -> x0, waiting for transfers between devices: 81.1 us -> none  [entering(): everything = lax.all_gather(flat, axis).astype(jnp.float32)]
    all_to_all x0 -> x2, waiting for transfers between devices: none -> 43.2 us  [the longest x1 27.6 us: entering(): returned = lax.all_to_all(carried, axis, 0, 0)]
    all_to_all x0 -> x2, starting transfers between devices: none -> 23.4 us  [the longest x1 12.3 us: entering(): incoming = lax.all_to_all(outgoing, axis, 0, 0).astype(jnp.float32)]
    reduce_scatter x1, waiting for transfers between devices: 34.5 us -> 53.5 us  [shards(): lax.psum_scatter(partials, 'dp', scatter_dimension=0, tiled=False)]
    all_gather x1 -> x0, blocking collectives: 13.4 us -> none  [shards(): group_all = lax.all_gather(convolved[:, x_cols:], 'mp', axis=1, tiled=True)]
    ppermute x0 -> x2, waiting for transfers between devices: none -> 4.53 us  [the longest x1 4.53 us: shards(): got_b = lax.ppermute(bc_own, 'mp', even_first)]
    all_gather x1, waiting for transfers between devices: 14.1 us -> 9.85 us  [shards(): panel = lax.all_gather(local_panel, 'ctx', axis=0, tiled=True)]
    ppermute x1, waiting for transfers between devices: 6.15 us -> 2.16 us  [passed_along(): lax.ppermute(value, axis, [(source, source + steps) for source in range(f...]
  transfers between devices with their start and end apart: 4 -> 7, of which waited for: 4 -> 6; matrix products, arithmetic and copies ran while one was open for 3% -> 4% of each run, Pallas kernels for 0% -> 0%
where the time goes in v3:
time: 244 us; the launch traced here: 242 us
  waiting for transfers between devices  113 us (46%)
  blocking collectives  60 us (25%)
  starting transfers between devices  27.7 us (11%)
  between operations  14.4 us (6%)
  matrix products  12.2 us (5%)
  other arithmetic  8.18 us (3%)
  local copies, waits for them, and re-layouts  6.43 us (3%)
    reduce_scatter x1, waiting for transfers between devices, shards(): lax.psum_scatter(partials, 'dp', scatter_dimension=0, tiled=False)  53.5 us
    psum x2, blocking collectives, shards(): totals = lax.psum(lax.psum(powers, 'ctx'), 'dp')  44.7 us
    all_to_all x1, waiting for transfers between devices, entering(): returned = lax.all_to_all(carried, axis, 0, 0)  27.6 us
    all_to_all x1, waiting for transfers between devices, entering(): incoming = lax.all_to_all(outgoing, axis, 0, 0).astype(jnp.float32)  15.6 us
    all_to_all x1, blocking collectives, shards(): incoming = lax.all_to_all(outgoing, 'dp', 0, 0)  15.3 us
    all_to_all x1, starting transfers between devices, entering(): incoming = lax.all_to_all(outgoing, axis, 0, 0).astype(jnp.float32)  12.3 us
    all_to_all x1, starting transfers between devices, entering(): returned = lax.all_to_all(carried, axis, 0, 0)  11.1 us
    all_gather x1, waiting for transfers between devices, shards(): panel = lax.all_gather(local_panel, 'ctx', axis=0, tiled=True)  9.85 us
  transfers between devices with their start and end apart: 7, of which 6 were waited for; matrix products, arithmetic and copies ran while one was open for 4% of the time, Pallas kernels for 0%

profile of v3, /device:TPU:6, one launch (start us, length us, event | category | flops | bytes accessed | tf_op | source)
XLA Modules:
  0.0 242.1 jit_solution(6396383410580309061)
XLA Ops:
  7.2 0.8 copy.82
  8.0 1.6 pad_maximum_fusion.2
  9.7 1.6 copy.76
  11.3 0.9 convolution_bitcast_fusion
  12.2 3.3 %multiply_convert_fusion = bf16[128,64,64]{0,2,1:T(8,128)(2,1)S(1)} fusion(f32[128,64,64]{0,1,2:T(8,128)S(1)} %convolution_bitcast_fusion), kind=kOutput, calls=%fused_computation.5 | convolution fusion | flops 403791872 | bytes 3145728 | tf_op jit(solution)/shard_map/tcb,bd->tcd/dot_general | solution.py:81
  15.9 37.1 %psum.14 = f32[4,512]{1,0:T(4,128)S(1)} all-reduce(f32[4,512]{1,0:T(4,128)S(1)} %pad_maximum_fusion.3), channel_id=1, replica_groups=mesh['dp'=4,'ctx'=16,'mp'=8] {'ctx'}, use_global_device_ids=true, to_apply=%region_4.0 | all-reduce | flops 2048 | bytes 16384 | tf_op jit(solution)/shard_map/psum | solution.py:97
  53.0 7.6 %psum.15 = f32[4,512]{1,0:T(4,128)S(1)} all-reduce(f32[4,512]{1,0:T(4,128)S(1)} %psum.14), channel_id=1, replica_groups=mesh['dp'=4,'ctx'=16,'mp'=8] {'dp'}, use_global_device_ids=true, to_apply=%region_5.0 | all-reduce | flops 2048 | bytes 16384 | tf_op jit(solution)/shard_map/psum | solution.py:97
  61.2 1.6 collective-permute-start
  62.8 2.2 collective-permute-done
  65.1 15.3 %all_to_all.15 = bf16[4,136,1024]{2,1,0:T(8,128)(2,1)S(1)} all-to-all(bf16[4,136,1024]{2,1,0:T(8,128)(2,1)S(1)} %bitcast.81), channel_id=1, replica_groups=mesh['dp'=4,'ctx'=16,'mp'=8] {'dp'}, dimensions={0} | all-to-all | bytes 2228224 | tf_op jit(solution)/shard_map/all_to_all | solution.py:108
  80.4 9.8 %all-gather.2.cloned.1.call-done = bf16[1024,1168]{1,0:T(8,128)(2,1)} async-done(((bf16[64,1168]{1,0:T(8,128)(2,1)}), bf16[1024,1168]{1,0:T(8,128)(2,1)}) %all-gather.2.cloned.1.call-update) | async-done | bytes 2392080 | tf_op jit(solution)/shard_map/all_gather | solution.py:101
  90.2 6.1 %fusion = f32[4,136,1168]{1,2,0:T(8,128)} fusion(bf16[4,136,1024]{2,1,0:T(8,128)(2,1)S(1)} %all_to_all.15, bf16[1024,1168]{1,0:T(8,128)(2,1)} %all-gather.2.cloned.1.call-done), kind=kOutput, calls=%fused_computation | convolution fusion | flops 1301282816 | bytes 6047744 | tf_op jit(solution)/shard_map/kti,io->kto/dot_general | solution.py:109
  97.1 53.5 %reduce-scatter.2.cloned.1.call-done = f32[1,136,1168]{1,2,0:T(8,128)} async-done(((f32[4,136,1168]{1,2,0:T(8,128)}), f32[1,136,1168]{1,2,0:T(8,128)}) %reduce-scatter.2.cloned.1.call-update) | async-done | bytes 635408 | tf_op jit(solution)/shard_map/reduce_scatter | solution.py:110
  150.6 1.4 convert.17
  152.7 1.3 multiply_convert_fusion.2
  154.1 1.9 collective-permute-start.1
  156.9 4.5 %collective-permute-done.1 = bf16[128,128]{0,1:T(8,128)(2,1)S(1)} collective-permute-done((bf16[128,128]{0,1:T(8,128)(2,1)S(1)}, bf16[128,128]{0,1:T(8,128)(2,1)S(1)}, u32[]{:S(2)}, u32[]{:S(2)}) %collective-permute-start.1) | collective-permute-done | bytes 32800 | tf_op jit(solution)/shard_map/ppermute | solution.py:139
  162.4 12.3 %all-to-all-start.1 = ((bf16[16,72,128]{2,1,0:T(8,128)(2,1)}), bf16[16,72,128]{2,1,0:T(8,128)(2,1)S(1)}, u32[]{:S(2)}, u32[]{:S(2)}) async-start(bf16[16,72,128]{2,1,0:T(8,128)(2,1)} %pad_maximum_fusion.1), calls=%async_computation.2 | async-start | bytes 589824 | tf_op jit(solution)/shard_map/all_to_all | solution.py:31
  174.8 15.6 %all-to-all-done.1 = bf16[16,72,128]{2,1,0:T(8,128)(2,1)S(1)} async-done(((bf16[16,72,128]{2,1,0:T(8,128)(2,1)}), bf16[16,72,128]{2,1,0:T(8,128)(2,1)S(1)}, u32[]{:S(2)}, u32[]{:S(2)}) %all-to-all-start.1) | async-done | bytes 294944 | tf_op jit(solution)/shard_map/all_to_all | solution.py:31
  190.5 1.0 select_reduce_fusion
  192.5 1.0 copy.92
  193.4 11.1 %all-to-all-start.2 = ((f32[16,64,128]{2,1,0:T(8,128)}), f32[16,64,128]{2,1,0:T(8,128)S(1)}, u32[]{:S(2)}, u32[]{:S(2)}) async-start(f32[16,64,128]{2,1,0:T(8,128)} %copy.92), calls=%async_computation.3 | async-start | bytes 1048576 | tf_op jit(solution)/shard_map/all_to_all | solution.py:45
  206.2 27.6 %all-to-all-done.2 = f32[16,64,128]{2,1,0:T(8,128)S(1)} async-done(((f32[16,64,128]{2,1,0:T(8,128)}), f32[16,64,128]{2,1,0:T(8,128)S(1)}, u32[]{:S(2)}, u32[]{:S(2)}) %all-to-all-start.2) | async-done | bytes 524320 | tf_op jit(solution)/shard_map/all_to_all | solution.py:45
  234.4 0.9 copy.94
  (70 shorter events, 7.8 us)
Async XLA Ops:
  7.2 83.0 %all-gather.2.cloned.1.call-start = ((), (), s32[]{:S(2)}) async-start(), calls=%async_computation.4 | async-start | bytes 2785280 | tf_op jit(solution)/shard_map/all_gather | solution.py:101
  9.6 141.0 %reduce-scatter.2.cloned.1.call-start = ((), (), s32[]{:S(2)}) async-start(), calls=%async_computation.5 | async-start | bytes 5980160 | tf_op jit(solution)/shard_map/reduce_scatter | solution.py:110
  61.2 3.8 %collective-permute-start = (bf16[8,4096]{1,0:T(8,128)(2,1)S(1)}, bf16[8,4096]{1,0:T(8,128)(2,1)S(1)}, u32[]{:S(2)}, u32[]{:S(2)}) collective-permute-start(bf16[8,4096]{1,0:T(8,128)(2,1)S(1)} %slice.136), channel_id=1, source_target_pairs={{0,8},{8,16},{16,24},{24,32},{32,40},{40,48},{48,56},{56,64},{64,7... | collective-permute-start | bytes 196616 | tf_op jit(solution)/shard_map/ppermute | solution.py:18
  96.3 0.7 copy-start.6
  96.3 0.8 copy-start.1
  96.3 0.8 copy-start.3
  96.3 55.9 %copy-start.4 = (f32[16]{0:T(128)S(1)}, f32[16]{0:T(128)}, u32[]{:S(2)}) copy-start(f32[16]{0:T(128)} %param.18) | copy-start | bytes 196
  150.6 2.0 copy-start
  154.1 7.3 %collective-permute-start.1 = (bf16[128,128]{0,1:T(8,128)(2,1)S(1)}, bf16[128,128]{0,1:T(8,128)(2,1)S(1)}, u32[]{:S(2)}, u32[]{:S(2)}) collective-permute-start(bf16[128,128]{0,1:T(8,128)(2,1)S(1)} %slice.145), channel_id=1, source_target_pairs={{4,0},{0,1},{5,2},{1,3},{6,4},{2,5},{7,6},{3,7},{12,8},{8,9},{13,1... | collective-permute-start | bytes 98312 | tf_op jit(solution)/shard_map/ppermute | solution.py:139
  156.0 5.4 %collective-permute-start.2 = (bf16[128,128]{0,1:T(8,128)(2,1)S(1)}, bf16[128,128]{0,1:T(8,128)(2,1)S(1)}, u32[]{:S(2)}, u32[]{:S(2)}) collective-permute-start(bf16[128,128]{0,1:T(8,128)(2,1)S(1)} %slice.145), channel_id=1, source_target_pairs={{0,0},{4,1},{1,2},{5,3},{2,4},{6,5},{3,6},{7,7},{8,8},{12,9},{9,10... | collective-permute-start | bytes 98312 | tf_op jit(solution)/shard_map/ppermute | solution.py:138
  162.4 28.0 %all-to-all-start.1 = ((bf16[16,72,128]{2,1,0:T(8,128)(2,1)}), bf16[16,72,128]{2,1,0:T(8,128)(2,1)S(1)}, u32[]{:S(2)}, u32[]{:S(2)}) async-start(bf16[16,72,128]{2,1,0:T(8,128)(2,1)} %pad_maximum_fusion.1), calls=%async_computation.2 | async-start | bytes 589824 | tf_op jit(solution)/shard_map/all_to_all | solution.py:31
  191.9 12.6 %copy-start.2 = (f32[1024]{0:T(1024)S(1)}, f32[1024]{0:T(1024)}, u32[]{:S(2)}) copy-start(f32[1024]{0:T(1024)} %param.21) | copy-start | bytes 12292
  193.4 40.4 %all-to-all-start.2 = ((f32[16,64,128]{2,1,0:T(8,128)}), f32[16,64,128]{2,1,0:T(8,128)S(1)}, u32[]{:S(2)}, u32[]{:S(2)}) async-start(f32[16,64,128]{2,1,0:T(8,128)} %copy.92), calls=%async_computation.3 | async-start | bytes 1048576 | tf_op jit(solution)/shard_map/all_to_all | solution.py:45
  204.6 29.2 %copy-start.5 = (f32[16]{0:T(128)S(1)}, f32[16]{0:T(128)}, u32[]{:S(2)}) copy-start(f32[16]{0:T(128)} %param.20) | copy-start | bytes 196
Sparse Core Ops, SparseCore 0:
  10.7 79.5 all-gather.1
  96.4 54.1 reduce-scatter.1

commit v4 on v3

--- a/solution.py
+++ b/solution.py
@@ -42,8 +42,8 @@
     weights = jnp.prod(factors, 2)
     weights = jnp.where((source[:, :, 0] < target[:, :, 0])[..., None], weights, 0.0)
     carried = jnp.einsum("kjr,jrl->krl", weights, states, precision=HIGH)
-    returned = lax.all_to_all(carried, axis, 0, 0)
-    return returned.reshape(contrib.shape)
+    returned = lax.all_to_all(carried.astype(jnp.bfloat16), axis, 0, 0)
+    return returned.astype(jnp.float32).reshape(contrib.shape)
 
 
 def hadamard_signs(sign_order):
@@ -107,7 +107,8 @@
     outgoing = extended.reshape(tok_rows + rim, seqs, share).transpose(1, 0, 2)
     incoming = lax.all_to_all(outgoing, "dp", 0, 0)
     partials = jnp.einsum("kti,io->kto", incoming, panel, preferred_element_type=jnp.float32)
-    both_ext = lax.psum_scatter(partials, "dp", scatter_dimension=0, tiled=False)
+    returned = lax.all_to_all(partials.astype(jnp.bfloat16), "dp", 0, 0)
+    both_ext = jnp.sum(returned.astype(jnp.float32), 0)
     both = both_ext[rim:]
     x_end = x_weight.shape[1]
     bc_end = x_end + bc_weight.shape[1]

time: 244 us -> 186 us (0.76)
  waiting for transfers between devices: 113 us -> 61 us
    reduce_scatter x1 -> x0, waiting for transfers between devices: 53.5 us -> none  [shards(): lax.psum_scatter(partials, 'dp', scatter_dimension=0, tiled=False)]
    all_to_all x1, starting transfers between devices: 12.3 us -> 7.69 us  [entering(): incoming = lax.all_to_all(outgoing, axis, 0, 0).astype(jnp.float32)]
    all_to_all x1 -> x2, starting transfers between devices: 11.1 us -> 13.7 us  [the longest x1 8.81 us: entering(): returned = lax.all_to_all(carried.astype(jnp.bfloat16), axis, 0, 0)]
    all_to_all x1 -> x2, waiting for transfers between devices: 27.6 us -> 27.6 us  [the longest x1 17.1 us: entering(): returned = lax.all_to_all(carried.astype(jnp.bfloat16), axis, 0, 0)]
  transfers between devices with their start and end apart: 7 -> 7, of which waited for: 6 -> 6; matrix products, arithmetic and copies ran while one was open for 4% -> 5% of each run, Pallas kernels for 0% -> 0%
where the time goes in v4:
time: 186 us; the launch traced here: 184 us
  waiting for transfers between devices  61 us (33%)
  blocking collectives  60.2 us (32%)
  starting transfers between devices  25.7 us (14%)
  between operations  14.4 us (8%)
  matrix products  10.4 us (6%)
  local copies, waits for them, and re-layouts  6.23 us (3%)
  other arithmetic  6.03 us (3%)
    psum x2, blocking collectives, shards(): totals = lax.psum(lax.psum(powers, 'ctx'), 'dp')  44.6 us
    all_to_all x1, waiting for transfers between devices, entering(): incoming = lax.all_to_all(outgoing, axis, 0, 0).astype(jnp.float32)  17.3 us
    all_to_all x1, waiting for transfers between devices, entering(): returned = lax.all_to_all(carried.astype(jnp.bfloat16), axis, 0, 0)  17.1 us
    all_to_all x1, blocking collectives, shards(): incoming = lax.all_to_all(outgoing, 'dp', 0, 0)  15.6 us
    all_to_all x1, waiting for transfers between devices, shards(): returned = lax.all_to_all(partials.astype(jnp.bfloat16), 'dp', 0, 0)  10.5 us
    all_gather x1, waiting for transfers between devices, shards(): panel = lax.all_gather(local_panel, 'ctx', axis=0, tiled=True)  9.73 us
    all_to_all x1, starting transfers between devices, entering(): returned = lax.all_to_all(carried.astype(jnp.bfloat16), axis, 0, 0)  8.81 us
    all_to_all x1, starting transfers between devices, entering(): incoming = lax.all_to_all(outgoing, axis, 0, 0).astype(jnp.float32)  7.69 us
  transfers between devices with their start and end apart: 7, of which 6 were waited for; matrix products, arithmetic and copies ran while one was open for 5% of the time, Pallas kernels for 0%

profile of v4, /device:TPU:6, one launch (start us, length us, event | category | flops | bytes accessed | tf_op | source)
XLA Modules:
  0.0 183.9 jit_solution(15305285099470118876)
XLA Ops:
  7.2 0.8 copy.100
  8.0 1.6 pad_maximum_fusion.2
  9.6 1.6 copy.94
  11.2 0.9 convolution_bitcast_fusion
  12.1 3.3 %multiply_convert_fusion = bf16[128,64,64]{0,2,1:T(8,128)(2,1)S(1)} fusion(f32[128,64,64]{0,1,2:T(8,128)S(1)} %convolution_bitcast_fusion), kind=kOutput, calls=%fused_computation.5 | convolution fusion | flops 403791872 | bytes 3145728 | tf_op jit(solution)/shard_map/tcb,bd->tcd/dot_general | solution.py:81
  15.8 37.0 %psum.14 = f32[4,512]{1,0:T(4,128)S(1)} all-reduce(f32[4,512]{1,0:T(4,128)S(1)} %pad_maximum_fusion.3), channel_id=1, replica_groups=mesh['dp'=4,'ctx'=16,'mp'=8] {'ctx'}, use_global_device_ids=true, to_apply=%region_4.0 | all-reduce | flops 2048 | bytes 16384 | tf_op jit(solution)/shard_map/psum | solution.py:97
  52.8 7.6 %psum.15 = f32[4,512]{1,0:T(4,128)S(1)} all-reduce(f32[4,512]{1,0:T(4,128)S(1)} %psum.14), channel_id=1, replica_groups=mesh['dp'=4,'ctx'=16,'mp'=8] {'dp'}, use_global_device_ids=true, to_apply=%region_5.0 | all-reduce | flops 2048 | bytes 16384 | tf_op jit(solution)/shard_map/psum | solution.py:97
  61.0 1.7 collective-permute-start
  62.7 2.1 %collective-permute-done = bf16[8,4096]{1,0:T(8,128)(2,1)S(1)} collective-permute-done((bf16[8,4096]{1,0:T(8,128)(2,1)S(1)}, bf16[8,4096]{1,0:T(8,128)(2,1)S(1)}, u32[]{:S(2)}, u32[]{:S(2)}) %collective-permute-start) | collective-permute-done | bytes 65568 | tf_op jit(solution)/shard_map/ppermute | solution.py:18
  65.0 15.6 %all_to_all.20 = bf16[4,136,1024]{2,1,0:T(8,128)(2,1)S(1)} all-to-all(bf16[4,136,1024]{2,1,0:T(8,128)(2,1)S(1)} %bitcast.74), channel_id=1, replica_groups=mesh['dp'=4,'ctx'=16,'mp'=8] {'dp'}, dimensions={0} | all-to-all | bytes 2228224 | tf_op jit(solution)/shard_map/all_to_all | solution.py:108
  80.6 9.7 %all-gather.2.cloned.1.call-done = bf16[1024,1168]{1,0:T(8,128)(2,1)} async-done(((bf16[64,1168]{1,0:T(8,128)(2,1)}), bf16[1024,1168]{1,0:T(8,128)(2,1)}) %all-gather.2.cloned.1.call-update) | async-done | bytes 2392080 | tf_op jit(solution)/shard_map/all_gather | solution.py:101
  90.3 4.4 %convolution_convert_fusion = bf16[4,136,1168]{2,1,0:T(8,128)(2,1)} fusion(bf16[4,136,1024]{2,1,0:T(8,128)(2,1)S(1)} %all_to_all.20, bf16[1024,1168]{1,0:T(8,128)(2,1)} %all-gather.2.cloned.1.call-done), kind=kOutput, calls=%fused_computation | convolution fusion | flops 1301918208 | bytes 4776960 | tf_op jit(solution)/shard_map/kti,io->kto/dot_general | solution.py:109
  94.8 4.9 %all-to-all-start.1 = ((bf16[4,136,1168]{2,1,0:T(8,128)(2,1)}), bf16[4,136,1168]{2,1,0:T(8,128)(2,1)S(1)}, u32[]{:S(2)}, u32[]{:S(2)}) async-start(bf16[4,136,1168]{2,1,0:T(8,128)(2,1)} %convolution_convert_fusion), calls=%async_computation.1 | async-start | bytes 2785280 | tf_op jit(solution)/shard_map/all_to_all | solution.py:110
  99.9 10.5 %all-to-all-done.1 = bf16[4,136,1168]{2,1,0:T(8,128)(2,1)S(1)} async-done(((bf16[4,136,1168]{2,1,0:T(8,128)(2,1)}), bf16[4,136,1168]{2,1,0:T(8,128)(2,1)S(1)}, u32[]{:S(2)}, u32[]{:S(2)}) %all-to-all-start.1) | async-done | bytes 1270816 | tf_op jit(solution)/shard_map/all_to_all | solution.py:110
  111.6 1.9 %collective-permute-start.1 = (bf16[128,128]{1,0:T(8,128)(2,1)S(1)}, bf16[128,128]{1,0:T(8,128)(2,1)S(1)}, u32[]{:S(2)}, u32[]{:S(2)}) collective-permute-start(bf16[128,128]{1,0:T(8,128)(2,1)S(1)} %slice.138), channel_id=1, source_target_pairs={{4,0},{0,1},{5,2},{1,3},{6,4},{2,5},{7,6},{3,7},{12,8},{8,9},{13,1... | collective-permute-start | bytes 98312 | tf_op jit(solution)/shard_map/ppermute | solution.py:140
  114.8 4.1 %collective-permute-done.1 = bf16[128,128]{1,0:T(8,128)(2,1)S(1)} collective-permute-done((bf16[128,128]{1,0:T(8,128)(2,1)S(1)}, bf16[128,128]{1,0:T(8,128)(2,1)S(1)}, u32[]{:S(2)}, u32[]{:S(2)}) %collective-permute-start.1) | collective-permute-done | bytes 32800 | tf_op jit(solution)/shard_map/ppermute | solution.py:140
  119.1 0.7 pad_maximum_fusion.1
  119.8 7.7 %all-to-all-start.2 = ((bf16[16,72,128]{2,1,0:T(8,128)(2,1)}), bf16[16,72,128]{2,1,0:T(8,128)(2,1)S(1)}, u32[]{:S(2)}, u32[]{:S(2)}) async-start(bf16[16,72,128]{2,1,0:T(8,128)(2,1)} %pad_maximum_fusion.1), calls=%async_computation.2 | async-start | bytes 589824 | tf_op jit(solution)/shard_map/all_to_all | solution.py:31
  128.2 17.3 %all-to-all-done.2 = bf16[16,72,128]{2,1,0:T(8,128)(2,1)S(1)} async-done(((bf16[16,72,128]{2,1,0:T(8,128)(2,1)}), bf16[16,72,128]{2,1,0:T(8,128)(2,1)S(1)}, u32[]{:S(2)}, u32[]{:S(2)}) %all-to-all-start.2) | async-done | bytes 294944 | tf_op jit(solution)/shard_map/all_to_all | solution.py:31
  145.7 1.0 select_reduce_fusion
  147.7 0.8 copy.112
  148.4 8.8 %all-to-all-start.3 = ((bf16[16,64,128]{2,1,0:T(8,128)(2,1)}), bf16[16,64,128]{2,1,0:T(8,128)(2,1)S(1)}, u32[]{:S(2)}, u32[]{:S(2)}) async-start(bf16[16,64,128]{2,1,0:T(8,128)(2,1)} %copy.112), calls=%async_computation.3 | async-start | bytes 524288 | tf_op jit(solution)/shard_map/all_to_all | solution.py:45
  158.6 17.1 %all-to-all-done.3 = bf16[16,64,128]{2,1,0:T(8,128)(2,1)S(1)} async-done(((bf16[16,64,128]{2,1,0:T(8,128)(2,1)}), bf16[16,64,128]{2,1,0:T(8,128)(2,1)S(1)}, u32[]{:S(2)}, u32[]{:S(2)}) %all-to-all-start.3) | async-done | bytes 262176 | tf_op jit(solution)/shard_map/all_to_all | solution.py:45
  176.2 0.9 copy.114
  (71 shorter events, 7.4 us)
Async XLA Ops:
  7.2 83.1 %all-gather.2.cloned.1.call-start = ((), (), s32[]{:S(2)}) async-start(), calls=%async_computation.4 | async-start | bytes 2785280 | tf_op jit(solution)/shard_map/all_gather | solution.py:101
  61.0 3.9 %collective-permute-start = (bf16[8,4096]{1,0:T(8,128)(2,1)S(1)}, bf16[8,4096]{1,0:T(8,128)(2,1)S(1)}, u32[]{:S(2)}, u32[]{:S(2)}) collective-permute-start(bf16[8,4096]{1,0:T(8,128)(2,1)S(1)} %slice.129), channel_id=1, source_target_pairs={{0,8},{8,16},{16,24},{24,32},{32,40},{40,48},{48,56},{56,64},{64,7... | collective-permute-start | bytes 196616 | tf_op jit(solution)/shard_map/ppermute | solution.py:18
  94.7 4.9 %copy-start.5 = (f32[16]{0:T(128)S(1)}, f32[16]{0:T(128)}, u32[]{:S(2)}) copy-start(f32[16]{0:T(128)} %param.19) | copy-start | bytes 196
  94.7 4.9 %copy-start.1 = (f32[1024]{0:T(1024)S(1)}, f32[1024]{0:T(1024)}, u32[]{:S(2)}) copy-start(f32[1024]{0:T(1024)} %param.21) | copy-start | bytes 12292
  94.7 5.0 %copy-start = (f32[5,1024]{1,0:T(8,128)S(1)}, f32[5,1024]{1,0:T(8,128)}, u32[]{:S(2)}) copy-start(f32[5,1024]{1,0:T(8,128)} %param.16) | copy-start | bytes 61444
  94.8 5.0 %copy-start.2 = (f32[5,128]{1,0:T(8,128)S(1)}, f32[5,128]{1,0:T(8,128)}, u32[]{:S(2)}) copy-start(f32[5,128]{1,0:T(8,128)} %param.17) | copy-start | bytes 7684
  94.8 15.9 %copy-start.3 = (f32[16]{0:T(128)S(1)}, f32[16]{0:T(128)}, u32[]{:S(2)}) copy-start(f32[16]{0:T(128)} %param.18) | copy-start | bytes 196
  94.8 15.6 %all-to-all-start.1 = ((bf16[4,136,1168]{2,1,0:T(8,128)(2,1)}), bf16[4,136,1168]{2,1,0:T(8,128)(2,1)S(1)}, u32[]{:S(2)}, u32[]{:S(2)}) async-start(bf16[4,136,1168]{2,1,0:T(8,128)(2,1)} %convolution_convert_fusion), calls=%async_computation.1 | async-start | bytes 2785280 | tf_op jit(solution)/shard_map/all_to_all | solution.py:110
  111.6 7.3 %collective-permute-start.1 = (bf16[128,128]{1,0:T(8,128)(2,1)S(1)}, bf16[128,128]{1,0:T(8,128)(2,1)S(1)}, u32[]{:S(2)}, u32[]{:S(2)}) collective-permute-start(bf16[128,128]{1,0:T(8,128)(2,1)S(1)} %slice.138), channel_id=1, source_target_pairs={{4,0},{0,1},{5,2},{1,3},{6,4},{2,5},{7,6},{3,7},{12,8},{8,9},{13,1... | collective-permute-start | bytes 98312 | tf_op jit(solution)/shard_map/ppermute | solution.py:140
  113.5 5.4 %collective-permute-start.2 = (bf16[128,128]{1,0:T(8,128)(2,1)S(1)}, bf16[128,128]{1,0:T(8,128)(2,1)S(1)}, u32[]{:S(2)}, u32[]{:S(2)}) collective-permute-start(bf16[128,128]{1,0:T(8,128)(2,1)S(1)} %slice.138), channel_id=1, source_target_pairs={{0,0},{4,1},{1,2},{5,3},{2,4},{6,5},{3,6},{7,7},{8,8},{12,9},{9,10... | collective-permute-start | bytes 98312 | tf_op jit(solution)/shard_map/ppermute | solution.py:139
  119.8 25.8 %all-to-all-start.2 = ((bf16[16,72,128]{2,1,0:T(8,128)(2,1)}), bf16[16,72,128]{2,1,0:T(8,128)(2,1)S(1)}, u32[]{:S(2)}, u32[]{:S(2)}) async-start(bf16[16,72,128]{2,1,0:T(8,128)(2,1)} %pad_maximum_fusion.1), calls=%async_computation.2 | async-start | bytes 589824 | tf_op jit(solution)/shard_map/all_to_all | solution.py:31
  148.4 27.3 %all-to-all-start.3 = ((bf16[16,64,128]{2,1,0:T(8,128)(2,1)}), bf16[16,64,128]{2,1,0:T(8,128)(2,1)S(1)}, u32[]{:S(2)}, u32[]{:S(2)}) async-start(bf16[16,64,128]{2,1,0:T(8,128)(2,1)} %copy.112), calls=%async_computation.3 | async-start | bytes 524288 | tf_op jit(solution)/shard_map/all_to_all | solution.py:45
  157.5 18.2 %copy-start.4 = (f32[16]{0:T(128)S(1)}, f32[16]{0:T(128)}, u32[]{:S(2)}) copy-start(f32[16]{0:T(128)} %param.20) | copy-start | bytes 196
Sparse Core Ops, SparseCore 0:
  10.7 79.6 all-gather.1

commit v5 on v4

--- a/solution.py
+++ b/solution.py
@@ -16,6 +16,26 @@
     count = lax.axis_size(axis)
     first, last = (max(0, -steps), min(count, count - steps))
     return lax.ppermute(value, axis, [(source, source + steps) for source in range(first, last)])
+
+
+def ring_gather(block, axis):
+    count, place = (lax.axis_size(axis), lax.axis_index(axis))
+    ahead = [(source, (source + 1) % count) for source in range(count)]
+    behind = [(source, (source - 1) % count) for source in range(count)]
+    back_steps = count // 2
+    fore_steps = count - 1 - back_steps
+    from_behind, from_ahead = ([], [])
+    moving_back, moving_fore = (block, block)
+    for step in range(back_steps):
+        moving_back = lax.ppermute(moving_back, axis, ahead)
+        from_behind.append(moving_back)
+        if step < fore_steps:
+            moving_fore = lax.ppermute(moving_fore, axis, behind)
+            from_ahead.append(moving_fore)
+    ordered = from_behind[::-1] + [block] + from_ahead
+    stacked = jnp.concatenate(ordered, 0)
+    rows = block.shape[0]
+    return jnp.roll(stacked, (place - back_steps) * rows, 0)
 
 
 def entering(decay, contrib, axis):
@@ -94,11 +114,8 @@
         ]
     )
     row_count = float(tok_rows * lax.axis_size("dp") * lax.axis_size("ctx"))
-    totals = lax.psum(lax.psum(powers, "ctx"), "dp")
-    totals, rotated = lax.optimization_barrier((totals, rotated))
-    kurtosis = kurtosis_from(totals, row_count)
     local_panel = jnp.concatenate([x_weight, bc_weight, dt_weight], 1)
-    panel = lax.all_gather(local_panel, "ctx", axis=0, tiled=True)
+    panel = ring_gather(local_panel, "ctx")
     seqs = lax.axis_size("dp")
     share = model_width // seqs
     rim = 8
@@ -173,6 +190,9 @@
         * x_heads
     ).astype(jnp.bfloat16)
     contrib = jnp.einsum("sghp,sgn->ghpn", update, write_here, preferred_element_type=jnp.float32)
+    powers, contrib = lax.optimization_barrier((powers, contrib))
+    totals = lax.psum(lax.psum(powers, "ctx"), "dp")
+    kurtosis = kurtosis_from(totals, row_count)
     carried = entering(jnp.exp(-block_end).reshape(groups_here, heads_local), contrib, "ctx")
     from_before = jnp.exp(-cumulative).reshape(tok_rows, groups_here, heads_local)[
         ..., None

time: 186 us -> 234 us (1.26)
  starting transfers between devices: 25.7 us -> 91.1 us
  local copies, waits for them, and re-layouts: 6.23 us -> 22 us
  blocking collectives: 60.2 us -> 46.4 us
  between operations: 14.4 us -> 1.27 us
  waiting for transfers between devices: 61 us -> 53.5 us
    ppermute x0 -> x15, starting transfers between devices: none -> 59.3 us  [the longest x7 42.1 us: ring_gather(): moving_fore = lax.ppermute(moving_fore, axis, behind)]
    ppermute x0 -> x15, waiting for transfers between devices: none -> 21.4 us  [the longest x7 12.4 us: ring_gather(): moving_fore = lax.ppermute(moving_fore, axis, behind)]
    all_to_all x1, waiting for transfers between devices: 17.1 us -> 0.01 us  [entering(): returned = lax.all_to_all(carried.astype(jnp.bfloat16), axis, 0, 0)]
    all_to_all x1 -> x0, blocking collectives: 15.6 us -> none  [shards(): incoming = lax.all_to_all(outgoing, 'dp', 0, 0)]
    concatenate x0 -> x1, local copies, waits for them, and re-layouts: none -> 12.9 us  [ring_gather(): return jnp.roll(stacked, (place - back_steps) * rows, 0)]
    all_gather x1 -> x0, waiting for transfers between devices: 9.73 us -> none  [shards(): panel = lax.all_gather(local_panel, 'ctx', axis=0, tiled=True)]
    all_to_all x0 -> x1, starting transfers between devices: none -> 4.76 us  [shards(): incoming = lax.all_to_all(outgoing, 'dp', 0, 0)]
  transfers between devices with their start and end apart: 7 -> 22, of which waited for: 6 -> 11; matrix products, arithmetic and copies ran while one was open for 5% -> 11% of each run, Pallas kernels for 0% -> 0%
where the time goes in v5:
time: 234 us; the launch traced here: 230 us
  starting transfers between devices  91.1 us (39%)
  waiting for transfers between devices  53.5 us (23%)
  blocking collectives  46.4 us (20%)
  local copies, waits for them, and re-layouts  22 us (9%)
  matrix products  10.9 us (5%)
  other arithmetic  5.17 us (2%)
    psum x2, blocking collectives, shards(): totals = lax.psum(lax.psum(powers, 'ctx'), 'dp')  46.4 us
    ppermute x7, starting transfers between devices, ring_gather(): moving_fore = lax.ppermute(moving_fore, axis, behind)  42.1 us
    all_to_all x1, waiting for transfers between devices, entering(): incoming = lax.all_to_all(outgoing, axis, 0, 0).astype(jnp.float32)  17.9 us
    ppermute x8, starting transfers between devices, ring_gather(): moving_back = lax.ppermute(moving_back, axis, ahead)  17.2 us
    concatenate x1, local copies, waits for them, and re-layouts, ring_gather(): return jnp.roll(stacked, (place - back_steps) * rows, 0)  12.9 us
    ppermute x7, waiting for transfers between devices, ring_gather(): moving_fore = lax.ppermute(moving_fore, axis, behind)  12.4 us
    all_to_all x1, waiting for transfers between devices, shards(): returned = lax.all_to_all(partials.astype(jnp.bfloat16), 'dp', 0, 0)  10.2 us
    all_to_all x1, starting transfers between devices, entering(): incoming = lax.all_to_all(outgoing, axis, 0, 0).astype(jnp.float32)  9.45 us
  transfers between devices with their start and end apart: 22, of which 11 were waited for; matrix products, arithmetic and copies ran while one was open for 11% of the time, Pallas kernels for 0%

profile of v5, /device:TPU:6, one launch (start us, length us, event | category | flops | bytes accessed | tf_op | source)
XLA Modules:
  0.0 230.4 jit_solution(5425799214749172258)
XLA Ops:
  3.3 3.8 %collective-permute-start.1 = (bf16[64,1168]{0,1:T(8,128)(2,1)S(1)}, bf16[64,1168]{0,1:T(8,128)(2,1)S(1)}, u32[]{:S(2)}, u32[]{:S(2)}) collective-permute-start(bf16[64,1168]{0,1:T(8,128)(2,1)S(1)} %pad_maximum_fusion.1), channel_id=1, source_target_pairs={{0,8},{8,16},{16,24},{24,32},{32,40},{40,48},{48,56},{56,64},{64,7... | collective-permute-start | bytes 448520 | tf_op jit(solution)/shard_map/ppermute | solution.py:30
  7.1 9.5 %collective-permute-start.9 = (bf16[64,1168]{0,1:T(8,128)(2,1)S(1)}, bf16[64,1168]{0,1:T(8,128)(2,1)S(1)}, u32[]{:S(2)}, u32[]{:S(2)}) collective-permute-start(bf16[64,1168]{0,1:T(8,128)(2,1)S(1)} %pad_maximum_fusion.1), channel_id=1, source_target_pairs={{0,120},{8,0},{16,8},{24,16},{32,24},{40,32},{48,40},{56,48},{64,5... | collective-permute-start | bytes 448520 | tf_op jit(solution)/shard_map/ppermute | solution.py:33
  19.2 2.6 %collective-permute-done.1 = bf16[64,1168]{0,1:T(8,128)(2,1)S(1)} collective-permute-done((bf16[64,1168]{0,1:T(8,128)(2,1)S(1)}, bf16[64,1168]{0,1:T(8,128)(2,1)S(1)}, u32[]{:S(2)}, u32[]{:S(2)}) %collective-permute-start.1) | collective-permute-done | bytes 149536 | tf_op jit(solution)/shard_map/ppermute | solution.py:30
  23.7 3.3 %multiply_convert_fusion = bf16[128,64,64]{0,2,1:T(8,128)(2,1)S(1)} fusion(f32[128,64,64]{0,1,2:T(8,128)S(1)} %convolution_bitcast_fusion), kind=kOutput, calls=%fused_computation.6 | convolution fusion | flops 403791872 | bytes 3145728 | tf_op jit(solution)/shard_map/tcb,bd->tcd/dot_general | solution.py:101
  29.6 5.1 %collective-permute-start.10 = (bf16[64,1168]{0,1:T(8,128)(2,1)S(1)}, bf16[64,1168]{0,1:T(8,128)(2,1)}, u32[]{:S(2)}, u32[]{:S(2)}) collective-permute-start(bf16[64,1168]{0,1:T(8,128)(2,1)S(1)} %collective-permute-done.9), channel_id=1, source_target_pairs={{0,120},{8,0},{16,8},{24,16},{32,24},{40,32},{48,40},{56,48},{64,5... | collective-permute-start | bytes 448520 | tf_op jit(solution)/shard_map/ppermute | solution.py:33
  37.9 4.8 %all-to-all-start = ((bf16[4,136,1024]{2,1,0:T(8,128)(2,1)}), bf16[4,136,1024]{2,1,0:T(8,128)(2,1)}, u32[]{:S(2)}, u32[]{:S(2)}) async-start(bf16[4,136,1024]{2,1,0:T(8,128)(2,1)} %bitcast.76), calls=%async_computation | async-start | bytes 2228224 | tf_op jit(solution)/shard_map/all_to_all | solution.py:125
  42.7 5.1 %collective-permute-start.11 = (bf16[64,1168]{0,1:T(8,128)(2,1)}, bf16[64,1168]{0,1:T(8,128)(2,1)S(1)}, u32[]{:S(2)}, u32[]{:S(2)}) collective-permute-start(bf16[64,1168]{0,1:T(8,128)(2,1)} %collective-permute-done.10), channel_id=1, source_target_pairs={{0,120},{8,0},{16,8},{24,16},{32,24},{40,32},{48,40},{56,48},{64,5... | collective-permute-start | bytes 448520 | tf_op jit(solution)/shard_map/ppermute | solution.py:33
  49.7 3.0 %collective-permute-done.11 = bf16[64,1168]{0,1:T(8,128)(2,1)S(1)} collective-permute-done((bf16[64,1168]{0,1:T(8,128)(2,1)}, bf16[64,1168]{0,1:T(8,128)(2,1)S(1)}, u32[]{:S(2)}, u32[]{:S(2)}) %collective-permute-start.11) | collective-permute-done | bytes 149536 | tf_op jit(solution)/shard_map/ppermute | solution.py:33
  52.7 5.5 %collective-permute-start.12 = (bf16[64,1168]{0,1:T(8,128)(2,1)S(1)}, bf16[64,1168]{0,1:T(8,128)(2,1)S(1)}, u32[]{:S(2)}, u32[]{:S(2)}) collective-permute-start(bf16[64,1168]{0,1:T(8,128)(2,1)S(1)} %collective-permute-done.11), channel_id=1, source_target_pairs={{0,120},{8,0},{16,8},{24,16},{32,24},{40,32},{48,40},{56,48},{64,5... | collective-permute-start | bytes 448520 | tf_op jit(solution)/shard_map/ppermute | solution.py:33
  62.5 5.6 %collective-permute-start.13 = (bf16[64,1168]{0,1:T(8,128)(2,1)S(1)}, bf16[64,1168]{0,1:T(8,128)(2,1)S(1)}, u32[]{:S(2)}, u32[]{:S(2)}) collective-permute-start(bf16[64,1168]{0,1:T(8,128)(2,1)S(1)} %collective-permute-done.12), channel_id=1, source_target_pairs={{0,120},{8,0},{16,8},{24,16},{32,24},{40,32},{48,40},{56,48},{64,5... | collective-permute-start | bytes 448520 | tf_op jit(solution)/shard_map/ppermute | solution.py:33
  72.3 5.6 %collective-permute-start.14 = (bf16[64,1168]{0,1:T(8,128)(2,1)S(1)}, bf16[64,1168]{0,1:T(8,128)(2,1)}, u32[]{:S(2)}, u32[]{:S(2)}) collective-permute-start(bf16[64,1168]{0,1:T(8,128)(2,1)S(1)} %collective-permute-done.13), channel_id=1, source_target_pairs={{0,120},{8,0},{16,8},{24,16},{32,24},{40,32},{48,40},{56,48},{64,5... | collective-permute-start | bytes 448520 | tf_op jit(solution)/shard_map/ppermute | solution.py:33
  79.9 2.5 %collective-permute-done.14 = bf16[64,1168]{0,1:T(8,128)(2,1)} collective-permute-done((bf16[64,1168]{0,1:T(8,128)(2,1)S(1)}, bf16[64,1168]{0,1:T(8,128)(2,1)}, u32[]{:S(2)}, u32[]{:S(2)}) %collective-permute-start.14) | collective-permute-done | bytes 149536 | tf_op jit(solution)/shard_map/ppermute | solution.py:33
  82.4 5.7 %collective-permute-start.15 = (bf16[64,1168]{0,1:T(8,128)(2,1)}, bf16[64,1168]{0,1:T(8,128)(2,1)}, u32[]{:S(2)}, u32[]{:S(2)}) collective-permute-start(bf16[64,1168]{0,1:T(8,128)(2,1)} %collective-permute-done.14), channel_id=1, source_target_pairs={{0,120},{8,0},{16,8},{24,16},{32,24},{40,32},{48,40},{56,48},{64,5... | collective-permute-start | bytes 448520 | tf_op jit(solution)/shard_map/ppermute | solution.py:33
  92.7 5.9 %collective-permute-done.8 = bf16[64,1168]{0,1:T(8,128)(2,1)} collective-permute-done((bf16[64,1168]{0,1:T(8,128)(2,1)}, bf16[64,1168]{0,1:T(8,128)(2,1)}, u32[]{:S(2)}, u32[]{:S(2)}) %collective-permute-start.8) | collective-permute-done | bytes 149536 | tf_op jit(solution)/shard_map/ppermute | solution.py:30
  98.6 12.9 %concatenate.24 = bf16[2048,1168]{0,1:T(8,128)(2,1)} concatenate(bf16[64,1168]{0,1:T(8,128)(2,1)} %collective-permute-done.8, bf16[64,1168]{0,1:T(8,128)(2,1)} %collective-permute-done.7, bf16[64,1168]{0,1:T(8,128)(2,1)} %copy-done.1, bf16[64,1168]{0,1:T(8,128)(2,1)S(1)} %collective-permute-done.5, bf16[64,1168]{0,1:T(8,128)(2,1)S(1)} %collective-permute-done.4, ...), dimensions={0} | concatenate | bytes 9568256 | tf_op jit(solution)/shard_map/jit(_roll_dynamic)/concatenate | solution.py:38
  111.6 4.9 %convolution_convert_fusion = bf16[4,136,1168]{2,1,0:T(8,128)(2,1)} fusion(bf16[4,136,1024]{2,1,0:T(8,128)(2,1)} %all-to-all-done, bf16[2048,1168]{0,1:T(8,128)(2,1)} %concatenate.24, s32[]{:T(128)S(6)} %select_n.71), kind=kOutput, calls=%fused_computation | convolution fusion | flops 1301918208 | bytes 4776964 | tf_op jit(solution)/shard_map/kti,io->kto/dot_general | solution.py:126
  116.5 4.9 %all-to-all-start.1 = ((bf16[4,136,1168]{2,1,0:T(8,128)(2,1)}), bf16[4,136,1168]{2,1,0:T(8,128)(2,1)S(1)}, u32[]{:S(2)}, u32[]{:S(2)}) async-start(bf16[4,136,1168]{2,1,0:T(8,128)(2,1)} %convolution_convert_fusion), calls=%async_computation.1 | async-start | bytes 2785280 | tf_op jit(solution)/shard_map/all_to_all | solution.py:127
  121.9 10.2 %all-to-all-done.1 = bf16[4,136,1168]{2,1,0:T(8,128)(2,1)S(1)} async-done(((bf16[4,136,1168]{2,1,0:T(8,128)(2,1)}), bf16[4,136,1168]{2,1,0:T(8,128)(2,1)S(1)}, u32[]{:S(2)}, u32[]{:S(2)}) %all-to-all-start.1) | async-done | bytes 1270816 | tf_op jit(solution)/shard_map/all_to_all | solution.py:127
  136.5 4.1 %collective-permute-done.16 = bf16[128,128]{1,0:T(8,128)(2,1)S(1)} collective-permute-done((bf16[128,128]{1,0:T(8,128)(2,1)S(1)}, bf16[128,128]{1,0:T(8,128)(2,1)S(1)}, u32[]{:S(2)}, u32[]{:S(2)}) %collective-permute-start.16) | collective-permute-done | bytes 32800 | tf_op jit(solution)/shard_map/ppermute | solution.py:157
  141.6 9.5 %all-to-all-start.2 = ((bf16[16,72,128]{2,1,0:T(8,128)(2,1)}), bf16[16,72,128]{2,1,0:T(8,128)(2,1)S(1)}, u32[]{:S(2)}, u32[]{:S(2)}) async-start(bf16[16,72,128]{2,1,0:T(8,128)(2,1)} %pad_maximum_fusion.2), calls=%async_computation.2 | async-start | bytes 589824 | tf_op jit(solution)/shard_map/all_to_all | solution.py:51
  151.3 17.9 %all-to-all-done.2 = bf16[16,72,128]{2,1,0:T(8,128)(2,1)S(1)} async-done(((bf16[16,72,128]{2,1,0:T(8,128)(2,1)}), bf16[16,72,128]{2,1,0:T(8,128)(2,1)S(1)}, u32[]{:S(2)}, u32[]{:S(2)}) %all-to-all-start.2) | async-done | bytes 294944 | tf_op jit(solution)/shard_map/all_to_all | solution.py:51
  172.0 8.7 %all-to-all-start.3 = ((bf16[16,64,128]{2,1,0:T(8,128)(2,1)}), bf16[16,64,128]{2,1,0:T(8,128)(2,1)S(1)}, u32[]{:S(2)}, u32[]{:S(2)}) async-start(bf16[16,64,128]{2,1,0:T(8,128)(2,1)} %copy.118), calls=%async_computation.3 | async-start | bytes 524288 | tf_op jit(solution)/shard_map/all_to_all | solution.py:65
  181.3 37.7 %psum.14 = f32[4,512]{1,0:T(4,128)S(1)} all-reduce(f32[4,512]{1,0:T(4,128)S(1)} %pad_maximum_fusion.3), channel_id=1, replica_groups=mesh['dp'=4,'ctx'=16,'mp'=8] {'ctx'}, use_global_device_ids=true, to_apply=%region_9.10 | all-reduce | flops 2048 | bytes 16384 | tf_op jit(solution)/shard_map/psum | solution.py:194
  219.0 8.7 %psum.15 = f32[4,512]{1,0:T(4,128)S(1)} all-reduce(f32[4,512]{1,0:T(4,128)S(1)} %psum.14), channel_id=1, replica_groups=mesh['dp'=4,'ctx'=16,'mp'=8] {'dp'}, use_global_device_ids=true, to_apply=%region_10.11 | all-reduce | flops 2048 | bytes 16384 | tf_op jit(solution)/shard_map/psum | solution.py:194
  (106 shorter events, 41.5 us)
Async XLA Ops:
  3.3 18.5 %collective-permute-start.1 = (bf16[64,1168]{0,1:T(8,128)(2,1)S(1)}, bf16[64,1168]{0,1:T(8,128)(2,1)S(1)}, u32[]{:S(2)}, u32[]{:S(2)}) collective-permute-start(bf16[64,1168]{0,1:T(8,128)(2,1)S(1)} %pad_maximum_fusion.1), channel_id=1, source_target_pairs={{0,8},{8,16},{16,24},{24,32},{32,40},{40,48},{48,56},{56,64},{64,7... | collective-permute-start | bytes 448520 | tf_op jit(solution)/shard_map/ppermute | solution.py:30
  7.1 22.4 %collective-permute-start.9 = (bf16[64,1168]{0,1:T(8,128)(2,1)S(1)}, bf16[64,1168]{0,1:T(8,128)(2,1)S(1)}, u32[]{:S(2)}, u32[]{:S(2)}) collective-permute-start(bf16[64,1168]{0,1:T(8,128)(2,1)S(1)} %pad_maximum_fusion.1), channel_id=1, source_target_pairs={{0,120},{8,0},{16,8},{24,16},{32,24},{40,32},{48,40},{56,48},{64,5... | collective-permute-start | bytes 448520 | tf_op jit(solution)/shard_map/ppermute | solution.py:33
  21.8 12.9 %collective-permute-start.2 = (bf16[64,1168]{0,1:T(8,128)(2,1)S(1)}, bf16[64,1168]{0,1:T(8,128)(2,1)S(1)}, u32[]{:S(2)}, u32[]{:S(2)}) collective-permute-start(bf16[64,1168]{0,1:T(8,128)(2,1)S(1)} %collective-permute-done.1), channel_id=1, source_target_pairs={{0,8},{8,16},{16,24},{24,32},{32,40},{40,48},{48,56},{56,64},{64,7... | collective-permute-start | bytes 448520 | tf_op jit(solution)/shard_map/ppermute | solution.py:30
  27.7 8.9 %collective-permute-start = (bf16[8,4096]{1,0:T(8,128)(2,1)S(1)}, bf16[8,4096]{1,0:T(8,128)(2,1)S(1)}, u32[]{:S(2)}, u32[]{:S(2)}) collective-permute-start(bf16[8,4096]{1,0:T(8,128)(2,1)S(1)} %copy.102), channel_id=1, source_target_pairs={{0,8},{8,16},{16,24},{24,32},{32,40},{40,48},{48,56},{56,64},{64,7... | collective-permute-start | bytes 196616 | tf_op jit(solution)/shard_map/ppermute | solution.py:18
  29.6 13.1 %collective-permute-start.10 = (bf16[64,1168]{0,1:T(8,128)(2,1)S(1)}, bf16[64,1168]{0,1:T(8,128)(2,1)}, u32[]{:S(2)}, u32[]{:S(2)}) collective-permute-start(bf16[64,1168]{0,1:T(8,128)(2,1)S(1)} %collective-permute-done.9), channel_id=1, source_target_pairs={{0,120},{8,0},{16,8},{24,16},{32,24},{40,32},{48,40},{56,48},{64,5... | collective-permute-start | bytes 448520 | tf_op jit(solution)/shard_map/ppermute | solution.py:33
  34.7 13.1 %collective-permute-start.3 = (bf16[64,1168]{0,1:T(8,128)(2,1)S(1)}, bf16[64,1168]{0,1:T(8,128)(2,1)}, u32[]{:S(2)}, u32[]{:S(2)}) collective-permute-start(bf16[64,1168]{0,1:T(8,128)(2,1)S(1)} %collective-permute-done.2), channel_id=1, source_target_pairs={{0,8},{8,16},{16,24},{24,32},{32,40},{40,48},{48,56},{56,64},{64,7... | collective-permute-start | bytes 448520 | tf_op jit(solution)/shard_map/ppermute | solution.py:30
  37.9 73.7 %all-to-all-start = ((bf16[4,136,1024]{2,1,0:T(8,128)(2,1)}), bf16[4,136,1024]{2,1,0:T(8,128)(2,1)}, u32[]{:S(2)}, u32[]{:S(2)}) async-start(bf16[4,136,1024]{2,1,0:T(8,128)(2,1)} %bitcast.76), calls=%async_computation | async-start | bytes 2228224 | tf_op jit(solution)/shard_map/all_to_all | solution.py:125
  42.7 10.0 %collective-permute-start.11 = (bf16[64,1168]{0,1:T(8,128)(2,1)}, bf16[64,1168]{0,1:T(8,128)(2,1)S(1)}, u32[]{:S(2)}, u32[]{:S(2)}) collective-permute-start(bf16[64,1168]{0,1:T(8,128)(2,1)} %collective-permute-done.10), channel_id=1, source_target_pairs={{0,120},{8,0},{16,8},{24,16},{32,24},{40,32},{48,40},{56,48},{64,5... | collective-permute-start | bytes 448520 | tf_op jit(solution)/shard_map/ppermute | solution.py:33
  47.8 10.4 %collective-permute-start.4 = (bf16[64,1168]{0,1:T(8,128)(2,1)}, bf16[64,1168]{0,1:T(8,128)(2,1)S(1)}, u32[]{:S(2)}, u32[]{:S(2)}) collective-permute-start(bf16[64,1168]{0,1:T(8,128)(2,1)} %collective-permute-done.3), channel_id=1, source_target_pairs={{0,8},{8,16},{16,24},{24,32},{32,40},{40,48},{48,56},{56,64},{64,7... | collective-permute-start | bytes 448520 | tf_op jit(solution)/shard_map/ppermute | solution.py:30
  52.7 9.8 %collective-permute-start.12 = (bf16[64,1168]{0,1:T(8,128)(2,1)S(1)}, bf16[64,1168]{0,1:T(8,128)(2,1)S(1)}, u32[]{:S(2)}, u32[]{:S(2)}) collective-permute-start(bf16[64,1168]{0,1:T(8,128)(2,1)S(1)} %collective-permute-done.11), channel_id=1, source_target_pairs={{0,120},{8,0},{16,8},{24,16},{32,24},{40,32},{48,40},{56,48},{64,5... | collective-permute-start | bytes 448520 | tf_op jit(solution)/shard_map/ppermute | solution.py:33
  58.2 9.9 %collective-permute-start.5 = (bf16[64,1168]{0,1:T(8,128)(2,1)S(1)}, bf16[64,1168]{0,1:T(8,128)(2,1)S(1)}, u32[]{:S(2)}, u32[]{:S(2)}) collective-permute-start(bf16[64,1168]{0,1:T(8,128)(2,1)S(1)} %collective-permute-done.4), channel_id=1, source_target_pairs={{0,8},{8,16},{16,24},{24,32},{32,40},{40,48},{48,56},{56,64},{64,7... | collective-permute-start | bytes 448520 | tf_op jit(solution)/shard_map/ppermute | solution.py:30
  62.5 9.9 %collective-permute-start.13 = (bf16[64,1168]{0,1:T(8,128)(2,1)S(1)}, bf16[64,1168]{0,1:T(8,128)(2,1)S(1)}, u32[]{:S(2)}, u32[]{:S(2)}) collective-permute-start(bf16[64,1168]{0,1:T(8,128)(2,1)S(1)} %collective-permute-done.12), channel_id=1, source_target_pairs={{0,120},{8,0},{16,8},{24,16},{32,24},{40,32},{48,40},{56,48},{64,5... | collective-permute-start | bytes 448520 | tf_op jit(solution)/shard_map/ppermute | solution.py:33
  68.1 9.9 %collective-permute-start.6 = (bf16[64,1168]{0,1:T(8,128)(2,1)S(1)}, bf16[64,1168]{0,1:T(8,128)(2,1)S(1)}, u32[]{:S(2)}, u32[]{:S(2)}) collective-permute-start(bf16[64,1168]{0,1:T(8,128)(2,1)S(1)} %collective-permute-done.5), channel_id=1, source_target_pairs={{0,8},{8,16},{16,24},{24,32},{32,40},{40,48},{48,56},{56,64},{64,7... | collective-permute-start | bytes 448520 | tf_op jit(solution)/shard_map/ppermute | solution.py:30
  72.3 10.1 %collective-permute-start.14 = (bf16[64,1168]{0,1:T(8,128)(2,1)S(1)}, bf16[64,1168]{0,1:T(8,128)(2,1)}, u32[]{:S(2)}, u32[]{:S(2)}) collective-permute-start(bf16[64,1168]{0,1:T(8,128)(2,1)S(1)} %collective-permute-done.13), channel_id=1, source_target_pairs={{0,120},{8,0},{16,8},{24,16},{32,24},{40,32},{48,40},{56,48},{64,5... | collective-permute-start | bytes 448520 | tf_op jit(solution)/shard_map/ppermute | solution.py:33
  78.0 10.5 %collective-permute-start.7 = (bf16[64,1168]{0,1:T(8,128)(2,1)S(1)}, bf16[64,1168]{0,1:T(8,128)(2,1)}, u32[]{:S(2)}, u32[]{:S(2)}) collective-permute-start(bf16[64,1168]{0,1:T(8,128)(2,1)S(1)} %collective-permute-done.6), channel_id=1, source_target_pairs={{0,8},{8,16},{16,24},{24,32},{32,40},{40,48},{48,56},{56,64},{64,7... | collective-permute-start | bytes 448520 | tf_op jit(solution)/shard_map/ppermute | solution.py:30
  82.4 10.3 %collective-permute-start.15 = (bf16[64,1168]{0,1:T(8,128)(2,1)}, bf16[64,1168]{0,1:T(8,128)(2,1)}, u32[]{:S(2)}, u32[]{:S(2)}) collective-permute-start(bf16[64,1168]{0,1:T(8,128)(2,1)} %collective-permute-done.14), channel_id=1, source_target_pairs={{0,120},{8,0},{16,8},{24,16},{32,24},{40,32},{48,40},{56,48},{64,5... | collective-permute-start | bytes 448520 | tf_op jit(solution)/shard_map/ppermute | solution.py:33
  88.4 10.2 %collective-permute-start.8 = (bf16[64,1168]{0,1:T(8,128)(2,1)}, bf16[64,1168]{0,1:T(8,128)(2,1)}, u32[]{:S(2)}, u32[]{:S(2)}) collective-permute-start(bf16[64,1168]{0,1:T(8,128)(2,1)} %collective-permute-done.7), channel_id=1, source_target_pairs={{0,8},{8,16},{16,24},{24,32},{32,40},{40,48},{48,56},{56,64},{64,7... | collective-permute-start | bytes 448520 | tf_op jit(solution)/shard_map/ppermute | solution.py:30
  116.5 15.9 %copy-start.5 = (f32[16]{0:T(128)S(1)}, f32[16]{0:T(128)}, u32[]{:S(2)}) copy-start(f32[16]{0:T(128)} %param.18) | copy-start | bytes 196
  116.5 15.6 %all-to-all-start.1 = ((bf16[4,136,1168]{2,1,0:T(8,128)(2,1)}), bf16[4,136,1168]{2,1,0:T(8,128)(2,1)S(1)}, u32[]{:S(2)}, u32[]{:S(2)}) async-start(bf16[4,136,1168]{2,1,0:T(8,128)(2,1)} %convolution_convert_fusion), calls=%async_computation.1 | async-start | bytes 2785280 | tf_op jit(solution)/shard_map/all_to_all | solution.py:127
  133.3 7.3 %collective-permute-start.16 = (bf16[128,128]{1,0:T(8,128)(2,1)S(1)}, bf16[128,128]{1,0:T(8,128)(2,1)S(1)}, u32[]{:S(2)}, u32[]{:S(2)}) collective-permute-start(bf16[128,128]{1,0:T(8,128)(2,1)S(1)} %slice.142), channel_id=1, source_target_pairs={{4,0},{0,1},{5,2},{1,3},{6,4},{2,5},{7,6},{3,7},{12,8},{8,9},{13,1... | collective-permute-start | bytes 98312 | tf_op jit(solution)/shard_map/ppermute | solution.py:157
  135.3 5.4 %collective-permute-start.17 = (bf16[128,128]{1,0:T(8,128)(2,1)S(1)}, bf16[128,128]{1,0:T(8,128)(2,1)S(1)}, u32[]{:S(2)}, u32[]{:S(2)}) collective-permute-start(bf16[128,128]{1,0:T(8,128)(2,1)S(1)} %slice.142), channel_id=1, source_target_pairs={{0,0},{4,1},{1,2},{5,3},{2,4},{6,5},{3,6},{7,7},{8,8},{12,9},{9,10... | collective-permute-start | bytes 98312 | tf_op jit(solution)/shard_map/ppermute | solution.py:156
  141.6 27.6 %all-to-all-start.2 = ((bf16[16,72,128]{2,1,0:T(8,128)(2,1)}), bf16[16,72,128]{2,1,0:T(8,128)(2,1)S(1)}, u32[]{:S(2)}, u32[]{:S(2)}) async-start(bf16[16,72,128]{2,1,0:T(8,128)(2,1)} %pad_maximum_fusion.2), calls=%async_computation.2 | async-start | bytes 589824 | tf_op jit(solution)/shard_map/all_to_all | solution.py:51
  172.0 57.0 %all-to-all-start.3 = ((bf16[16,64,128]{2,1,0:T(8,128)(2,1)}), bf16[16,64,128]{2,1,0:T(8,128)(2,1)S(1)}, u32[]{:S(2)}, u32[]{:S(2)}) async-start(bf16[16,64,128]{2,1,0:T(8,128)(2,1)} %copy.118), calls=%async_computation.3 | async-start | bytes 524288 | tf_op jit(solution)/shard_map/all_to_all | solution.py:65
  181.0 48.1 %copy-start.6 = (f32[16]{0:T(128)S(1)}, f32[16]{0:T(128)}, u32[]{:S(2)}) copy-start(f32[16]{0:T(128)} %param.20) | copy-start | bytes 196
  (6 other events, 40.6 us)

commit v6 on v4

--- a/solution.py
+++ b/solution.py
@@ -106,31 +106,38 @@
     extended = jnp.concatenate([earlier, rotated], 0)
     outgoing = extended.reshape(tok_rows + rim, seqs, share).transpose(1, 0, 2)
     incoming = lax.all_to_all(outgoing, "dp", 0, 0)
-    partials = jnp.einsum("kti,io->kto", incoming, panel, preferred_element_type=jnp.float32)
-    returned = lax.all_to_all(partials.astype(jnp.bfloat16), "dp", 0, 0)
-    both_ext = jnp.sum(returned.astype(jnp.float32), 0)
-    both = both_ext[rim:]
     x_end = x_weight.shape[1]
     bc_end = x_end + bc_weight.shape[1]
-    projected = (both[:, :x_end], both[:, x_end:bc_end], both[:, bc_end:])
-    x_cols = x_weight.shape[1]
-    joined_ext = both_ext[:, :bc_end].astype(jnp.bfloat16)
-    dt_proj = lax.optimization_barrier(projected[2].astype(jnp.bfloat16))
-    conv_taps = jnp.concatenate([conv_x, conv_bc], 1)
-    kernel = conv_taps.shape[0] - 1
-    padded = joined_ext[rim - (kernel - 1) :]
-    conv_sum = conv_taps[kernel]
-    for tap_index in range(kernel):
-        conv_sum = conv_sum + conv_taps[tap_index] * padded[tap_index : tap_index + tok_rows]
-    convolved = jax.nn.silu(conv_sum).astype(jnp.bfloat16)
-    x_conv = convolved[:, :x_cols]
+    side_partials = jnp.einsum(
+        "kti,io->kto", incoming, panel[:, x_end:], preferred_element_type=jnp.float32
+    )
+    side_back = lax.all_to_all(side_partials.astype(jnp.bfloat16), "dp", 0, 0)
+    x_partials = jnp.einsum(
+        "kti,io->kto", incoming, panel[:, :x_end], preferred_element_type=jnp.float32
+    )
+    x_back = lax.all_to_all(x_partials.astype(jnp.bfloat16), "dp", 0, 0)
+    side_ext = jnp.sum(side_back.astype(jnp.float32), 0)
+    x_ext = jnp.sum(x_back.astype(jnp.float32), 0)
+    x_cols = x_end
+    bc_width = bc_end - x_end
+    dt_proj = lax.optimization_barrier(side_ext[rim:, bc_width:].astype(jnp.bfloat16))
+    kernel = conv_x.shape[0] - 1
+
+    def causal_conv(rows, taps):
+        padded = rows.astype(jnp.bfloat16)[rim - (kernel - 1) :]
+        total = taps[kernel]
+        for tap_index in range(kernel):
+            total = total + taps[tap_index] * padded[tap_index : tap_index + tok_rows]
+        return jax.nn.silu(total).astype(jnp.bfloat16)
+
+    bc_own = causal_conv(side_ext[:, :bc_width], conv_bc)
+    x_conv = causal_conv(x_ext, conv_x)
     heads_dev = dt_weight.shape[1]
     head_size = x_cols // heads_dev
     per_group = HEADS // G
     groups_here = max(1, heads_dev // per_group)
     heads_local = heads_dev // groups_here
     first_group = lax.axis_index("mp") * heads_dev // per_group
-    bc_own = convolved[:, x_cols:]
     mp_count = lax.axis_size("mp")
     if bc_own.shape[1] == NS and mp_count == 2 * G and groups_here == 1:
         owner = [m * heads_dev // per_group for m in range(mp_count)]

time: 186 us -> 183 us (0.984)
  blocking collectives: 60.2 us -> 44.6 us
  starting transfers between devices: 25.7 us -> 35 us
    all_to_all x1 -> x0, blocking collectives: 15.6 us -> none  [shards(): incoming = lax.all_to_all(outgoing, 'dp', 0, 0)]
    all_to_all x1 -> x3, starting transfers between devices: 4.92 us -> 17.7 us  [the longest x1 7.28 us: shards(): incoming = lax.all_to_all(outgoing, 'dp', 0, 0)]
    all_to_all x1 -> x3, waiting for transfers between devices: 10.5 us -> 16.9 us  [the longest x1 9.11 us: shards(): incoming = lax.all_to_all(outgoing, 'dp', 0, 0)]
    ppermute x1, waiting for transfers between devices: 4.1 us -> 0.01 us  [shards(): got_b = lax.ppermute(bc_own, 'mp', even_first)]
    all_to_all x1, starting transfers between devices: 8.81 us -> 5.57 us  [entering(): returned = lax.all_to_all(carried.astype(jnp.bfloat16), axis, 0, 0)]
    all_to_all x1, waiting for transfers between devices: 17.3 us -> 19.4 us  [entering(): incoming = lax.all_to_all(outgoing, axis, 0, 0).astype(jnp.float32)]
    all_gather x1, waiting for transfers between devices: 9.73 us -> 7.79 us  [shards(): panel = lax.all_gather(local_panel, 'ctx', axis=0, tiled=True)]
    dot_general x1 -> x2, matrix products: 4.43 us -> 6.14 us  [the longest x1 3.94 us: shards(): jnp.einsum('kti,io->kto', incoming, panel[:, :x_end], preferred_element_t...]
  transfers between devices with their start and end apart: 7 -> 9, of which waited for: 6 -> 7; matrix products, arithmetic and copies ran while one was open for 5% -> 9% of each run, Pallas kernels for 0% -> 0%
where the time goes in v6:
time: 183 us; the launch traced here: 182 us
  waiting for transfers between devices  62.7 us (34%)
  blocking collectives  44.6 us (24%)
  starting transfers between devices  35 us (19%)
  between operations  14.5 us (8%)
  matrix products  12.1 us (7%)
  local copies, waits for them, and re-layouts  7.15 us (4%)
  other arithmetic  6.01 us (3%)
    psum x2, blocking collectives, shards(): totals = lax.psum(lax.psum(powers, 'ctx'), 'dp')  44.6 us
    all_to_all x1, waiting for transfers between devices, entering(): incoming = lax.all_to_all(outgoing, axis, 0, 0).astype(jnp.float32)  19.4 us
    all_to_all x1, waiting for transfers between devices, entering(): returned = lax.all_to_all(carried.astype(jnp.bfloat16), axis, 0, 0)  16.5 us
    all_to_all x1, waiting for transfers between devices, shards(): incoming = lax.all_to_all(outgoing, 'dp', 0, 0)  9.11 us
    all_gather x1, waiting for transfers between devices, shards(): panel = lax.all_gather(local_panel, 'ctx', axis=0, tiled=True)  7.79 us
    all_to_all x1, starting transfers between devices, entering(): incoming = lax.all_to_all(outgoing, axis, 0, 0).astype(jnp.float32)  7.42 us
    all_to_all x1, starting transfers between devices, shards(): incoming = lax.all_to_all(outgoing, 'dp', 0, 0)  7.28 us
    all_to_all x1, starting transfers between devices, shards(): x_back = lax.all_to_all(x_partials.astype(jnp.bfloat16), 'dp', 0, 0)  5.57 us
  transfers between devices with their start and end apart: 9, of which 7 were waited for; matrix products, arithmetic and copies ran while one was open for 9% of the time, Pallas kernels for 0%

profile of v6, /device:TPU:6, one launch (start us, length us, event | category | flops | bytes accessed | tf_op | source)
XLA Modules:
  0.0 182.0 jit_solution(14899012043355915375)
XLA Ops:
  8.0 1.6 pad_maximum_fusion.2
  9.6 1.6 copy.134
  11.2 0.9 convolution_bitcast_fusion
  12.1 3.3 %multiply_convert_fusion = bf16[128,64,64]{0,2,1:T(8,128)(2,1)S(1)} fusion(f32[128,64,64]{0,1,2:T(8,128)S(1)} %convolution_bitcast_fusion), kind=kOutput, calls=%fused_computation.5 | convolution fusion | flops 403791872 | bytes 3145728 | tf_op jit(solution)/shard_map/tcb,bd->tcd/dot_general | solution.py:81
  15.8 37.0 %psum.14 = f32[4,512]{1,0:T(4,128)S(1)} all-reduce(f32[4,512]{1,0:T(4,128)S(1)} %pad_maximum_fusion.3), channel_id=1, replica_groups=mesh['dp'=4,'ctx'=16,'mp'=8] {'ctx'}, use_global_device_ids=true, to_apply=%region_4.0 | all-reduce | flops 2048 | bytes 16384 | tf_op jit(solution)/shard_map/psum | solution.py:97
  52.8 7.6 %psum.15 = f32[4,512]{1,0:T(4,128)S(1)} all-reduce(f32[4,512]{1,0:T(4,128)S(1)} %psum.14), channel_id=1, replica_groups=mesh['dp'=4,'ctx'=16,'mp'=8] {'dp'}, use_global_device_ids=true, to_apply=%region_5.0 | all-reduce | flops 2048 | bytes 16384 | tf_op jit(solution)/shard_map/psum | solution.py:97
  61.0 1.7 collective-permute-start
  62.7 2.1 %collective-permute-done = bf16[8,4096]{1,0:T(8,128)(2,1)S(1)} collective-permute-done((bf16[8,4096]{1,0:T(8,128)(2,1)S(1)}, bf16[8,4096]{1,0:T(8,128)(2,1)S(1)}, u32[]{:S(2)}, u32[]{:S(2)}) %collective-permute-start) | collective-permute-done | bytes 65568 | tf_op jit(solution)/shard_map/ppermute | solution.py:18
  65.0 1.1 copy.169
  66.1 7.3 %all-to-all-start = ((bf16[4,136,1024]{2,1,0:T(8,128)(2,1)}), bf16[4,136,1024]{2,1,0:T(8,128)(2,1)S(1)}, u32[]{:S(2)}, u32[]{:S(2)}) async-start(bf16[4,136,1024]{2,1,0:T(8,128)(2,1)} %bitcast.91), calls=%async_computation | async-start | bytes 2228224 | tf_op jit(solution)/shard_map/all_to_all | solution.py:108
  73.4 9.1 %all-to-all-done = bf16[4,136,1024]{2,1,0:T(8,128)(2,1)S(1)} async-done(((bf16[4,136,1024]{2,1,0:T(8,128)(2,1)}), bf16[4,136,1024]{2,1,0:T(8,128)(2,1)S(1)}, u32[]{:S(2)}, u32[]{:S(2)}) %all-to-all-start) | async-done | bytes 1114144 | tf_op jit(solution)/shard_map/all_to_all | solution.py:108
  82.5 7.8 %all-gather.2.cloned.1.call-done = bf16[1024,1168]{1,0:T(8,128)(2,1)} async-done(((bf16[64,1168]{1,0:T(8,128)(2,1)}), bf16[1024,1168]{1,0:T(8,128)(2,1)}) %all-gather.2.cloned.1.call-update) | async-done | bytes 2392080 | tf_op jit(solution)/shard_map/all_gather | solution.py:101
  90.3 2.2 %convolution_convert_fusion = bf16[4,136,144]{2,1,0:T(8,128)(2,1)} fusion(bf16[4,136,1024]{2,1,0:T(8,128)(2,1)S(1)} %all-to-all-done, bf16[1024,1168]{1,0:T(8,128)(2,1)} %all-gather.2.cloned.1.call-done), kind=kOutput, calls=%fused_computation.13 | convolution fusion | flops 160510464 | bytes 1795072 | tf_op jit(solution)/shard_map/kti,io->kto/dot_general | solution.py:111
  92.5 4.8 %all-to-all-start.2 = ((bf16[4,136,144]{2,1,0:T(8,128)(2,1)}), bf16[4,136,144]{2,1,0:T(8,128)(2,1)S(1)}, u32[]{:S(2)}, u32[]{:S(2)}) async-start(bf16[4,136,144]{2,1,0:T(8,128)(2,1)} %convolution_convert_fusion), calls=%async_computation.2 | async-start | bytes 557056 | tf_op jit(solution)/shard_map/all_to_all | solution.py:114
  97.3 3.9 %fusion.5 = bf16[4,136,1024]{2,1,0:T(8,128)(2,1)} fusion(bf16[4,136,1024]{2,1,0:T(8,128)(2,1)S(1)} %all-to-all-done, bf16[1024,1168]{1,0:T(8,128)(2,1)} %all-gather.2.cloned.1.call-done), kind=kOutput, calls=%fused_computation.7 | convolution fusion | flops 1141407744 | bytes 4325376 | tf_op jit(solution)/shard_map/kti,io->kto/dot_general | solution.py:115
  101.3 2.2 %all-to-all-done.2 = bf16[4,136,144]{2,1,0:T(8,128)(2,1)S(1)} async-done(((bf16[4,136,144]{2,1,0:T(8,128)(2,1)}), bf16[4,136,144]{2,1,0:T(8,128)(2,1)S(1)}, u32[]{:S(2)}, u32[]{:S(2)}) %all-to-all-start.2) | async-done | bytes 156704 | tf_op jit(solution)/shard_map/all_to_all | solution.py:114
  103.5 5.6 %all-to-all-start.1 = ((bf16[4,136,1024]{2,1,0:T(8,128)(2,1)}), bf16[4,136,1024]{2,1,0:T(8,128)(2,1)S(1)}, u32[]{:S(2)}, u32[]{:S(2)}) async-start(bf16[4,136,1024]{2,1,0:T(8,128)(2,1)} %fusion.5), calls=%async_computation.1 | async-start | bytes 2228224 | tf_op jit(solution)/shard_map/all_to_all | solution.py:118
  109.2 1.9 %collective-permute-start.1 = (bf16[128,128]{1,0:T(8,128)(2,1)S(1)}, bf16[128,128]{1,0:T(8,128)(2,1)S(1)}, u32[]{:S(2)}, u32[]{:S(2)}) collective-permute-start(bf16[128,128]{1,0:T(8,128)(2,1)S(1)} %multiply_convert_fusion.6), channel_id=1, source_target_pairs={{4,0},{0,1},{5,2},{1,3},{6,4},{2,5},{7,6},{3,7},{12,8},{8,9},{13,1... | collective-permute-start | bytes 98312 | tf_op jit(solution)/shard_map/ppermute | solution.py:147
  112.7 5.5 %all-to-all-done.1 = bf16[4,136,1024]{2,1,0:T(8,128)(2,1)S(1)} async-done(((bf16[4,136,1024]{2,1,0:T(8,128)(2,1)}), bf16[4,136,1024]{2,1,0:T(8,128)(2,1)S(1)}, u32[]{:S(2)}, u32[]{:S(2)}) %all-to-all-start.1) | async-done | bytes 1114144 | tf_op jit(solution)/shard_map/all_to_all | solution.py:118
  120.0 7.4 %all-to-all-start.3 = ((bf16[16,72,128]{2,1,0:T(8,128)(2,1)}), bf16[16,72,128]{2,1,0:T(8,128)(2,1)S(1)}, u32[]{:S(2)}, u32[]{:S(2)}) async-start(bf16[16,72,128]{2,1,0:T(8,128)(2,1)} %pad_maximum_fusion.1), calls=%async_computation.3 | async-start | bytes 589824 | tf_op jit(solution)/shard_map/all_to_all | solution.py:31
  127.6 19.4 %all-to-all-done.3 = bf16[16,72,128]{2,1,0:T(8,128)(2,1)S(1)} async-done(((bf16[16,72,128]{2,1,0:T(8,128)(2,1)}), bf16[16,72,128]{2,1,0:T(8,128)(2,1)S(1)}, u32[]{:S(2)}, u32[]{:S(2)}) %all-to-all-start.3) | async-done | bytes 294944 | tf_op jit(solution)/shard_map/all_to_all | solution.py:31
  147.1 1.0 select_reduce_fusion
  149.8 5.6 %all-to-all-start.4 = ((bf16[16,64,128]{2,1,0:T(8,128)(2,1)}), bf16[16,64,128]{2,1,0:T(8,128)(2,1)S(1)}, u32[]{:S(2)}, u32[]{:S(2)}) async-start(bf16[16,64,128]{2,1,0:T(8,128)(2,1)} %copy.153), calls=%async_computation.4 | async-start | bytes 524288 | tf_op jit(solution)/shard_map/all_to_all | solution.py:45
  157.2 16.5 %all-to-all-done.4 = bf16[16,64,128]{2,1,0:T(8,128)(2,1)S(1)} async-done(((bf16[16,64,128]{2,1,0:T(8,128)(2,1)}), bf16[16,64,128]{2,1,0:T(8,128)(2,1)S(1)}, u32[]{:S(2)}, u32[]{:S(2)}) %all-to-all-start.4) | async-done | bytes 262176 | tf_op jit(solution)/shard_map/all_to_all | solution.py:45
  (73 shorter events, 10.3 us)
Async XLA Ops:
  7.2 83.1 %all-gather.2.cloned.1.call-start = ((), (), s32[]{:S(2)}) async-start(), calls=%async_computation.5 | async-start | bytes 2785280 | tf_op jit(solution)/shard_map/all_gather | solution.py:101
  61.0 3.8 %collective-permute-start = (bf16[8,4096]{1,0:T(8,128)(2,1)S(1)}, bf16[8,4096]{1,0:T(8,128)(2,1)S(1)}, u32[]{:S(2)}, u32[]{:S(2)}) collective-permute-start(bf16[8,4096]{1,0:T(8,128)(2,1)S(1)} %slice.166), channel_id=1, source_target_pairs={{0,8},{8,16},{16,24},{24,32},{32,40},{40,48},{48,56},{56,64},{64,7... | collective-permute-start | bytes 196616 | tf_op jit(solution)/shard_map/ppermute | solution.py:18
  64.9 8.4 %copy-start.5 = (f32[16]{0:T(128)S(1)}, f32[16]{0:T(128)}, u32[]{:S(2)}) copy-start(f32[16]{0:T(128)} %param.19) | copy-start | bytes 196
  64.9 8.4 %copy-start.3 = (f32[5,128]{1,0:T(8,128)S(1)}, f32[5,128]{1,0:T(8,128)}, u32[]{:S(2)}) copy-start(f32[5,128]{1,0:T(8,128)} %param.17) | copy-start | bytes 7684
  65.0 8.4 %copy-start = (f32[5,1024]{1,0:T(8,128)S(1)}, f32[5,1024]{1,0:T(8,128)}, u32[]{:S(2)}) copy-start(f32[5,1024]{1,0:T(8,128)} %param.16) | copy-start | bytes 61444
  66.1 16.5 %all-to-all-start = ((bf16[4,136,1024]{2,1,0:T(8,128)(2,1)}), bf16[4,136,1024]{2,1,0:T(8,128)(2,1)S(1)}, u32[]{:S(2)}, u32[]{:S(2)}) async-start(bf16[4,136,1024]{2,1,0:T(8,128)(2,1)} %bitcast.91), calls=%async_computation | async-start | bytes 2228224 | tf_op jit(solution)/shard_map/all_to_all | solution.py:108
  92.5 11.0 %all-to-all-start.2 = ((bf16[4,136,144]{2,1,0:T(8,128)(2,1)}), bf16[4,136,144]{2,1,0:T(8,128)(2,1)S(1)}, u32[]{:S(2)}, u32[]{:S(2)}) async-start(bf16[4,136,144]{2,1,0:T(8,128)(2,1)} %convolution_convert_fusion), calls=%async_computation.2 | async-start | bytes 557056 | tf_op jit(solution)/shard_map/all_to_all | solution.py:114
  101.3 10.6 %copy-start.2 = (f32[16]{0:T(128)S(1)}, f32[16]{0:T(128)}, u32[]{:S(2)}) copy-start(f32[16]{0:T(128)} %param.18) | copy-start | bytes 196
  103.5 14.7 %all-to-all-start.1 = ((bf16[4,136,1024]{2,1,0:T(8,128)(2,1)}), bf16[4,136,1024]{2,1,0:T(8,128)(2,1)S(1)}, u32[]{:S(2)}, u32[]{:S(2)}) async-start(bf16[4,136,1024]{2,1,0:T(8,128)(2,1)} %fusion.5), calls=%async_computation.1 | async-start | bytes 2228224 | tf_op jit(solution)/shard_map/all_to_all | solution.py:118
  109.2 9.8 %collective-permute-start.1 = (bf16[128,128]{1,0:T(8,128)(2,1)S(1)}, bf16[128,128]{1,0:T(8,128)(2,1)S(1)}, u32[]{:S(2)}, u32[]{:S(2)}) collective-permute-start(bf16[128,128]{1,0:T(8,128)(2,1)S(1)} %multiply_convert_fusion.6), channel_id=1, source_target_pairs={{4,0},{0,1},{5,2},{1,3},{6,4},{2,5},{7,6},{3,7},{12,8},{8,9},{13,1... | collective-permute-start | bytes 98312 | tf_op jit(solution)/shard_map/ppermute | solution.py:147
  111.2 7.9 %collective-permute-start.2 = (bf16[128,128]{1,0:T(8,128)(2,1)S(1)}, bf16[128,128]{1,0:T(8,128)(2,1)S(1)}, u32[]{:S(2)}, u32[]{:S(2)}) collective-permute-start(bf16[128,128]{1,0:T(8,128)(2,1)S(1)} %multiply_convert_fusion.6), channel_id=1, source_target_pairs={{0,0},{4,1},{1,2},{5,3},{2,4},{6,5},{3,6},{7,7},{8,8},{12,9},{9,10... | collective-permute-start | bytes 98312 | tf_op jit(solution)/shard_map/ppermute | solution.py:146
  120.0 35.3 %copy-start.1 = (f32[1024]{0:T(1024)S(1)}, f32[1024]{0:T(1024)}, u32[]{:S(2)}) copy-start(f32[1024]{0:T(1024)} %param.21) | copy-start | bytes 12292
  120.0 26.9 %all-to-all-start.3 = ((bf16[16,72,128]{2,1,0:T(8,128)(2,1)}), bf16[16,72,128]{2,1,0:T(8,128)(2,1)S(1)}, u32[]{:S(2)}, u32[]{:S(2)}) async-start(bf16[16,72,128]{2,1,0:T(8,128)(2,1)} %pad_maximum_fusion.1), calls=%async_computation.3 | async-start | bytes 589824 | tf_op jit(solution)/shard_map/all_to_all | solution.py:31
  149.8 24.0 %all-to-all-start.4 = ((bf16[16,64,128]{2,1,0:T(8,128)(2,1)}), bf16[16,64,128]{2,1,0:T(8,128)(2,1)S(1)}, u32[]{:S(2)}, u32[]{:S(2)}) async-start(bf16[16,64,128]{2,1,0:T(8,128)(2,1)} %copy.153), calls=%async_computation.4 | async-start | bytes 524288 | tf_op jit(solution)/shard_map/all_to_all | solution.py:45
  156.1 17.6 %copy-start.4 = (f32[16]{0:T(128)S(1)}, f32[16]{0:T(128)}, u32[]{:S(2)}) copy-start(f32[16]{0:T(128)} %param.20) | copy-start | bytes 196
Sparse Core Ops, SparseCore 0:
  10.7 79.6 all-gather.1

commit v7 on v6

--- a/solution.py
+++ b/solution.py
@@ -97,8 +97,13 @@
     totals = lax.psum(lax.psum(powers, "ctx"), "dp")
     totals, rotated = lax.optimization_barrier((totals, rotated))
     kurtosis = kurtosis_from(totals, row_count)
-    local_panel = jnp.concatenate([x_weight, bc_weight, dt_weight], 1)
-    panel = lax.all_gather(local_panel, "ctx", axis=0, tiled=True)
+    x_end = x_weight.shape[1]
+    half = x_end // 2
+    first_panel = lax.all_gather(
+        jnp.concatenate([x_weight[:, :half], bc_weight, dt_weight], 1), "ctx", axis=0, tiled=True
+    )
+    second_local, rotated = lax.optimization_barrier((x_weight[:, half:], rotated))
+    second_panel = lax.all_gather(second_local, "ctx", axis=0, tiled=True)
     seqs = lax.axis_size("dp")
     share = model_width // seqs
     rim = 8
@@ -106,20 +111,15 @@
     extended = jnp.concatenate([earlier, rotated], 0)
     outgoing = extended.reshape(tok_rows + rim, seqs, share).transpose(1, 0, 2)
     incoming = lax.all_to_all(outgoing, "dp", 0, 0)
-    x_end = x_weight.shape[1]
-    bc_end = x_end + bc_weight.shape[1]
-    side_partials = jnp.einsum(
-        "kti,io->kto", incoming, panel[:, x_end:], preferred_element_type=jnp.float32
-    )
-    side_back = lax.all_to_all(side_partials.astype(jnp.bfloat16), "dp", 0, 0)
-    x_partials = jnp.einsum(
-        "kti,io->kto", incoming, panel[:, :x_end], preferred_element_type=jnp.float32
-    )
-    x_back = lax.all_to_all(x_partials.astype(jnp.bfloat16), "dp", 0, 0)
-    side_ext = jnp.sum(side_back.astype(jnp.float32), 0)
-    x_ext = jnp.sum(x_back.astype(jnp.float32), 0)
+    def projected_rows(panel):
+        partials = jnp.einsum("kti,io->kto", incoming, panel, preferred_element_type=jnp.float32)
+        back = lax.all_to_all(partials.astype(jnp.bfloat16), "dp", 0, 0)
+        return jnp.sum(back.astype(jnp.float32), 0)
+
+    first_ext = projected_rows(first_panel)
+    side_ext = first_ext[:, half:]
     x_cols = x_end
-    bc_width = bc_end - x_end
+    bc_width = bc_weight.shape[1]
     dt_proj = lax.optimization_barrier(side_ext[rim:, bc_width:].astype(jnp.bfloat16))
     kernel = conv_x.shape[0] - 1
 
@@ -131,7 +131,7 @@
         return jax.nn.silu(total).astype(jnp.bfloat16)
 
     bc_own = causal_conv(side_ext[:, :bc_width], conv_bc)
-    x_conv = causal_conv(x_ext, conv_x)
+    x_conv_parts = [causal_conv(first_ext[:, :half], conv_x[:, :half])]
     heads_dev = dt_weight.shape[1]
     head_size = x_cols // heads_dev
     per_group = HEADS // G
@@ -169,18 +169,35 @@
         * decay_mask.reshape(groups_here, heads_local, tok_rows, tok_rows)
         * step_size.T.reshape(groups_here, heads_local, 1, tok_rows)
     ).astype(jnp.bfloat16)
+    head_share = heads_local // 2
+    factor = (jnp.exp(-(block_end - cumulative)) * step_size).reshape(
+        tok_rows, groups_here, heads_local
+    )
+    block_decay = jnp.exp(-block_end).reshape(groups_here, heads_local)
+    carried_parts = []
+    for part_index in range(2):
+        if part_index == 1:
+            second_panel, carried_parts[0] = lax.optimization_barrier(
+                (second_panel, carried_parts[0])
+            )
+            second_ext = projected_rows(second_panel)
+            x_conv_parts.append(causal_conv(second_ext, conv_x[:, half:]))
+        part = x_conv_parts[part_index]
+        heads_part = slice(part_index * head_share, (part_index + 1) * head_share)
+        update = (
+            factor[:, :, heads_part, None]
+            * part.reshape(tok_rows, groups_here, head_share, head_size)
+        ).astype(jnp.bfloat16)
+        contrib = jnp.einsum(
+            "sghp,sgn->ghpn", update, write_here, preferred_element_type=jnp.float32
+        )
+        carried_parts.append(entering(block_decay[:, heads_part], contrib, "ctx"))
+    carried = jnp.concatenate(carried_parts, 1)
+    x_conv = jnp.concatenate(x_conv_parts, 1)
     x_heads = x_conv.reshape(tok_rows, groups_here, heads_local, head_size)
     within_block = jnp.einsum(
         "ghts,sghp->tghp", weights, x_heads, preferred_element_type=jnp.float32
     )
-    update = (
-        (jnp.exp(-(block_end - cumulative)) * step_size).reshape(
-            tok_rows, groups_here, heads_local
-        )[..., None]
-        * x_heads
-    ).astype(jnp.bfloat16)
-    contrib = jnp.einsum("sghp,sgn->ghpn", update, write_here, preferred_element_type=jnp.float32)
-    carried = entering(jnp.exp(-block_end).reshape(groups_here, heads_local), contrib, "ctx")
     from_before = jnp.exp(-cumulative).reshape(tok_rows, groups_here, heads_local)[
         ..., None
     ] * jnp.einsum("tgn,ghpn->tghp", read_here.astype(jnp.float32), carried, precision=HIGH)

time: 183 us -> 238 us (1.30); the launches traced: 182 us -> 234 us
  blocking collectives: 44.6 us -> 91 us
  waiting for transfers between devices: 62.7 us -> 69.9 us
  starting transfers between devices: 35 us -> 31.8 us
    all_to_all x0 -> x3, blocking collectives: none -> 46.2 us  [the longest x1 19.8 us: entering(): returned = lax.all_to_all(carried.astype(jnp.bfloat16), axis, 0, 0)]
    all_to_all x3 -> x1, starting transfers between devices: 17.7 us -> 5 us  [projected_rows(): back = lax.all_to_all(partials.astype(jnp.bfloat16), 'dp', 0, 0)]
    all_to_all x3 -> x1, waiting for transfers between devices: 16.9 us -> 6.85 us  [projected_rows(): back = lax.all_to_all(partials.astype(jnp.bfloat16), 'dp', 0, 0)]
    all_to_all x1 -> x2, waiting for transfers between devices: 19.4 us -> 28.9 us  [entering(): incoming = lax.all_to_all(outgoing, axis, 0, 0).astype(jnp.float32)]
    all_gather x1 -> x2, waiting for transfers between devices: 7.79 us -> 17 us  [the longest x1 10.9 us: shards(): second_panel = lax.all_gather(second_local, 'ctx', axis=0, tiled=True)]
    all_to_all x1 -> x2, starting transfers between devices: 7.42 us -> 15.2 us  [entering(): incoming = lax.all_to_all(outgoing, axis, 0, 0).astype(jnp.float32)]
    all_to_all x1, waiting for transfers between devices: 16.5 us -> 11.9 us  [entering(): returned = lax.all_to_all(carried.astype(jnp.bfloat16), axis, 0, 0)]
    ppermute x1, starting transfers between devices: 1.92 us -> 4.81 us  [shards(): got_b = lax.ppermute(bc_own, 'mp', even_first)]
  transfers between devices with their start and end apart: 9 -> 9, of which waited for: 7 -> 8; matrix products, arithmetic and copies ran while one was open for 9% -> 5% of each run, Pallas kernels for 0% -> 0%
where the time goes in v7:
time: 238 us; the launch traced here: 234 us
  blocking collectives  91 us (38%)
  waiting for transfers between devices  69.9 us (29%)
  starting transfers between devices  31.8 us (13%)
  between operations  14.6 us (6%)
  matrix products  11.5 us (5%)
  local copies, waits for them, and re-layouts  7.87 us (3%)
  other arithmetic  7.68 us (3%)
    psum x2, blocking collectives, shards(): totals = lax.psum(lax.psum(powers, 'ctx'), 'dp')  44.7 us
    all_to_all x2, waiting for transfers between devices, entering(): incoming = lax.all_to_all(outgoing, axis, 0, 0).astype(jnp.float32)  28.9 us
    all_to_all x1, blocking collectives, entering(): returned = lax.all_to_all(carried.astype(jnp.bfloat16), axis, 0, 0)  19.8 us
    all_to_all x2, starting transfers between devices, entering(): incoming = lax.all_to_all(outgoing, axis, 0, 0).astype(jnp.float32)  15.2 us
    all_to_all x1, blocking collectives, shards(): incoming = lax.all_to_all(outgoing, 'dp', 0, 0)  15.1 us
    all_to_all x1, waiting for transfers between devices, entering(): returned = lax.all_to_all(carried.astype(jnp.bfloat16), axis, 0, 0)  11.9 us
    all_to_all x1, blocking collectives, projected_rows(): back = lax.all_to_all(partials.astype(jnp.bfloat16), 'dp', 0, 0)  11.4 us
    all_gather x1, waiting for transfers between devices, shards(): second_panel = lax.all_gather(second_local, 'ctx', axis=0, tiled=True)  10.9 us
  transfers between devices with their start and end apart: 9, of which 8 were waited for; matrix products, arithmetic and copies ran while one was open for 5% of the time, Pallas kernels for 0%

profile of v7, /device:TPU:6, one launch (start us, length us, event | category | flops | bytes accessed | tf_op | source)
XLA Modules:
  0.0 234.3 jit_solution(9584893080130262534)
XLA Ops:
  7.2 1.5 fusion.61
  10.9 1.6 copy.132
  13.4 3.3 %multiply_convert_fusion = bf16[128,64,64]{0,2,1:T(8,128)(2,1)S(1)} fusion(f32[128,64,64]{0,1,2:T(8,128)S(1)} %convolution_bitcast_fusion), kind=kOutput, calls=%fused_computation.4 | convolution fusion | flops 403791872 | bytes 3145728 | tf_op jit(solution)/shard_map/tcb,bd->tcd/dot_general | solution.py:81
  17.1 37.1 %psum.14 = f32[4,512]{1,0:T(4,128)S(1)} all-reduce(f32[4,512]{1,0:T(4,128)S(1)} %pad_maximum_fusion.5), channel_id=1, replica_groups=mesh['dp'=4,'ctx'=16,'mp'=8] {'ctx'}, use_global_device_ids=true, to_apply=%region_4.0 | all-reduce | flops 2048 | bytes 16384 | tf_op jit(solution)/shard_map/psum | solution.py:97
  54.2 7.6 %psum.15 = f32[4,512]{1,0:T(4,128)S(1)} all-reduce(f32[4,512]{1,0:T(4,128)S(1)} %psum.14), channel_id=1, replica_groups=mesh['dp'=4,'ctx'=16,'mp'=8] {'dp'}, use_global_device_ids=true, to_apply=%region_5.0 | all-reduce | flops 2048 | bytes 16384 | tf_op jit(solution)/shard_map/psum | solution.py:97
  62.4 1.6 collective-permute-start
  64.0 2.2 collective-permute-done
  66.4 15.1 %all_to_all.35 = bf16[4,136,1024]{2,1,0:T(8,128)(2,1)S(1)} all-to-all(bf16[4,136,1024]{2,1,0:T(8,128)(2,1)S(1)} %bitcast.132), channel_id=1, replica_groups=mesh['dp'=4,'ctx'=16,'mp'=8] {'dp'}, dimensions={0} | all-to-all | bytes 2228224 | tf_op jit(solution)/shard_map/all_to_all | solution.py:113
  81.5 6.1 %all-gather.3.cloned.1.call-done = bf16[1024,656]{1,0:T(8,128)(2,1)} async-done(((bf16[64,656]{1,0:T(8,128)(2,1)}), bf16[1024,656]{1,0:T(8,128)(2,1)}) %all-gather.3.cloned.1.call-update) | async-done | bytes 1343504 | tf_op jit(solution)/shard_map/all_gather | solution.py:102
  87.6 3.3 %fusion.6 = bf16[4,136,656]{2,1,0:T(8,128)(2,1)} fusion(bf16[4,136,1024]{2,1,0:T(8,128)(2,1)S(1)} %all_to_all.35, bf16[1024,656]{1,0:T(8,128)(2,1)} %all-gather.3.cloned.1.call-done), kind=kOutput, calls=%fused_computation.8 | convolution fusion | flops 731214336 | bytes 3171328 | tf_op jit(solution)/shard_map/kti,io->kto/dot_general | solution.py:115
  90.9 5.0 %all-to-all-start.1 = ((bf16[4,136,656]{2,1,0:T(8,128)(2,1)}), bf16[4,136,656]{2,1,0:T(8,128)(2,1)S(1)}, u32[]{:S(2)}, u32[]{:S(2)}) async-start(bf16[4,136,656]{2,1,0:T(8,128)(2,1)} %fusion.6), calls=%async_computation.1 | async-start | bytes 1671168 | tf_op jit(solution)/shard_map/all_to_all | solution.py:116
  96.8 6.9 %all-to-all-done.1 = bf16[4,136,656]{2,1,0:T(8,128)(2,1)S(1)} async-done(((bf16[4,136,656]{2,1,0:T(8,128)(2,1)}), bf16[4,136,656]{2,1,0:T(8,128)(2,1)S(1)}, u32[]{:S(2)}, u32[]{:S(2)}) %all-to-all-start.1) | async-done | bytes 713760 | tf_op jit(solution)/shard_map/all_to_all | solution.py:116
  104.5 4.8 %collective-permute-start.2 = (bf16[128,128]{1,0:T(8,128)(2,1)S(1)}, bf16[128,128]{1,0:T(8,128)(2,1)S(1)}, u32[]{:S(2)}, u32[]{:S(2)}) collective-permute-start(bf16[128,128]{1,0:T(8,128)(2,1)S(1)} %multiply_convert_fusion.8), channel_id=1, source_target_pairs={{4,0},{0,1},{5,2},{1,3},{6,4},{2,5},{7,6},{3,7},{12,8},{8,9},{13,1... | collective-permute-start | bytes 98312 | tf_op jit(solution)/shard_map/ppermute | solution.py:147
  110.4 2.2 collective-permute-done.2
  113.5 7.8 %all-to-all-start.2 = ((bf16[16,40,128]{2,1,0:T(8,128)(2,1)}), bf16[16,40,128]{2,1,0:T(8,128)(2,1)S(1)}, u32[]{:S(2)}, u32[]{:S(2)}) async-start(bf16[16,40,128]{2,1,0:T(8,128)(2,1)} %pad_maximum_fusion.2), calls=%async_computation.2 | async-start | bytes 327680 | tf_op jit(solution)/shard_map/all_to_all | solution.py:31
  121.4 16.4 %all-to-all-done.2 = bf16[16,40,128]{2,1,0:T(8,128)(2,1)S(1)} async-done(((bf16[16,40,128]{2,1,0:T(8,128)(2,1)}), bf16[16,40,128]{2,1,0:T(8,128)(2,1)S(1)}, u32[]{:S(2)}, u32[]{:S(2)}) %all-to-all-start.2) | async-done | bytes 163872 | tf_op jit(solution)/shard_map/all_to_all | solution.py:31
  139.7 19.8 %all_to_all.36 = bf16[16,32,128]{2,1,0:T(8,128)(2,1)S(1)} all-to-all(bf16[16,32,128]{2,1,0:T(8,128)(2,1)S(1)} %copy.147), channel_id=1, replica_groups=mesh['dp'=4,'ctx'=16,'mp'=8] {'ctx'}, dimensions={0} | all-to-all | bytes 262144 | tf_op jit(solution)/shard_map/all_to_all | solution.py:45
  159.5 10.9 %all-gather.5.cloned.1.call-done = bf16[1024,512]{1,0:T(8,128)(2,1)} async-done(((bf16[64,512]{1,0:T(8,128)(2,1)}), bf16[1024,512]{1,0:T(8,128)(2,1)}) %all-gather.5.cloned.1.call-update) | async-done | bytes 1048592 | tf_op jit(solution)/shard_map/all_gather | solution.py:106
  170.4 2.0 convolution_convert_fusion
  172.4 11.4 %all_to_all.37 = bf16[4,136,512]{2,1,0:T(8,128)(2,1)S(1)} all-to-all(bf16[4,136,512]{2,1,0:T(8,128)(2,1)S(1)} %convolution_convert_fusion), channel_id=1, replica_groups=mesh['dp'=4,'ctx'=16,'mp'=8] {'dp'}, dimensions={0} | all-to-all | bytes 1114112 | tf_op jit(solution)/shard_map/all_to_all | solution.py:116
  185.1 7.4 %all-to-all-start.5 = ((bf16[16,40,128]{2,1,0:T(8,128)(2,1)}), bf16[16,40,128]{2,1,0:T(8,128)(2,1)S(1)}, u32[]{:S(2)}, u32[]{:S(2)}) async-start(bf16[16,40,128]{2,1,0:T(8,128)(2,1)} %pad_maximum_fusion.3), calls=%async_computation.5 | async-start | bytes 327680 | tf_op jit(solution)/shard_map/all_to_all | solution.py:31
  193.3 12.5 %all-to-all-done.5 = bf16[16,40,128]{2,1,0:T(8,128)(2,1)S(1)} async-done(((bf16[16,40,128]{2,1,0:T(8,128)(2,1)}), bf16[16,40,128]{2,1,0:T(8,128)(2,1)S(1)}, u32[]{:S(2)}, u32[]{:S(2)}) %all-to-all-start.5) | async-done | bytes 163872 | tf_op jit(solution)/shard_map/all_to_all | solution.py:31
  208.4 4.5 %all-to-all-start.6 = ((bf16[16,32,128]{2,1,0:T(8,128)(2,1)}), bf16[16,32,128]{2,1,0:T(8,128)(2,1)S(1)}, u32[]{:S(2)}, u32[]{:S(2)}) async-start(bf16[16,32,128]{2,1,0:T(8,128)(2,1)} %copy.157), calls=%async_computation.6 | async-start | bytes 262144 | tf_op jit(solution)/shard_map/all_to_all | solution.py:45
  214.0 11.9 %all-to-all-done.6 = bf16[16,32,128]{2,1,0:T(8,128)(2,1)S(1)} async-done(((bf16[16,32,128]{2,1,0:T(8,128)(2,1)}), bf16[16,32,128]{2,1,0:T(8,128)(2,1)S(1)}, u32[]{:S(2)}, u32[]{:S(2)}) %all-to-all-start.6) | async-done | bytes 131104 | tf_op jit(solution)/shard_map/all_to_all | solution.py:45
  (103 shorter events, 16.8 us)
Async XLA Ops:
  7.2 80.4 %all-gather.3.cloned.1.call-start = ((), (), s32[]{:S(2)}) async-start(), calls=%async_computation.7 | async-start | bytes 1671168 | tf_op jit(solution)/shard_map/all_gather | solution.py:102
  62.4 3.8 %collective-permute-start = (bf16[8,4096]{1,0:T(8,128)(2,1)S(1)}, bf16[8,4096]{1,0:T(8,128)(2,1)S(1)}, u32[]{:S(2)}, u32[]{:S(2)}) collective-permute-start(bf16[8,4096]{1,0:T(8,128)(2,1)S(1)} %slice.282), channel_id=1, source_target_pairs={{0,8},{8,16},{16,24},{24,32},{32,40},{40,48},{48,56},{56,64},{64,7... | collective-permute-start | bytes 196616 | tf_op jit(solution)/shard_map/ppermute | solution.py:18
  81.5 15.2 %copy-start.5 = (f32[16]{0:T(128)S(1)}, f32[16]{0:T(128)}, u32[]{:S(2)}) copy-start(f32[16]{0:T(128)} %param.21) | copy-start | bytes 196
  81.5 15.2 %copy-start.3 = (f32[5,128]{1,0:T(8,128)S(1)}, f32[5,128]{1,0:T(8,128)}, u32[]{:S(2)}) copy-start(f32[5,128]{1,0:T(8,128)} %param.19) | copy-start | bytes 7684
  81.5 15.3 %copy-start = (f32[5,1024]{1,0:T(8,128)S(1)}, f32[5,1024]{1,0:T(8,128)}, u32[]{:S(2)}) copy-start(f32[5,1024]{1,0:T(8,128)} %param.18) | copy-start | bytes 61444
  90.9 18.5 %copy-start.2 = (f32[16]{0:T(128)S(1)}, f32[16]{0:T(128)}, u32[]{:S(2)}) copy-start(f32[16]{0:T(128)} %param.20) | copy-start | bytes 196
  90.9 12.7 %all-to-all-start.1 = ((bf16[4,136,656]{2,1,0:T(8,128)(2,1)}), bf16[4,136,656]{2,1,0:T(8,128)(2,1)S(1)}, u32[]{:S(2)}, u32[]{:S(2)}) async-start(bf16[4,136,656]{2,1,0:T(8,128)(2,1)} %fusion.6), calls=%async_computation.1 | async-start | bytes 1671168 | tf_op jit(solution)/shard_map/all_to_all | solution.py:116
  95.9 74.5 %all-gather.5.cloned.1.call-start = ((), (), s32[]{:S(2)}) async-start(), calls=%async_computation.8 | async-start | bytes 1114112 | tf_op jit(solution)/shard_map/all_gather | solution.py:106
  103.8 6.6 %collective-permute-start.1 = (bf16[128,128]{1,0:T(8,128)(2,1)S(1)}, bf16[128,128]{1,0:T(8,128)(2,1)S(1)}, u32[]{:S(2)}, u32[]{:S(2)}) collective-permute-start(bf16[128,128]{1,0:T(8,128)(2,1)S(1)} %multiply_convert_fusion.8), channel_id=1, source_target_pairs={{0,0},{4,1},{1,2},{5,3},{2,4},{6,5},{3,6},{7,7},{8,8},{12,9},{9,10... | collective-permute-start | bytes 98312 | tf_op jit(solution)/shard_map/ppermute | solution.py:146
  104.5 8.1 %collective-permute-start.2 = (bf16[128,128]{1,0:T(8,128)(2,1)S(1)}, bf16[128,128]{1,0:T(8,128)(2,1)S(1)}, u32[]{:S(2)}, u32[]{:S(2)}) collective-permute-start(bf16[128,128]{1,0:T(8,128)(2,1)S(1)} %multiply_convert_fusion.8), channel_id=1, source_target_pairs={{4,0},{0,1},{5,2},{1,3},{6,4},{2,5},{7,6},{3,7},{12,8},{8,9},{13,1... | collective-permute-start | bytes 98312 | tf_op jit(solution)/shard_map/ppermute | solution.py:147
  113.5 24.3 %all-to-all-start.2 = ((bf16[16,40,128]{2,1,0:T(8,128)(2,1)}), bf16[16,40,128]{2,1,0:T(8,128)(2,1)S(1)}, u32[]{:S(2)}, u32[]{:S(2)}) async-start(bf16[16,40,128]{2,1,0:T(8,128)(2,1)} %pad_maximum_fusion.2), calls=%async_computation.2 | async-start | bytes 327680 | tf_op jit(solution)/shard_map/all_to_all | solution.py:31
  172.4 20.1 %copy-start.1 = (f32[1024]{0:T(1024)S(1)}, f32[1024]{0:T(1024)}, u32[]{:S(2)}) copy-start(f32[1024]{0:T(1024)} %param.23) | copy-start | bytes 12292
  185.1 20.7 %all-to-all-start.5 = ((bf16[16,40,128]{2,1,0:T(8,128)(2,1)}), bf16[16,40,128]{2,1,0:T(8,128)(2,1)S(1)}, u32[]{:S(2)}, u32[]{:S(2)}) async-start(bf16[16,40,128]{2,1,0:T(8,128)(2,1)} %pad_maximum_fusion.3), calls=%async_computation.5 | async-start | bytes 327680 | tf_op jit(solution)/shard_map/all_to_all | solution.py:31
  208.4 17.6 %all-to-all-start.6 = ((bf16[16,32,128]{2,1,0:T(8,128)(2,1)}), bf16[16,32,128]{2,1,0:T(8,128)(2,1)S(1)}, u32[]{:S(2)}, u32[]{:S(2)}) async-start(bf16[16,32,128]{2,1,0:T(8,128)(2,1)} %copy.157), calls=%async_computation.6 | async-start | bytes 262144 | tf_op jit(solution)/shard_map/all_to_all | solution.py:45
  213.2 12.7 %copy-start.4 = (f32[16]{0:T(128)S(1)}, f32[16]{0:T(128)}, u32[]{:S(2)}) copy-start(f32[16]{0:T(128)} %param.22) | copy-start | bytes 196
Sparse Core Ops, SparseCore 0:
  11.0 76.5 all-gather.2
  98.8 71.5 all-gather.4

commit v8 on v6

--- a/solution.py
+++ b/solution.py
@@ -10,39 +10,64 @@
 
 
 HIGH = lax.Precision.HIGHEST
-
-
-def passed_along(value, axis, steps):
-    count = lax.axis_size(axis)
+CTX = ("ch", "cl")
+
+
+def passed_along(value, axis, steps, count):
     first, last = (max(0, -steps), min(count, count - steps))
     return lax.ppermute(value, axis, [(source, source + steps) for source in range(first, last)])
 
 
-def entering(decay, contrib, axis):
-    count, place = (lax.axis_size(axis), lax.axis_index(axis))
+def decay_products(row_decay, targets):
+    count = row_decay.shape[0]
+    target = lax.broadcasted_iota(jnp.int32, (targets, count, count), 0)
+    source = lax.broadcasted_iota(jnp.int32, (targets, count, count), 1)
+    between = lax.broadcasted_iota(jnp.int32, (targets, count, count), 2)
+    inside = jnp.logical_and(between > source, between < target)
+    factors = jnp.where(inside[..., None], row_decay[None, None], 1.0)
+    products = jnp.prod(factors, 2)
+    return jnp.where((source[:, :, 0] < target[:, :, 0])[..., None], products, 0.0)
+
+
+def entering(decay, contrib):
+    quads, quad = (lax.axis_index("ch"), lax.axis_size("cl"))
+    place = lax.axis_index("cl")
     lanes = contrib.shape[-1]
     head_rows = contrib.shape[-2]
     heads = decay.size
-    chunk = contrib.size // lanes // count
-    pieces = contrib.reshape(count, chunk, lanes)
-    tail = jnp.zeros((count, 8, lanes), jnp.float32)
-    tail = tail.at[:, 0, :heads].set(jnp.broadcast_to(decay.reshape(1, heads), (count, heads)))
+    chunk = contrib.size // lanes // quad
+    pieces = contrib.reshape(quad, chunk, lanes)
+    tail = jnp.zeros((quad, 8, lanes), jnp.float32)
+    tail = tail.at[:, 0, :heads].set(jnp.broadcast_to(decay.reshape(1, heads), (quad, heads)))
     outgoing = jnp.concatenate([pieces, tail], 1).astype(jnp.bfloat16)
-    incoming = lax.all_to_all(outgoing, axis, 0, 0).astype(jnp.float32)
+    incoming = lax.all_to_all(outgoing, "cl", 0, 0).astype(jnp.float32)
     states = incoming[:, :chunk]
     decays = incoming[:, chunk, :heads]
     row_head = (place * chunk + lax.broadcasted_iota(jnp.int32, (chunk, heads), 0)) // head_rows
     pick = row_head == lax.broadcasted_iota(jnp.int32, (chunk, heads), 1)
     row_decay = jnp.sum(jnp.where(pick[None], decays[:, None, :], 0.0), -1)
-    target = lax.broadcasted_iota(jnp.int32, (count, count, count), 0)
-    source = lax.broadcasted_iota(jnp.int32, (count, count, count), 1)
-    between = lax.broadcasted_iota(jnp.int32, (count, count, count), 2)
-    inside = jnp.logical_and(between > source, between < target)
-    factors = jnp.where(inside[..., None], row_decay[None, None], 1.0)
-    weights = jnp.prod(factors, 2)
-    weights = jnp.where((source[:, :, 0] < target[:, :, 0])[..., None], weights, 0.0)
-    carried = jnp.einsum("kjr,jrl->krl", weights, states, precision=HIGH)
-    returned = lax.all_to_all(carried.astype(jnp.bfloat16), axis, 0, 0)
+    local = jnp.einsum(
+        "kjr,jrl->krl", decay_products(row_decay, quad + 1), states, precision=HIGH
+    )
+    step = lax.broadcasted_iota(jnp.int32, (quad + 1, quad, chunk), 0)
+    index = lax.broadcasted_iota(jnp.int32, (quad + 1, quad, chunk), 1)
+    entry = jnp.prod(jnp.where(index < step, row_decay[None], 1.0), 1)
+    pad_rows = 8 - (chunk // lanes) % 8
+    summary = jnp.concatenate(
+        [local[quad], entry[quad].reshape(chunk // lanes, lanes), jnp.zeros((pad_rows, lanes))]
+    )
+    count_hi = lax.axis_size("ch")
+    shared = lax.all_to_all(jnp.broadcast_to(summary, (count_hi,) + summary.shape), "ch", 0, 0)
+    totals = shared[:, :chunk]
+    quad_decay = shared[:, chunk : chunk + chunk // lanes].reshape(count_hi, chunk)
+    earlier = lax.broadcasted_iota(jnp.int32, (count_hi, count_hi, chunk), 0)
+    middle = lax.broadcasted_iota(jnp.int32, (count_hi, count_hi, chunk), 1)
+    spans = jnp.logical_and(middle > earlier, middle < quads)
+    across = jnp.prod(jnp.where(spans, quad_decay[None], 1.0), 1)
+    across = jnp.where(earlier[:, 0] < quads, across, 0.0)
+    entering_state = jnp.einsum("qr,qrl->rl", across, totals, precision=HIGH)
+    carried = local[:quad] + entry[:quad, :, None] * entering_state[None]
+    returned = lax.all_to_all(carried.astype(jnp.bfloat16), "cl", 0, 0)
     return returned.astype(jnp.float32).reshape(contrib.shape)
 
 
@@ -93,16 +118,17 @@
             jnp.sum(square * square, 0),
         ]
     )
-    row_count = float(tok_rows * lax.axis_size("dp") * lax.axis_size("ctx"))
-    totals = lax.psum(lax.psum(powers, "ctx"), "dp")
+    ctx_count = lax.axis_size("ch") * lax.axis_size("cl")
+    row_count = float(tok_rows * lax.axis_size("dp") * ctx_count)
+    totals = lax.psum(lax.psum(powers, CTX), "dp")
     totals, rotated = lax.optimization_barrier((totals, rotated))
     kurtosis = kurtosis_from(totals, row_count)
     local_panel = jnp.concatenate([x_weight, bc_weight, dt_weight], 1)
-    panel = lax.all_gather(local_panel, "ctx", axis=0, tiled=True)
+    panel = lax.all_gather(local_panel, CTX, axis=0, tiled=True)
     seqs = lax.axis_size("dp")
     share = model_width // seqs
     rim = 8
-    earlier = passed_along(rotated[tok_rows - rim :], "ctx", 1)
+    earlier = passed_along(rotated[tok_rows - rim :], CTX, 1, ctx_count)
     extended = jnp.concatenate([earlier, rotated], 0)
     outgoing = extended.reshape(tok_rows + rim, seqs, share).transpose(1, 0, 2)
     incoming = lax.all_to_all(outgoing, "dp", 0, 0)
@@ -180,7 +206,7 @@
         * x_heads
     ).astype(jnp.bfloat16)
     contrib = jnp.einsum("sghp,sgn->ghpn", update, write_here, preferred_element_type=jnp.float32)
-    carried = entering(jnp.exp(-block_end).reshape(groups_here, heads_local), contrib, "ctx")
+    carried = entering(jnp.exp(-block_end).reshape(groups_here, heads_local), contrib)
     from_before = jnp.exp(-cumulative).reshape(tok_rows, groups_here, heads_local)[
         ..., None
     ] * jnp.einsum("tgn,ghpn->tghp", read_here.astype(jnp.float32), carried, precision=HIGH)
@@ -199,14 +225,20 @@
 
 
 def solution(mesh):
+    grid = mesh.devices
+    quad = 4 if grid.shape[1] % 4 == 0 else 1
+    split = jax.sharding.Mesh(
+        grid.reshape(grid.shape[0], grid.shape[1] // quad, quad, grid.shape[2]),
+        ("dp", "ch", "cl", "mp"),
+    )
     return jax.shard_map(
         shards,
-        mesh=mesh,
+        mesh=split,
         in_specs=(
-            P("dp", "ctx", None),
-            P(("dp", "ctx"), "mp"),
-            P(("dp", "ctx"), "mp"),
-            P(("dp", "ctx"), "mp"),
+            P("dp", CTX, None),
+            P(("dp",) + CTX, "mp"),
+            P(("dp",) + CTX, "mp"),
+            P(("dp",) + CTX, "mp"),
             P(None, "mp"),
             P(None, "mp"),
             P("mp"),
@@ -214,6 +246,6 @@
             P("mp"),
             P("mp"),
         ),
-        out_specs=(P("dp", "ctx", "mp"), P("mp")),
+        out_specs=(P("dp", CTX, "mp"), P("mp")),
         check_vma=False,
     )

time: 183 us -> 195 us (1.066)
  waiting for transfers between devices: 62.7 us -> 69.7 us
  matrix products: 12.1 us -> 14.8 us
    all_to_all x2 -> x3, waiting for transfers between devices: 35.9 us -> 42.6 us  [the longest x1 29.1 us: entering(): lax.all_to_all(jnp.broadcast_to(summary, (count_hi,) + summary.shape), 'c...]
    dot_general x1 -> x2, matrix products: 0.54 us -> 3.25 us  [the longest x1 2.05 us: entering(): entering_state = jnp.einsum('qr,qrl->rl', across, totals, precision=HIGH)]
    all_to_all x2 -> x3, starting transfers between devices: 13 us -> 14.5 us  [the longest x1 7.21 us: entering(): lax.all_to_all(jnp.broadcast_to(summary, (count_hi,) + summary.shape), 'c...]
  transfers between devices with their start and end apart: 9 -> 10, of which waited for: 7 -> 8; matrix products, arithmetic and copies ran while one was open for 9% -> 8% of each run, Pallas kernels for 0% -> 0%
where the time goes in v8:
time: 195 us; the launch traced here: 194 us
  waiting for transfers between devices  69.7 us (36%)
  blocking collectives  44.6 us (23%)
  starting transfers between devices  36.4 us (19%)
  matrix products  14.8 us (8%)
  between operations  14.5 us (7%)
  local copies, waits for them, and re-layouts  8.18 us (4%)
  other arithmetic  5.66 us (3%)
    psum x2, blocking collectives, shards(): totals = lax.psum(lax.psum(powers, CTX), 'dp')  44.6 us
    all_to_all x1, waiting for transfers between devices, entering(): lax.all_to_all(jnp.broadcast_to(summary, (count_hi,) + summary.shape), 'c...  29.1 us
    all_to_all x1, waiting for transfers between devices, shards(): incoming = lax.all_to_all(outgoing, 'dp', 0, 0)  9.11 us
    all_to_all x1, waiting for transfers between devices, entering(): incoming = lax.all_to_all(outgoing, 'cl', 0, 0).astype(jnp.float32)  8.41 us
    all_gather x1, waiting for transfers between devices, shards(): panel = lax.all_gather(local_panel, CTX, axis=0, tiled=True)  7.81 us
    all_to_all x1, starting transfers between devices, shards(): incoming = lax.all_to_all(outgoing, 'dp', 0, 0)  7.28 us
    all_to_all x1, starting transfers between devices, entering(): lax.all_to_all(jnp.broadcast_to(summary, (count_hi,) + summary.shape), 'c...  7.21 us
    all_to_all x1, waiting for transfers between devices, shards(): x_back = lax.all_to_all(x_partials.astype(jnp.bfloat16), 'dp', 0, 0)  5.79 us
  transfers between devices with their start and end apart: 10, of which 8 were waited for; matrix products, arithmetic and copies ran while one was open for 8% of the time, Pallas kernels for 0%

profile of v8, /device:TPU:6, one launch (start us, length us, event | category | flops | bytes accessed | tf_op | source)
XLA Modules:
  0.0 193.8 jit_solution(9356052190049795253)
XLA Ops:
  8.0 1.6 pad_maximum_fusion.2
  9.6 1.6 copy.119
  12.1 3.3 %multiply_convert_fusion = bf16[128,64,64]{0,2,1:T(8,128)(2,1)S(1)} fusion(f32[128,64,64]{0,1,2:T(8,128)S(1)} %convolution_bitcast_fusion), kind=kOutput, calls=%fused_computation.4 | convolution fusion | flops 403791872 | bytes 3145728 | tf_op jit(solution)/shard_map/tcb,bd->tcd/dot_general | solution.py:106
  15.8 37.0 %psum.14 = f32[4,512]{1,0:T(4,128)S(1)} all-reduce(f32[4,512]{1,0:T(4,128)S(1)} %pad_maximum_fusion.3), channel_id=1, replica_groups=mesh['dp'=4,'ch'=4,'cl'=4,'mp'=8] {'ch','cl'}, use_global_device_ids=true, to_apply=%region_4.0 | all-reduce | flops 2048 | bytes 16384 | tf_op jit(solution)/shard_map/psum | solution.py:123
  52.8 7.6 %psum.15 = f32[4,512]{1,0:T(4,128)S(1)} all-reduce(f32[4,512]{1,0:T(4,128)S(1)} %psum.14), channel_id=1, replica_groups=mesh['dp'=4,'ch'=4,'cl'=4,'mp'=8] {'dp'}, use_global_device_ids=true, to_apply=%region_5.0 | all-reduce | flops 2048 | bytes 16384 | tf_op jit(solution)/shard_map/psum | solution.py:123
  61.0 1.7 collective-permute-start
  62.7 2.1 %collective-permute-done = bf16[8,4096]{1,0:T(8,128)(2,1)S(1)} collective-permute-done((bf16[8,4096]{1,0:T(8,128)(2,1)S(1)}, bf16[8,4096]{1,0:T(8,128)(2,1)S(1)}, u32[]{:S(2)}, u32[]{:S(2)}) %collective-permute-start) | collective-permute-done | bytes 65568 | tf_op jit(solution)/shard_map/ppermute | solution.py:18
  66.0 7.3 %all-to-all-start = ((bf16[4,136,1024]{2,1,0:T(8,128)(2,1)}), bf16[4,136,1024]{2,1,0:T(8,128)(2,1)S(1)}, u32[]{:S(2)}, u32[]{:S(2)}) async-start(bf16[4,136,1024]{2,1,0:T(8,128)(2,1)} %bitcast.108), calls=%async_computation | async-start | bytes 2228224 | tf_op jit(solution)/shard_map/all_to_all | solution.py:134
  73.4 9.1 %all-to-all-done = bf16[4,136,1024]{2,1,0:T(8,128)(2,1)S(1)} async-done(((bf16[4,136,1024]{2,1,0:T(8,128)(2,1)}), bf16[4,136,1024]{2,1,0:T(8,128)(2,1)S(1)}, u32[]{:S(2)}, u32[]{:S(2)}) %all-to-all-start) | async-done | bytes 1114144 | tf_op jit(solution)/shard_map/all_to_all | solution.py:134
  82.5 7.8 %all-gather.2.cloned.1.call-done = bf16[1024,1168]{1,0:T(8,128)(2,1)} async-done(((bf16[64,1168]{1,0:T(8,128)(2,1)}), bf16[1024,1168]{1,0:T(8,128)(2,1)}) %all-gather.2.cloned.1.call-update) | async-done | bytes 2392080 | tf_op jit(solution)/shard_map/all_gather | solution.py:127
  90.3 2.2 %convolution_convert_fusion = bf16[4,136,144]{2,1,0:T(8,128)(2,1)} fusion(bf16[4,136,1024]{2,1,0:T(8,128)(2,1)S(1)} %all-to-all-done, bf16[1024,1168]{1,0:T(8,128)(2,1)} %all-gather.2.cloned.1.call-done), kind=kOutput, calls=%fused_computation.13 | convolution fusion | flops 160510464 | bytes 1795072 | tf_op jit(solution)/shard_map/kti,io->kto/dot_general | solution.py:137
  92.5 4.8 %all-to-all-start.2 = ((bf16[4,136,144]{2,1,0:T(8,128)(2,1)}), bf16[4,136,144]{2,1,0:T(8,128)(2,1)S(1)}, u32[]{:S(2)}, u32[]{:S(2)}) async-start(bf16[4,136,144]{2,1,0:T(8,128)(2,1)} %convolution_convert_fusion), calls=%async_computation.2 | async-start | bytes 557056 | tf_op jit(solution)/shard_map/all_to_all | solution.py:140
  97.3 3.9 %fusion.5 = bf16[4,136,1024]{2,1,0:T(8,128)(2,1)} fusion(bf16[4,136,1024]{2,1,0:T(8,128)(2,1)S(1)} %all-to-all-done, bf16[1024,1168]{1,0:T(8,128)(2,1)} %all-gather.2.cloned.1.call-done), kind=kOutput, calls=%fused_computation.6 | convolution fusion | flops 1141407744 | bytes 4325376 | tf_op jit(solution)/shard_map/kti,io->kto/dot_general | solution.py:141
  101.2 2.2 %all-to-all-done.2 = bf16[4,136,144]{2,1,0:T(8,128)(2,1)S(1)} async-done(((bf16[4,136,144]{2,1,0:T(8,128)(2,1)}), bf16[4,136,144]{2,1,0:T(8,128)(2,1)S(1)}, u32[]{:S(2)}, u32[]{:S(2)}) %all-to-all-start.2) | async-done | bytes 156704 | tf_op jit(solution)/shard_map/all_to_all | solution.py:140
  103.5 5.6 %all-to-all-start.1 = ((bf16[4,136,1024]{2,1,0:T(8,128)(2,1)}), bf16[4,136,1024]{2,1,0:T(8,128)(2,1)S(1)}, u32[]{:S(2)}, u32[]{:S(2)}) async-start(bf16[4,136,1024]{2,1,0:T(8,128)(2,1)} %fusion.5), calls=%async_computation.1 | async-start | bytes 2228224 | tf_op jit(solution)/shard_map/all_to_all | solution.py:144
  109.2 1.9 collective-permute-start.1
  112.4 5.8 %all-to-all-done.1 = bf16[4,136,1024]{2,1,0:T(8,128)(2,1)S(1)} async-done(((bf16[4,136,1024]{2,1,0:T(8,128)(2,1)}), bf16[4,136,1024]{2,1,0:T(8,128)(2,1)S(1)}, u32[]{:S(2)}, u32[]{:S(2)}) %all-to-all-start.1) | async-done | bytes 1114144 | tf_op jit(solution)/shard_map/all_to_all | solution.py:144
  120.0 3.5 %all-to-all-start.3 = ((bf16[4,264,128]{2,1,0:T(8,128)(2,1)}), bf16[4,264,128]{2,1,0:T(8,128)(2,1)S(1)}, u32[]{:S(2)}, u32[]{:S(2)}) async-start(bf16[4,264,128]{2,1,0:T(8,128)(2,1)} %pad_maximum_fusion.1), calls=%async_computation.3 | async-start | bytes 540672 | tf_op jit(solution)/shard_map/all_to_all | solution.py:43
  123.8 8.4 %all-to-all-done.3 = bf16[4,264,128]{2,1,0:T(8,128)(2,1)S(1)} async-done(((bf16[4,264,128]{2,1,0:T(8,128)(2,1)}), bf16[4,264,128]{2,1,0:T(8,128)(2,1)S(1)}, u32[]{:S(2)}, u32[]{:S(2)}) %all-to-all-start.3) | async-done | bytes 270368 | tf_op jit(solution)/shard_map/all_to_all | solution.py:43
  135.1 7.2 %all-to-all-start.4 = ((f32[4,264,128]{2,1,0:T(8,128)}), f32[4,264,128]{2,1,0:T(8,128)S(1)}, u32[]{:S(2)}, u32[]{:S(2)}) async-start(f32[4,264,128]{2,1,0:T(8,128)} %broadcast_in_dim.140), calls=%async_computation.4 | async-start | bytes 1081344 | tf_op jit(solution)/shard_map/all_to_all | solution.py:60
  142.5 29.1 %all-to-all-done.4 = f32[4,264,128]{2,1,0:T(8,128)S(1)} async-done(((f32[4,264,128]{2,1,0:T(8,128)}), f32[4,264,128]{2,1,0:T(8,128)S(1)}, u32[]{:S(2)}, u32[]{:S(2)}) %all-to-all-start.4) | async-done | bytes 540704 | tf_op jit(solution)/shard_map/all_to_all | solution.py:60
  171.9 2.0 %fusion.16 = f32[256,1,128]{2,1,0:T(1,128)S(1)} fusion(f32[4,256,1]{0,2,1:T(1,128)S(1)} %copy.142, f32[4,256,128]{2,1,0:T(8,128)S(1)} %slice.214), kind=kOutput, calls=%fused_computation.31 | convolution fusion | flops 1572864 | bytes 659456 | tf_op jit(solution)/shard_map/qr,qrl->rl/dot_general | solution.py:68
  175.1 3.8 %all-to-all-start.5 = ((bf16[4,256,128]{2,1,0:T(8,128)(2,1)}), bf16[4,256,128]{2,1,0:T(8,128)(2,1)S(1)}, u32[]{:S(2)}, u32[]{:S(2)}) async-start(bf16[4,256,128]{2,1,0:T(8,128)(2,1)} %copy.138), calls=%async_computation.5 | async-start | bytes 524288 | tf_op jit(solution)/shard_map/all_to_all | solution.py:70
  180.5 5.1 %all-to-all-done.5 = bf16[4,256,128]{2,1,0:T(8,128)(2,1)S(1)} async-done(((bf16[4,256,128]{2,1,0:T(8,128)(2,1)}), bf16[4,256,128]{2,1,0:T(8,128)(2,1)S(1)}, u32[]{:S(2)}, u32[]{:S(2)}) %all-to-all-start.5) | async-done | bytes 262176 | tf_op jit(solution)/shard_map/all_to_all | solution.py:70
  (92 shorter events, 14.6 us)
Async XLA Ops:
  7.2 83.1 %all-gather.2.cloned.1.call-start = ((), (), s32[]{:S(2)}) async-start(), calls=%async_computation.6 | async-start | bytes 2785280 | tf_op jit(solution)/shard_map/all_gather | solution.py:127
  61.0 3.9 %collective-permute-start = (bf16[8,4096]{1,0:T(8,128)(2,1)S(1)}, bf16[8,4096]{1,0:T(8,128)(2,1)S(1)}, u32[]{:S(2)}, u32[]{:S(2)}) collective-permute-start(bf16[8,4096]{1,0:T(8,128)(2,1)S(1)} %slice.194), channel_id=1, source_target_pairs={{0,8},{8,16},{16,24},{24,32},{32,40},{40,48},{48,56},{56,64},{64,7... | collective-permute-start | bytes 196616 | tf_op jit(solution)/shard_map/ppermute | solution.py:18
  64.9 8.4 %copy-start.5 = (f32[16]{0:T(128)S(1)}, f32[16]{0:T(128)}, u32[]{:S(2)}) copy-start(f32[16]{0:T(128)} %param.19) | copy-start | bytes 196
  64.9 8.4 %copy-start.3 = (f32[5,128]{1,0:T(8,128)S(1)}, f32[5,128]{1,0:T(8,128)}, u32[]{:S(2)}) copy-start(f32[5,128]{1,0:T(8,128)} %param.17) | copy-start | bytes 7684
  64.9 8.4 %copy-start = (f32[5,1024]{1,0:T(8,128)S(1)}, f32[5,1024]{1,0:T(8,128)}, u32[]{:S(2)}) copy-start(f32[5,1024]{1,0:T(8,128)} %param.16) | copy-start | bytes 61444
  66.0 16.5 %all-to-all-start = ((bf16[4,136,1024]{2,1,0:T(8,128)(2,1)}), bf16[4,136,1024]{2,1,0:T(8,128)(2,1)S(1)}, u32[]{:S(2)}, u32[]{:S(2)}) async-start(bf16[4,136,1024]{2,1,0:T(8,128)(2,1)} %bitcast.108), calls=%async_computation | async-start | bytes 2228224 | tf_op jit(solution)/shard_map/all_to_all | solution.py:134
  92.5 10.9 %all-to-all-start.2 = ((bf16[4,136,144]{2,1,0:T(8,128)(2,1)}), bf16[4,136,144]{2,1,0:T(8,128)(2,1)S(1)}, u32[]{:S(2)}, u32[]{:S(2)}) async-start(bf16[4,136,144]{2,1,0:T(8,128)(2,1)} %convolution_convert_fusion), calls=%async_computation.2 | async-start | bytes 557056 | tf_op jit(solution)/shard_map/all_to_all | solution.py:140
  101.2 10.6 %copy-start.2 = (f32[16]{0:T(128)S(1)}, f32[16]{0:T(128)}, u32[]{:S(2)}) copy-start(f32[16]{0:T(128)} %param.18) | copy-start | bytes 196
  103.5 14.7 %all-to-all-start.1 = ((bf16[4,136,1024]{2,1,0:T(8,128)(2,1)}), bf16[4,136,1024]{2,1,0:T(8,128)(2,1)S(1)}, u32[]{:S(2)}, u32[]{:S(2)}) async-start(bf16[4,136,1024]{2,1,0:T(8,128)(2,1)} %fusion.5), calls=%async_computation.1 | async-start | bytes 2228224 | tf_op jit(solution)/shard_map/all_to_all | solution.py:144
  109.2 9.9 %collective-permute-start.1 = (bf16[128,128]{1,0:T(8,128)(2,1)S(1)}, bf16[128,128]{1,0:T(8,128)(2,1)S(1)}, u32[]{:S(2)}, u32[]{:S(2)}) collective-permute-start(bf16[128,128]{1,0:T(8,128)(2,1)S(1)} %multiply_convert_fusion.6), channel_id=1, source_target_pairs={{4,0},{0,1},{5,2},{1,3},{6,4},{2,5},{7,6},{3,7},{12,8},{8,9},{13,1... | collective-permute-start | bytes 98312 | tf_op jit(solution)/shard_map/ppermute | solution.py:173
  111.1 8.0 %collective-permute-start.2 = (bf16[128,128]{1,0:T(8,128)(2,1)S(1)}, bf16[128,128]{1,0:T(8,128)(2,1)S(1)}, u32[]{:S(2)}, u32[]{:S(2)}) collective-permute-start(bf16[128,128]{1,0:T(8,128)(2,1)S(1)} %multiply_convert_fusion.6), channel_id=1, source_target_pairs={{0,0},{4,1},{1,2},{5,3},{2,4},{6,5},{3,6},{7,7},{8,8},{12,9},{9,10... | collective-permute-start | bytes 98312 | tf_op jit(solution)/shard_map/ppermute | solution.py:172
  120.0 12.2 %all-to-all-start.3 = ((bf16[4,264,128]{2,1,0:T(8,128)(2,1)}), bf16[4,264,128]{2,1,0:T(8,128)(2,1)S(1)}, u32[]{:S(2)}, u32[]{:S(2)}) async-start(bf16[4,264,128]{2,1,0:T(8,128)(2,1)} %pad_maximum_fusion.1), calls=%async_computation.3 | async-start | bytes 540672 | tf_op jit(solution)/shard_map/all_to_all | solution.py:43
  135.1 36.5 %all-to-all-start.4 = ((f32[4,264,128]{2,1,0:T(8,128)}), f32[4,264,128]{2,1,0:T(8,128)S(1)}, u32[]{:S(2)}, u32[]{:S(2)}) async-start(f32[4,264,128]{2,1,0:T(8,128)} %broadcast_in_dim.140), calls=%async_computation.4 | async-start | bytes 1081344 | tf_op jit(solution)/shard_map/all_to_all | solution.py:60
  171.9 7.5 %copy-start.1 = (f32[1024]{0:T(1024)S(1)}, f32[1024]{0:T(1024)}, u32[]{:S(2)}) copy-start(f32[1024]{0:T(1024)} %param.21) | copy-start | bytes 12292
  175.1 10.5 %copy-start.4 = (f32[16]{0:T(128)S(1)}, f32[16]{0:T(128)}, u32[]{:S(2)}) copy-start(f32[16]{0:T(128)} %param.20) | copy-start | bytes 196
  175.1 10.5 %all-to-all-start.5 = ((bf16[4,256,128]{2,1,0:T(8,128)(2,1)}), bf16[4,256,128]{2,1,0:T(8,128)(2,1)S(1)}, u32[]{:S(2)}, u32[]{:S(2)}) async-start(bf16[4,256,128]{2,1,0:T(8,128)(2,1)} %copy.138), calls=%async_computation.5 | async-start | bytes 524288 | tf_op jit(solution)/shard_map/all_to_all | solution.py:70
Sparse Core Ops, SparseCore 0:
  10.7 79.6 all-gather.1

commit v9 on v8

--- a/solution.py
+++ b/solution.py
@@ -57,7 +57,9 @@
         [local[quad], entry[quad].reshape(chunk // lanes, lanes), jnp.zeros((pad_rows, lanes))]
     )
     count_hi = lax.axis_size("ch")
-    shared = lax.all_to_all(jnp.broadcast_to(summary, (count_hi,) + summary.shape), "ch", 0, 0)
+    shared = lax.all_to_all(
+        jnp.broadcast_to(summary.astype(jnp.bfloat16), (count_hi,) + summary.shape), "ch", 0, 0
+    ).astype(jnp.float32)
     totals = shared[:, :chunk]
     quad_decay = shared[:, chunk : chunk + chunk // lanes].reshape(count_hi, chunk)
     earlier = lax.broadcasted_iota(jnp.int32, (count_hi, count_hi, chunk), 0)

time: 195 us -> 183 us (0.938)
  waiting for transfers between devices: 69.7 us -> 57.9 us
    all_to_all x1, waiting for transfers between devices: 29.1 us -> 17.3 us  [entering(): lax.all_to_all(jnp.broadcast_to(summary.astype(jnp.bfloat16), (count_hi,)...]
  transfers between devices with their start and end apart: 10 -> 10, of which waited for: 8 -> 8; matrix products, arithmetic and copies ran while one was open for 8% -> 9% of each run, Pallas kernels for 0% -> 0%
where the time goes in v9:
time: 183 us; the launch traced here: 181 us
  waiting for transfers between devices  57.9 us (32%)
  blocking collectives  44.6 us (24%)
  starting transfers between devices  36.8 us (20%)
  between operations  14.5 us (8%)
  matrix products  13.8 us (8%)
  local copies, waits for them, and re-layouts  8.1 us (4%)
  other arithmetic  5.67 us (3%)
    psum x2, blocking collectives, shards(): totals = lax.psum(lax.psum(powers, CTX), 'dp')  44.6 us
    all_to_all x1, waiting for transfers between devices, entering(): lax.all_to_all(jnp.broadcast_to(summary.astype(jnp.bfloat16), (count_hi,)...  17.3 us
    all_to_all x1, waiting for transfers between devices, shards(): incoming = lax.all_to_all(outgoing, 'dp', 0, 0)  9.11 us
    all_to_all x1, waiting for transfers between devices, entering(): incoming = lax.all_to_all(outgoing, 'cl', 0, 0).astype(jnp.float32)  8.4 us
    all_gather x1, waiting for transfers between devices, shards(): panel = lax.all_gather(local_panel, CTX, axis=0, tiled=True)  7.81 us
    all_to_all x1, starting transfers between devices, shards(): incoming = lax.all_to_all(outgoing, 'dp', 0, 0)  7.28 us
    all_to_all x1, starting transfers between devices, entering(): lax.all_to_all(jnp.broadcast_to(summary.astype(jnp.bfloat16), (count_hi,)...  7.21 us
    all_to_all x1, waiting for transfers between devices, shards(): x_back = lax.all_to_all(x_partials.astype(jnp.bfloat16), 'dp', 0, 0)  5.79 us
  transfers between devices with their start and end apart: 10, of which 8 were waited for; matrix products, arithmetic and copies ran while one was open for 9% of the time, Pallas kernels for 0%

profile of v9, /device:TPU:6, one launch (start us, length us, event | category | flops | bytes accessed | tf_op | source)
XLA Modules:
  0.0 181.4 jit_solution(13436363650932718093)
XLA Ops:
  8.0 1.6 pad_maximum_fusion.2
  9.6 1.6 copy.135
  12.1 3.3 %multiply_convert_fusion = bf16[128,64,64]{0,2,1:T(8,128)(2,1)S(1)} fusion(f32[128,64,64]{0,1,2:T(8,128)S(1)} %convolution_bitcast_fusion), kind=kOutput, calls=%fused_computation.4 | convolution fusion | flops 403791872 | bytes 3145728 | tf_op jit(solution)/shard_map/tcb,bd->tcd/dot_general | solution.py:108
  15.8 37.0 %psum.14 = f32[4,512]{1,0:T(4,128)S(1)} all-reduce(f32[4,512]{1,0:T(4,128)S(1)} %pad_maximum_fusion.3), channel_id=1, replica_groups=mesh['dp'=4,'ch'=4,'cl'=4,'mp'=8] {'ch','cl'}, use_global_device_ids=true, to_apply=%region_4.0 | all-reduce | flops 2048 | bytes 16384 | tf_op jit(solution)/shard_map/psum | solution.py:125
  52.8 7.6 %psum.15 = f32[4,512]{1,0:T(4,128)S(1)} all-reduce(f32[4,512]{1,0:T(4,128)S(1)} %psum.14), channel_id=1, replica_groups=mesh['dp'=4,'ch'=4,'cl'=4,'mp'=8] {'dp'}, use_global_device_ids=true, to_apply=%region_5.0 | all-reduce | flops 2048 | bytes 16384 | tf_op jit(solution)/shard_map/psum | solution.py:125
  61.0 1.7 collective-permute-start
  62.7 2.1 %collective-permute-done = bf16[8,4096]{1,0:T(8,128)(2,1)S(1)} collective-permute-done((bf16[8,4096]{1,0:T(8,128)(2,1)S(1)}, bf16[8,4096]{1,0:T(8,128)(2,1)S(1)}, u32[]{:S(2)}, u32[]{:S(2)}) %collective-permute-start) | collective-permute-done | bytes 65568 | tf_op jit(solution)/shard_map/ppermute | solution.py:18
  66.0 7.3 %all-to-all-start = ((bf16[4,136,1024]{2,1,0:T(8,128)(2,1)}), bf16[4,136,1024]{2,1,0:T(8,128)(2,1)S(1)}, u32[]{:S(2)}, u32[]{:S(2)}) async-start(bf16[4,136,1024]{2,1,0:T(8,128)(2,1)} %bitcast.109), calls=%async_computation | async-start | bytes 2228224 | tf_op jit(solution)/shard_map/all_to_all | solution.py:136
  73.4 9.1 %all-to-all-done = bf16[4,136,1024]{2,1,0:T(8,128)(2,1)S(1)} async-done(((bf16[4,136,1024]{2,1,0:T(8,128)(2,1)}), bf16[4,136,1024]{2,1,0:T(8,128)(2,1)S(1)}, u32[]{:S(2)}, u32[]{:S(2)}) %all-to-all-start) | async-done | bytes 1114144 | tf_op jit(solution)/shard_map/all_to_all | solution.py:136
  82.5 7.8 %all-gather.2.cloned.1.call-done = bf16[1024,1168]{1,0:T(8,128)(2,1)} async-done(((bf16[64,1168]{1,0:T(8,128)(2,1)}), bf16[1024,1168]{1,0:T(8,128)(2,1)}) %all-gather.2.cloned.1.call-update) | async-done | bytes 2392080 | tf_op jit(solution)/shard_map/all_gather | solution.py:129
  90.3 2.2 %convolution_convert_fusion = bf16[4,136,144]{2,1,0:T(8,128)(2,1)} fusion(bf16[4,136,1024]{2,1,0:T(8,128)(2,1)S(1)} %all-to-all-done, bf16[1024,1168]{1,0:T(8,128)(2,1)} %all-gather.2.cloned.1.call-done), kind=kOutput, calls=%fused_computation.13 | convolution fusion | flops 160510464 | bytes 1795072 | tf_op jit(solution)/shard_map/kti,io->kto/dot_general | solution.py:139
  92.5 4.8 %all-to-all-start.2 = ((bf16[4,136,144]{2,1,0:T(8,128)(2,1)}), bf16[4,136,144]{2,1,0:T(8,128)(2,1)S(1)}, u32[]{:S(2)}, u32[]{:S(2)}) async-start(bf16[4,136,144]{2,1,0:T(8,128)(2,1)} %convolution_convert_fusion), calls=%async_computation.2 | async-start | bytes 557056 | tf_op jit(solution)/shard_map/all_to_all | solution.py:142
  97.3 3.9 %fusion.5 = bf16[4,136,1024]{2,1,0:T(8,128)(2,1)} fusion(bf16[4,136,1024]{2,1,0:T(8,128)(2,1)S(1)} %all-to-all-done, bf16[1024,1168]{1,0:T(8,128)(2,1)} %all-gather.2.cloned.1.call-done), kind=kOutput, calls=%fused_computation.6 | convolution fusion | flops 1141407744 | bytes 4325376 | tf_op jit(solution)/shard_map/kti,io->kto/dot_general | solution.py:143
  101.2 2.2 %all-to-all-done.2 = bf16[4,136,144]{2,1,0:T(8,128)(2,1)S(1)} async-done(((bf16[4,136,144]{2,1,0:T(8,128)(2,1)}), bf16[4,136,144]{2,1,0:T(8,128)(2,1)S(1)}, u32[]{:S(2)}, u32[]{:S(2)}) %all-to-all-start.2) | async-done | bytes 156704 | tf_op jit(solution)/shard_map/all_to_all | solution.py:142
  103.5 5.6 %all-to-all-start.1 = ((bf16[4,136,1024]{2,1,0:T(8,128)(2,1)}), bf16[4,136,1024]{2,1,0:T(8,128)(2,1)S(1)}, u32[]{:S(2)}, u32[]{:S(2)}) async-start(bf16[4,136,1024]{2,1,0:T(8,128)(2,1)} %fusion.5), calls=%async_computation.1 | async-start | bytes 2228224 | tf_op jit(solution)/shard_map/all_to_all | solution.py:146
  109.2 1.9 %collective-permute-start.1 = (bf16[128,128]{1,0:T(8,128)(2,1)S(1)}, bf16[128,128]{1,0:T(8,128)(2,1)S(1)}, u32[]{:S(2)}, u32[]{:S(2)}) collective-permute-start(bf16[128,128]{1,0:T(8,128)(2,1)S(1)} %multiply_convert_fusion.6), channel_id=1, source_target_pairs={{4,0},{0,1},{5,2},{1,3},{6,4},{2,5},{7,6},{3,7},{12,8},{8,9},{13,1... | collective-permute-start | bytes 98312 | tf_op jit(solution)/shard_map/ppermute | solution.py:175
  112.4 5.8 %all-to-all-done.1 = bf16[4,136,1024]{2,1,0:T(8,128)(2,1)S(1)} async-done(((bf16[4,136,1024]{2,1,0:T(8,128)(2,1)}), bf16[4,136,1024]{2,1,0:T(8,128)(2,1)S(1)}, u32[]{:S(2)}, u32[]{:S(2)}) %all-to-all-start.1) | async-done | bytes 1114144 | tf_op jit(solution)/shard_map/all_to_all | solution.py:146
  120.0 3.5 %all-to-all-start.3 = ((bf16[4,264,128]{2,1,0:T(8,128)(2,1)}), bf16[4,264,128]{2,1,0:T(8,128)(2,1)S(1)}, u32[]{:S(2)}, u32[]{:S(2)}) async-start(bf16[4,264,128]{2,1,0:T(8,128)(2,1)} %pad_maximum_fusion.1), calls=%async_computation.3 | async-start | bytes 540672 | tf_op jit(solution)/shard_map/all_to_all | solution.py:43
  123.8 8.4 %all-to-all-done.3 = bf16[4,264,128]{2,1,0:T(8,128)(2,1)S(1)} async-done(((bf16[4,264,128]{2,1,0:T(8,128)(2,1)}), bf16[4,264,128]{2,1,0:T(8,128)(2,1)S(1)}, u32[]{:S(2)}, u32[]{:S(2)}) %all-to-all-start.3) | async-done | bytes 270368 | tf_op jit(solution)/shard_map/all_to_all | solution.py:43
  132.8 1.2 convolution_bitcast_fusion.1
  135.1 7.2 %all-to-all-start.4 = ((bf16[4,264,128]{2,1,0:T(8,128)(2,1)}), bf16[4,264,128]{2,1,0:T(8,128)(2,1)S(1)}, u32[]{:S(2)}, u32[]{:S(2)}) async-start(bf16[4,264,128]{2,1,0:T(8,128)(2,1)} %broadcast_in_dim.143), calls=%async_computation.4 | async-start | bytes 540672 | tf_op jit(solution)/shard_map/all_to_all | solution.py:60
  142.5 17.3 %all-to-all-done.4 = bf16[4,264,128]{2,1,0:T(8,128)(2,1)S(1)} async-done(((bf16[4,264,128]{2,1,0:T(8,128)(2,1)}), bf16[4,264,128]{2,1,0:T(8,128)(2,1)S(1)}, u32[]{:S(2)}, u32[]{:S(2)}) %all-to-all-start.4) | async-done | bytes 270368 | tf_op jit(solution)/shard_map/all_to_all | solution.py:60
  162.2 4.2 %all-to-all-start.5 = ((bf16[4,256,128]{2,1,0:T(8,128)(2,1)}), bf16[4,256,128]{2,1,0:T(8,128)(2,1)S(1)}, u32[]{:S(2)}, u32[]{:S(2)}) async-start(bf16[4,256,128]{2,1,0:T(8,128)(2,1)} %copy.154), calls=%async_computation.5 | async-start | bytes 524288 | tf_op jit(solution)/shard_map/all_to_all | solution.py:72
  168.1 5.1 %all-to-all-done.5 = bf16[4,256,128]{2,1,0:T(8,128)(2,1)S(1)} async-done(((bf16[4,256,128]{2,1,0:T(8,128)(2,1)}), bf16[4,256,128]{2,1,0:T(8,128)(2,1)S(1)}, u32[]{:S(2)}, u32[]{:S(2)}) %all-to-all-start.5) | async-done | bytes 262176 | tf_op jit(solution)/shard_map/all_to_all | solution.py:72
  (93 shorter events, 14.4 us)
Async XLA Ops:
  7.2 83.1 %all-gather.2.cloned.1.call-start = ((), (), s32[]{:S(2)}) async-start(), calls=%async_computation.6 | async-start | bytes 2785280 | tf_op jit(solution)/shard_map/all_gather | solution.py:129
  61.0 3.9 %collective-permute-start = (bf16[8,4096]{1,0:T(8,128)(2,1)S(1)}, bf16[8,4096]{1,0:T(8,128)(2,1)S(1)}, u32[]{:S(2)}, u32[]{:S(2)}) collective-permute-start(bf16[8,4096]{1,0:T(8,128)(2,1)S(1)} %slice.197), channel_id=1, source_target_pairs={{0,8},{8,16},{16,24},{24,32},{32,40},{40,48},{48,56},{56,64},{64,7... | collective-permute-start | bytes 196616 | tf_op jit(solution)/shard_map/ppermute | solution.py:18
  64.9 8.4 %copy-start.5 = (f32[16]{0:T(128)S(1)}, f32[16]{0:T(128)}, u32[]{:S(2)}) copy-start(f32[16]{0:T(128)} %param.19) | copy-start | bytes 196
  64.9 8.4 %copy-start.3 = (f32[5,128]{1,0:T(8,128)S(1)}, f32[5,128]{1,0:T(8,128)}, u32[]{:S(2)}) copy-start(f32[5,128]{1,0:T(8,128)} %param.17) | copy-start | bytes 7684
  64.9 8.4 %copy-start = (f32[5,1024]{1,0:T(8,128)S(1)}, f32[5,1024]{1,0:T(8,128)}, u32[]{:S(2)}) copy-start(f32[5,1024]{1,0:T(8,128)} %param.16) | copy-start | bytes 61444
  66.0 16.5 %all-to-all-start = ((bf16[4,136,1024]{2,1,0:T(8,128)(2,1)}), bf16[4,136,1024]{2,1,0:T(8,128)(2,1)S(1)}, u32[]{:S(2)}, u32[]{:S(2)}) async-start(bf16[4,136,1024]{2,1,0:T(8,128)(2,1)} %bitcast.109), calls=%async_computation | async-start | bytes 2228224 | tf_op jit(solution)/shard_map/all_to_all | solution.py:136
  92.5 10.9 %all-to-all-start.2 = ((bf16[4,136,144]{2,1,0:T(8,128)(2,1)}), bf16[4,136,144]{2,1,0:T(8,128)(2,1)S(1)}, u32[]{:S(2)}, u32[]{:S(2)}) async-start(bf16[4,136,144]{2,1,0:T(8,128)(2,1)} %convolution_convert_fusion), calls=%async_computation.2 | async-start | bytes 557056 | tf_op jit(solution)/shard_map/all_to_all | solution.py:142
  101.2 10.6 %copy-start.2 = (f32[16]{0:T(128)S(1)}, f32[16]{0:T(128)}, u32[]{:S(2)}) copy-start(f32[16]{0:T(128)} %param.18) | copy-start | bytes 196
  103.5 14.7 %all-to-all-start.1 = ((bf16[4,136,1024]{2,1,0:T(8,128)(2,1)}), bf16[4,136,1024]{2,1,0:T(8,128)(2,1)S(1)}, u32[]{:S(2)}, u32[]{:S(2)}) async-start(bf16[4,136,1024]{2,1,0:T(8,128)(2,1)} %fusion.5), calls=%async_computation.1 | async-start | bytes 2228224 | tf_op jit(solution)/shard_map/all_to_all | solution.py:146
  109.2 9.9 %collective-permute-start.1 = (bf16[128,128]{1,0:T(8,128)(2,1)S(1)}, bf16[128,128]{1,0:T(8,128)(2,1)S(1)}, u32[]{:S(2)}, u32[]{:S(2)}) collective-permute-start(bf16[128,128]{1,0:T(8,128)(2,1)S(1)} %multiply_convert_fusion.6), channel_id=1, source_target_pairs={{4,0},{0,1},{5,2},{1,3},{6,4},{2,5},{7,6},{3,7},{12,8},{8,9},{13,1... | collective-permute-start | bytes 98312 | tf_op jit(solution)/shard_map/ppermute | solution.py:175
  111.1 8.0 %collective-permute-start.2 = (bf16[128,128]{1,0:T(8,128)(2,1)S(1)}, bf16[128,128]{1,0:T(8,128)(2,1)S(1)}, u32[]{:S(2)}, u32[]{:S(2)}) collective-permute-start(bf16[128,128]{1,0:T(8,128)(2,1)S(1)} %multiply_convert_fusion.6), channel_id=1, source_target_pairs={{0,0},{4,1},{1,2},{5,3},{2,4},{6,5},{3,6},{7,7},{8,8},{12,9},{9,10... | collective-permute-start | bytes 98312 | tf_op jit(solution)/shard_map/ppermute | solution.py:174
  120.0 12.2 %all-to-all-start.3 = ((bf16[4,264,128]{2,1,0:T(8,128)(2,1)}), bf16[4,264,128]{2,1,0:T(8,128)(2,1)S(1)}, u32[]{:S(2)}, u32[]{:S(2)}) async-start(bf16[4,264,128]{2,1,0:T(8,128)(2,1)} %pad_maximum_fusion.1), calls=%async_computation.3 | async-start | bytes 540672 | tf_op jit(solution)/shard_map/all_to_all | solution.py:43
  135.1 24.7 %all-to-all-start.4 = ((bf16[4,264,128]{2,1,0:T(8,128)(2,1)}), bf16[4,264,128]{2,1,0:T(8,128)(2,1)S(1)}, u32[]{:S(2)}, u32[]{:S(2)}) async-start(bf16[4,264,128]{2,1,0:T(8,128)(2,1)} %broadcast_in_dim.143), calls=%async_computation.4 | async-start | bytes 540672 | tf_op jit(solution)/shard_map/all_to_all | solution.py:60
  142.3 24.7 %copy-start.1 = (f32[1024]{0:T(1024)S(1)}, f32[1024]{0:T(1024)}, u32[]{:S(2)}) copy-start(f32[1024]{0:T(1024)} %param.21) | copy-start | bytes 12292
  162.2 10.9 %copy-start.4 = (f32[16]{0:T(128)S(1)}, f32[16]{0:T(128)}, u32[]{:S(2)}) copy-start(f32[16]{0:T(128)} %param.20) | copy-start | bytes 196
  162.2 10.9 %all-to-all-start.5 = ((bf16[4,256,128]{2,1,0:T(8,128)(2,1)}), bf16[4,256,128]{2,1,0:T(8,128)(2,1)S(1)}, u32[]{:S(2)}, u32[]{:S(2)}) async-start(bf16[4,256,128]{2,1,0:T(8,128)(2,1)} %copy.154), calls=%async_computation.5 | async-start | bytes 524288 | tf_op jit(solution)/shard_map/all_to_all | solution.py:72
Sparse Core Ops, SparseCore 0:
  10.7 79.6 all-gather.1

commit v10 on v8

--- a/solution.py
+++ b/solution.py
@@ -57,7 +57,7 @@
         [local[quad], entry[quad].reshape(chunk // lanes, lanes), jnp.zeros((pad_rows, lanes))]
     )
     count_hi = lax.axis_size("ch")
-    shared = lax.all_to_all(jnp.broadcast_to(summary, (count_hi,) + summary.shape), "ch", 0, 0)
+    shared = lax.all_gather(summary.astype(jnp.bfloat16), "ch").astype(jnp.float32)
     totals = shared[:, :chunk]
     quad_decay = shared[:, chunk : chunk + chunk // lanes].reshape(count_hi, chunk)
     earlier = lax.broadcasted_iota(jnp.int32, (count_hi, count_hi, chunk), 0)

time: 195 us -> 178 us (0.913)
  waiting for transfers between devices: 69.7 us -> 40.5 us
  blocking collectives: 44.6 us -> 64.9 us
  starting transfers between devices: 36.4 us -> 29 us
    all_to_all x1 -> x0, waiting for transfers between devices: 29.1 us -> none  [entering(): lax.all_to_all(jnp.broadcast_to(summary, (count_hi,) + summary.shape), 'c...]
    all_gather x0 -> x1, blocking collectives: none -> 20.3 us  [entering(): lax.all_gather(summary.astype(jnp.bfloat16), 'ch').astype(jnp.float32)]
    all_to_all x1 -> x0, starting transfers between devices: 7.21 us -> none  [entering(): lax.all_to_all(jnp.broadcast_to(summary, (count_hi,) + summary.shape), 'c...]
  transfers between devices with their start and end apart: 10 -> 9, of which waited for: 8 -> 7; matrix products, arithmetic and copies ran while one was open for 8% -> 9% of each run, Pallas kernels for 0% -> 0%
where the time goes in v10:
time: 178 us; the launch traced here: 176 us
  blocking collectives  64.9 us (36%)
  waiting for transfers between devices  40.5 us (23%)
  starting transfers between devices  29 us (16%)
  between operations  14.5 us (8%)
  matrix products  13.8 us (8%)
  local copies, waits for them, and re-layouts  7.35 us (4%)
  other arithmetic  5.93 us (3%)
    psum x2, blocking collectives, shards(): totals = lax.psum(lax.psum(powers, CTX), 'dp')  44.6 us
    all_gather x1, blocking collectives, entering(): lax.all_gather(summary.astype(jnp.bfloat16), 'ch').astype(jnp.float32)  20.3 us
    all_to_all x1, waiting for transfers between devices, shards(): incoming = lax.all_to_all(outgoing, 'dp', 0, 0)  9.1 us
    all_to_all x1, waiting for transfers between devices, entering(): incoming = lax.all_to_all(outgoing, 'cl', 0, 0).astype(jnp.float32)  8.39 us
    all_gather x1, waiting for transfers between devices, shards(): panel = lax.all_gather(local_panel, CTX, axis=0, tiled=True)  7.78 us
    all_to_all x1, starting transfers between devices, shards(): incoming = lax.all_to_all(outgoing, 'dp', 0, 0)  7.28 us
    all_to_all x1, waiting for transfers between devices, shards(): x_back = lax.all_to_all(x_partials.astype(jnp.bfloat16), 'dp', 0, 0)  5.79 us
    all_to_all x1, starting transfers between devices, shards(): x_back = lax.all_to_all(x_partials.astype(jnp.bfloat16), 'dp', 0, 0)  5.57 us
  transfers between devices with their start and end apart: 9, of which 7 were waited for; matrix products, arithmetic and copies ran while one was open for 9% of the time, Pallas kernels for 0%

profile of v10, /device:TPU:6, one launch (start us, length us, event | category | flops | bytes accessed | tf_op | source)
XLA Modules:
  0.0 175.9 jit_solution(554264727969521265)
XLA Ops:
  8.0 1.6 pad_maximum_fusion.2
  9.6 1.6 copy.123
  12.1 3.3 %multiply_convert_fusion = bf16[128,64,64]{0,2,1:T(8,128)(2,1)S(1)} fusion(f32[128,64,64]{0,1,2:T(8,128)S(1)} %convolution_bitcast_fusion), kind=kOutput, calls=%fused_computation.4 | convolution fusion | flops 403791872 | bytes 3145728 | tf_op jit(solution)/shard_map/tcb,bd->tcd/dot_general | solution.py:106
  15.8 37.0 %psum.14 = f32[4,512]{1,0:T(4,128)S(1)} all-reduce(f32[4,512]{1,0:T(4,128)S(1)} %pad_maximum_fusion.3), channel_id=1, replica_groups=mesh['dp'=4,'ch'=4,'cl'=4,'mp'=8] {'ch','cl'}, use_global_device_ids=true, to_apply=%region_4.0 | all-reduce | flops 2048 | bytes 16384 | tf_op jit(solution)/shard_map/psum | solution.py:123
  52.8 7.6 %psum.15 = f32[4,512]{1,0:T(4,128)S(1)} all-reduce(f32[4,512]{1,0:T(4,128)S(1)} %psum.14), channel_id=1, replica_groups=mesh['dp'=4,'ch'=4,'cl'=4,'mp'=8] {'dp'}, use_global_device_ids=true, to_apply=%region_5.0 | all-reduce | flops 2048 | bytes 16384 | tf_op jit(solution)/shard_map/psum | solution.py:123
  61.0 1.7 collective-permute-start
  62.7 2.1 %collective-permute-done = bf16[8,4096]{1,0:T(8,128)(2,1)S(1)} collective-permute-done((bf16[8,4096]{1,0:T(8,128)(2,1)S(1)}, bf16[8,4096]{1,0:T(8,128)(2,1)S(1)}, u32[]{:S(2)}, u32[]{:S(2)}) %collective-permute-start) | collective-permute-done | bytes 65568 | tf_op jit(solution)/shard_map/ppermute | solution.py:18
  65.0 1.1 copy.166
  66.1 7.3 %all-to-all-start = ((bf16[4,136,1024]{2,1,0:T(8,128)(2,1)}), bf16[4,136,1024]{2,1,0:T(8,128)(2,1)S(1)}, u32[]{:S(2)}, u32[]{:S(2)}) async-start(bf16[4,136,1024]{2,1,0:T(8,128)(2,1)} %bitcast.108), calls=%async_computation | async-start | bytes 2228224 | tf_op jit(solution)/shard_map/all_to_all | solution.py:134
  73.4 9.1 %all-to-all-done = bf16[4,136,1024]{2,1,0:T(8,128)(2,1)S(1)} async-done(((bf16[4,136,1024]{2,1,0:T(8,128)(2,1)}), bf16[4,136,1024]{2,1,0:T(8,128)(2,1)S(1)}, u32[]{:S(2)}, u32[]{:S(2)}) %all-to-all-start) | async-done | bytes 1114144 | tf_op jit(solution)/shard_map/all_to_all | solution.py:134
  82.5 7.8 %all-gather.2.cloned.1.call-done = bf16[1024,1168]{1,0:T(8,128)(2,1)} async-done(((bf16[64,1168]{1,0:T(8,128)(2,1)}), bf16[1024,1168]{1,0:T(8,128)(2,1)}) %all-gather.2.cloned.1.call-update) | async-done | bytes 2392080 | tf_op jit(solution)/shard_map/all_gather | solution.py:127
  90.3 2.2 %convolution_convert_fusion = bf16[4,136,144]{2,1,0:T(8,128)(2,1)} fusion(bf16[4,136,1024]{2,1,0:T(8,128)(2,1)S(1)} %all-to-all-done, bf16[1024,1168]{1,0:T(8,128)(2,1)} %all-gather.2.cloned.1.call-done), kind=kOutput, calls=%fused_computation.13 | convolution fusion | flops 160510464 | bytes 1795072 | tf_op jit(solution)/shard_map/kti,io->kto/dot_general | solution.py:137
  92.5 4.8 %all-to-all-start.2 = ((bf16[4,136,144]{2,1,0:T(8,128)(2,1)}), bf16[4,136,144]{2,1,0:T(8,128)(2,1)S(1)}, u32[]{:S(2)}, u32[]{:S(2)}) async-start(bf16[4,136,144]{2,1,0:T(8,128)(2,1)} %convolution_convert_fusion), calls=%async_computation.2 | async-start | bytes 557056 | tf_op jit(solution)/shard_map/all_to_all | solution.py:140
  97.3 3.9 %fusion.5 = bf16[4,136,1024]{2,1,0:T(8,128)(2,1)} fusion(bf16[4,136,1024]{2,1,0:T(8,128)(2,1)S(1)} %all-to-all-done, bf16[1024,1168]{1,0:T(8,128)(2,1)} %all-gather.2.cloned.1.call-done), kind=kOutput, calls=%fused_computation.6 | convolution fusion | flops 1141407744 | bytes 4325376 | tf_op jit(solution)/shard_map/kti,io->kto/dot_general | solution.py:141
  101.2 2.2 %all-to-all-done.2 = bf16[4,136,144]{2,1,0:T(8,128)(2,1)S(1)} async-done(((bf16[4,136,144]{2,1,0:T(8,128)(2,1)}), bf16[4,136,144]{2,1,0:T(8,128)(2,1)S(1)}, u32[]{:S(2)}, u32[]{:S(2)}) %all-to-all-start.2) | async-done | bytes 156704 | tf_op jit(solution)/shard_map/all_to_all | solution.py:140
  103.5 5.6 %all-to-all-start.1 = ((bf16[4,136,1024]{2,1,0:T(8,128)(2,1)}), bf16[4,136,1024]{2,1,0:T(8,128)(2,1)S(1)}, u32[]{:S(2)}, u32[]{:S(2)}) async-start(bf16[4,136,1024]{2,1,0:T(8,128)(2,1)} %fusion.5), calls=%async_computation.1 | async-start | bytes 2228224 | tf_op jit(solution)/shard_map/all_to_all | solution.py:144
  109.2 1.9 %collective-permute-start.1 = (bf16[128,128]{1,0:T(8,128)(2,1)S(1)}, bf16[128,128]{1,0:T(8,128)(2,1)S(1)}, u32[]{:S(2)}, u32[]{:S(2)}) collective-permute-start(bf16[128,128]{1,0:T(8,128)(2,1)S(1)} %multiply_convert_fusion.6), channel_id=1, source_target_pairs={{4,0},{0,1},{5,2},{1,3},{6,4},{2,5},{7,6},{3,7},{12,8},{8,9},{13,1... | collective-permute-start | bytes 98312 | tf_op jit(solution)/shard_map/ppermute | solution.py:173
  112.4 5.8 %all-to-all-done.1 = bf16[4,136,1024]{2,1,0:T(8,128)(2,1)S(1)} async-done(((bf16[4,136,1024]{2,1,0:T(8,128)(2,1)}), bf16[4,136,1024]{2,1,0:T(8,128)(2,1)S(1)}, u32[]{:S(2)}, u32[]{:S(2)}) %all-to-all-start.1) | async-done | bytes 1114144 | tf_op jit(solution)/shard_map/all_to_all | solution.py:144
  120.0 3.5 %all-to-all-start.3 = ((bf16[4,264,128]{2,1,0:T(8,128)(2,1)}), bf16[4,264,128]{2,1,0:T(8,128)(2,1)S(1)}, u32[]{:S(2)}, u32[]{:S(2)}) async-start(bf16[4,264,128]{2,1,0:T(8,128)(2,1)} %pad_maximum_fusion.1), calls=%async_computation.3 | async-start | bytes 540672 | tf_op jit(solution)/shard_map/all_to_all | solution.py:43
  123.8 8.4 %all-to-all-done.3 = bf16[4,264,128]{2,1,0:T(8,128)(2,1)S(1)} async-done(((bf16[4,264,128]{2,1,0:T(8,128)(2,1)}), bf16[4,264,128]{2,1,0:T(8,128)(2,1)S(1)}, u32[]{:S(2)}, u32[]{:S(2)}) %all-to-all-start.3) | async-done | bytes 270368 | tf_op jit(solution)/shard_map/all_to_all | solution.py:43
  132.8 1.2 convolution_bitcast_fusion.1
  134.6 20.3 %all_gather.8 = bf16[4,264,128]{2,1,0:T(8,128)(2,1)S(1)} all-gather(bf16[1,264,128]{2,1,0:T(8,128)(2,1)S(1)} %copy.142), channel_id=1, replica_groups=mesh['dp'=4,'ch'=4,'cl'=4,'mp'=8] {'ch'}, dimensions={0}, use_global_device_ids=true | all-gather | bytes 337920 | tf_op jit(solution)/shard_map/all_gather | solution.py:60
  157.4 3.5 %all-to-all-start.4 = ((bf16[4,256,128]{2,1,0:T(8,128)(2,1)}), bf16[4,256,128]{2,1,0:T(8,128)(2,1)S(1)}, u32[]{:S(2)}, u32[]{:S(2)}) async-start(bf16[4,256,128]{2,1,0:T(8,128)(2,1)} %copy.143), calls=%async_computation.4 | async-start | bytes 524288 | tf_op jit(solution)/shard_map/all_to_all | solution.py:70
  162.7 5.0 %all-to-all-done.4 = bf16[4,256,128]{2,1,0:T(8,128)(2,1)S(1)} async-done(((bf16[4,256,128]{2,1,0:T(8,128)(2,1)}), bf16[4,256,128]{2,1,0:T(8,128)(2,1)S(1)}, u32[]{:S(2)}, u32[]{:S(2)}) %all-to-all-start.4) | async-done | bytes 262176 | tf_op jit(solution)/shard_map/all_to_all | solution.py:70
  (91 shorter events, 12.8 us)
Async XLA Ops:
  7.2 83.1 %all-gather.2.cloned.1.call-start = ((), (), s32[]{:S(2)}) async-start(), calls=%async_computation.5 | async-start | bytes 2785280 | tf_op jit(solution)/shard_map/all_gather | solution.py:127
  61.0 3.9 %collective-permute-start = (bf16[8,4096]{1,0:T(8,128)(2,1)S(1)}, bf16[8,4096]{1,0:T(8,128)(2,1)S(1)}, u32[]{:S(2)}, u32[]{:S(2)}) collective-permute-start(bf16[8,4096]{1,0:T(8,128)(2,1)S(1)} %slice.197), channel_id=1, source_target_pairs={{0,8},{8,16},{16,24},{24,32},{32,40},{40,48},{48,56},{56,64},{64,7... | collective-permute-start | bytes 196616 | tf_op jit(solution)/shard_map/ppermute | solution.py:18
  64.9 8.4 %copy-start.5 = (f32[16]{0:T(128)S(1)}, f32[16]{0:T(128)}, u32[]{:S(2)}) copy-start(f32[16]{0:T(128)} %param.19) | copy-start | bytes 196
  65.0 8.4 %copy-start.3 = (f32[5,128]{1,0:T(8,128)S(1)}, f32[5,128]{1,0:T(8,128)}, u32[]{:S(2)}) copy-start(f32[5,128]{1,0:T(8,128)} %param.17) | copy-start | bytes 7684
  65.0 8.4 %copy-start = (f32[5,1024]{1,0:T(8,128)S(1)}, f32[5,1024]{1,0:T(8,128)}, u32[]{:S(2)}) copy-start(f32[5,1024]{1,0:T(8,128)} %param.16) | copy-start | bytes 61444
  66.1 16.4 %all-to-all-start = ((bf16[4,136,1024]{2,1,0:T(8,128)(2,1)}), bf16[4,136,1024]{2,1,0:T(8,128)(2,1)S(1)}, u32[]{:S(2)}, u32[]{:S(2)}) async-start(bf16[4,136,1024]{2,1,0:T(8,128)(2,1)} %bitcast.108), calls=%async_computation | async-start | bytes 2228224 | tf_op jit(solution)/shard_map/all_to_all | solution.py:134
  92.5 11.0 %all-to-all-start.2 = ((bf16[4,136,144]{2,1,0:T(8,128)(2,1)}), bf16[4,136,144]{2,1,0:T(8,128)(2,1)S(1)}, u32[]{:S(2)}, u32[]{:S(2)}) async-start(bf16[4,136,144]{2,1,0:T(8,128)(2,1)} %convolution_convert_fusion), calls=%async_computation.2 | async-start | bytes 557056 | tf_op jit(solution)/shard_map/all_to_all | solution.py:140
  101.2 10.6 %copy-start.2 = (f32[16]{0:T(128)S(1)}, f32[16]{0:T(128)}, u32[]{:S(2)}) copy-start(f32[16]{0:T(128)} %param.18) | copy-start | bytes 196
  103.5 14.7 %all-to-all-start.1 = ((bf16[4,136,1024]{2,1,0:T(8,128)(2,1)}), bf16[4,136,1024]{2,1,0:T(8,128)(2,1)S(1)}, u32[]{:S(2)}, u32[]{:S(2)}) async-start(bf16[4,136,1024]{2,1,0:T(8,128)(2,1)} %fusion.5), calls=%async_computation.1 | async-start | bytes 2228224 | tf_op jit(solution)/shard_map/all_to_all | solution.py:144
  109.2 9.9 %collective-permute-start.1 = (bf16[128,128]{1,0:T(8,128)(2,1)S(1)}, bf16[128,128]{1,0:T(8,128)(2,1)S(1)}, u32[]{:S(2)}, u32[]{:S(2)}) collective-permute-start(bf16[128,128]{1,0:T(8,128)(2,1)S(1)} %multiply_convert_fusion.6), channel_id=1, source_target_pairs={{4,0},{0,1},{5,2},{1,3},{6,4},{2,5},{7,6},{3,7},{12,8},{8,9},{13,1... | collective-permute-start | bytes 98312 | tf_op jit(solution)/shard_map/ppermute | solution.py:173
  111.1 8.0 %collective-permute-start.2 = (bf16[128,128]{1,0:T(8,128)(2,1)S(1)}, bf16[128,128]{1,0:T(8,128)(2,1)S(1)}, u32[]{:S(2)}, u32[]{:S(2)}) collective-permute-start(bf16[128,128]{1,0:T(8,128)(2,1)S(1)} %multiply_convert_fusion.6), channel_id=1, source_target_pairs={{0,0},{4,1},{1,2},{5,3},{2,4},{6,5},{3,6},{7,7},{8,8},{12,9},{9,10... | collective-permute-start | bytes 98312 | tf_op jit(solution)/shard_map/ppermute | solution.py:172
  120.0 12.2 %all-to-all-start.3 = ((bf16[4,264,128]{2,1,0:T(8,128)(2,1)}), bf16[4,264,128]{2,1,0:T(8,128)(2,1)S(1)}, u32[]{:S(2)}, u32[]{:S(2)}) async-start(bf16[4,264,128]{2,1,0:T(8,128)(2,1)} %pad_maximum_fusion.1), calls=%async_computation.3 | async-start | bytes 540672 | tf_op jit(solution)/shard_map/all_to_all | solution.py:43
  134.6 27.0 %copy-start.1 = (f32[1024]{0:T(1024)S(1)}, f32[1024]{0:T(1024)}, u32[]{:S(2)}) copy-start(f32[1024]{0:T(1024)} %param.21) | copy-start | bytes 12292
  157.4 10.3 %copy-start.4 = (f32[16]{0:T(128)S(1)}, f32[16]{0:T(128)}, u32[]{:S(2)}) copy-start(f32[16]{0:T(128)} %param.20) | copy-start | bytes 196
  157.4 10.3 %all-to-all-start.4 = ((bf16[4,256,128]{2,1,0:T(8,128)(2,1)}), bf16[4,256,128]{2,1,0:T(8,128)(2,1)S(1)}, u32[]{:S(2)}, u32[]{:S(2)}) async-start(bf16[4,256,128]{2,1,0:T(8,128)(2,1)} %copy.143), calls=%async_computation.4 | async-start | bytes 524288 | tf_op jit(solution)/shard_map/all_to_all | solution.py:70
Sparse Core Ops, SparseCore 0:
  10.7 79.6 all-gather.1

commit v11 on v10

--- a/solution.py
+++ b/solution.py
@@ -57,15 +57,14 @@
         [local[quad], entry[quad].reshape(chunk // lanes, lanes), jnp.zeros((pad_rows, lanes))]
     )
     count_hi = lax.axis_size("ch")
-    shared = lax.all_gather(summary.astype(jnp.bfloat16), "ch").astype(jnp.float32)
-    totals = shared[:, :chunk]
-    quad_decay = shared[:, chunk : chunk + chunk // lanes].reshape(count_hi, chunk)
-    earlier = lax.broadcasted_iota(jnp.int32, (count_hi, count_hi, chunk), 0)
-    middle = lax.broadcasted_iota(jnp.int32, (count_hi, count_hi, chunk), 1)
-    spans = jnp.logical_and(middle > earlier, middle < quads)
-    across = jnp.prod(jnp.where(spans, quad_decay[None], 1.0), 1)
-    across = jnp.where(earlier[:, 0] < quads, across, 0.0)
-    entering_state = jnp.einsum("qr,qrl->rl", across, totals, precision=HIGH)
+    summary = summary.astype(jnp.bfloat16)
+    entering_state = jnp.zeros((chunk, lanes), jnp.float32)
+    scale = jnp.ones((chunk,), jnp.float32)
+    for shift in range(1, count_hi):
+        pairs = [(source, source + shift) for source in range(count_hi - shift)]
+        arrived = lax.ppermute(summary, "ch", pairs).astype(jnp.float32)
+        entering_state = entering_state + scale[:, None] * arrived[:chunk]
+        scale = scale * arrived[chunk : chunk + chunk // lanes].reshape(chunk)
     carried = local[:quad] + entry[:quad, :, None] * entering_state[None]
     returned = lax.all_to_all(carried.astype(jnp.bfloat16), "cl", 0, 0)
     return returned.astype(jnp.float32).reshape(contrib.shape)

time: 178 us -> 179 us (level)
  blocking collectives: 64.9 us -> 44.6 us
  starting transfers between devices: 29 us -> 42.9 us
  waiting for transfers between devices: 40.5 us -> 49.7 us
    all_gather x1 -> x0, blocking collectives: 20.3 us -> none  [entering(): lax.all_gather(summary.astype(jnp.bfloat16), 'ch').astype(jnp.float32)]
    ppermute x0 -> x3, starting transfers between devices: none -> 13.9 us  [entering(): arrived = lax.ppermute(summary, 'ch', pairs).astype(jnp.float32)]
    ppermute x0 -> x3, waiting for transfers between devices: none -> 6.68 us  [entering(): arrived = lax.ppermute(summary, 'ch', pairs).astype(jnp.float32)]
    all_to_all x1, waiting for transfers between devices: 5.05 us -> 7.51 us  [entering(): returned = lax.all_to_all(carried.astype(jnp.bfloat16), 'cl', 0, 0)]
  transfers between devices with their start and end apart: 9 -> 12, of which waited for: 7 -> 9; matrix products, arithmetic and copies ran while one was open for 9% -> 9% of each run, Pallas kernels for 0% -> 0%
where the time goes in v11:
time: 179 us; the launch traced here: 177 us
  waiting for transfers between devices  49.7 us (28%)
  blocking collectives  44.6 us (25%)
  starting transfers between devices  42.9 us (24%)
  between operations  14.5 us (8%)
  matrix products  12.8 us (7%)
  local copies, waits for them, and re-layouts  7.21 us (4%)
  other arithmetic  5.74 us (3%)
    psum x2, blocking collectives, shards(): totals = lax.psum(lax.psum(powers, CTX), 'dp')  44.6 us
    ppermute x3, starting transfers between devices, entering(): arrived = lax.ppermute(summary, 'ch', pairs).astype(jnp.float32)  13.9 us
    all_to_all x1, waiting for transfers between devices, shards(): incoming = lax.all_to_all(outgoing, 'dp', 0, 0)  9.11 us
    all_to_all x1, waiting for transfers between devices, entering(): incoming = lax.all_to_all(outgoing, 'cl', 0, 0).astype(jnp.float32)  8.45 us
    all_gather x1, waiting for transfers between devices, shards(): panel = lax.all_gather(local_panel, CTX, axis=0, tiled=True)  7.81 us
    all_to_all x1, waiting for transfers between devices, entering(): returned = lax.all_to_all(carried.astype(jnp.bfloat16), 'cl', 0, 0)  7.51 us
    all_to_all x1, starting transfers between devices, shards(): incoming = lax.all_to_all(outgoing, 'dp', 0, 0)  7.28 us
    ppermute x3, waiting for transfers between devices, entering(): arrived = lax.ppermute(summary, 'ch', pairs).astype(jnp.float32)  6.68 us
  transfers between devices with their start and end apart: 12, of which 9 were waited for; matrix products, arithmetic and copies ran while one was open for 9% of the time, Pallas kernels for 0%

profile of v11, /device:TPU:6, one launch (start us, length us, event | category | flops | bytes accessed | tf_op | source)
XLA Modules:
  0.0 177.4 jit_solution(3171912691565294006)
XLA Ops:
  8.0 1.6 pad_maximum_fusion.2
  9.6 1.6 copy.135
  12.1 3.3 %multiply_convert_fusion = bf16[128,64,64]{0,2,1:T(8,128)(2,1)S(1)} fusion(f32[128,64,64]{0,1,2:T(8,128)S(1)} %convolution_bitcast_fusion), kind=kOutput, calls=%fused_computation.4 | convolution fusion | flops 403791872 | bytes 3145728 | tf_op jit(solution)/shard_map/tcb,bd->tcd/dot_general | solution.py:105
  15.8 37.0 %psum.14 = f32[4,512]{1,0:T(4,128)S(1)} all-reduce(f32[4,512]{1,0:T(4,128)S(1)} %pad_maximum_fusion.3), channel_id=1, replica_groups=mesh['dp'=4,'ch'=4,'cl'=4,'mp'=8] {'ch','cl'}, use_global_device_ids=true, to_apply=%region_4.0 | all-reduce | flops 2048 | bytes 16384 | tf_op jit(solution)/shard_map/psum | solution.py:122
  52.8 7.6 %psum.15 = f32[4,512]{1,0:T(4,128)S(1)} all-reduce(f32[4,512]{1,0:T(4,128)S(1)} %psum.14), channel_id=1, replica_groups=mesh['dp'=4,'ch'=4,'cl'=4,'mp'=8] {'dp'}, use_global_device_ids=true, to_apply=%region_5.0 | all-reduce | flops 2048 | bytes 16384 | tf_op jit(solution)/shard_map/psum | solution.py:122
  61.0 1.7 collective-permute-start
  62.7 2.1 %collective-permute-done = bf16[8,4096]{1,0:T(8,128)(2,1)S(1)} collective-permute-done((bf16[8,4096]{1,0:T(8,128)(2,1)S(1)}, bf16[8,4096]{1,0:T(8,128)(2,1)S(1)}, u32[]{:S(2)}, u32[]{:S(2)}) %collective-permute-start) | collective-permute-done | bytes 65568 | tf_op jit(solution)/shard_map/ppermute | solution.py:18
  66.0 7.3 %all-to-all-start = ((bf16[4,136,1024]{2,1,0:T(8,128)(2,1)}), bf16[4,136,1024]{2,1,0:T(8,128)(2,1)S(1)}, u32[]{:S(2)}, u32[]{:S(2)}) async-start(bf16[4,136,1024]{2,1,0:T(8,128)(2,1)} %bitcast.104), calls=%async_computation | async-start | bytes 2228224 | tf_op jit(solution)/shard_map/all_to_all | solution.py:133
  73.4 9.1 %all-to-all-done = bf16[4,136,1024]{2,1,0:T(8,128)(2,1)S(1)} async-done(((bf16[4,136,1024]{2,1,0:T(8,128)(2,1)}), bf16[4,136,1024]{2,1,0:T(8,128)(2,1)S(1)}, u32[]{:S(2)}, u32[]{:S(2)}) %all-to-all-start) | async-done | bytes 1114144 | tf_op jit(solution)/shard_map/all_to_all | solution.py:133
  82.5 7.8 %all-gather.2.cloned.1.call-done = bf16[1024,1168]{1,0:T(8,128)(2,1)} async-done(((bf16[64,1168]{1,0:T(8,128)(2,1)}), bf16[1024,1168]{1,0:T(8,128)(2,1)}) %all-gather.2.cloned.1.call-update) | async-done | bytes 2392080 | tf_op jit(solution)/shard_map/all_gather | solution.py:126
  90.3 2.2 %convolution_convert_fusion = bf16[4,136,144]{2,1,0:T(8,128)(2,1)} fusion(bf16[4,136,1024]{2,1,0:T(8,128)(2,1)S(1)} %all-to-all-done, bf16[1024,1168]{1,0:T(8,128)(2,1)} %all-gather.2.cloned.1.call-done), kind=kOutput, calls=%fused_computation.13 | convolution fusion | flops 160510464 | bytes 1795072 | tf_op jit(solution)/shard_map/kti,io->kto/dot_general | solution.py:136
  92.5 4.9 %all-to-all-start.2 = ((bf16[4,136,144]{2,1,0:T(8,128)(2,1)}), bf16[4,136,144]{2,1,0:T(8,128)(2,1)S(1)}, u32[]{:S(2)}, u32[]{:S(2)}) async-start(bf16[4,136,144]{2,1,0:T(8,128)(2,1)} %convolution_convert_fusion), calls=%async_computation.2 | async-start | bytes 557056 | tf_op jit(solution)/shard_map/all_to_all | solution.py:139
  97.4 3.9 %fusion.5 = bf16[4,136,1024]{2,1,0:T(8,128)(2,1)} fusion(bf16[4,136,1024]{2,1,0:T(8,128)(2,1)S(1)} %all-to-all-done, bf16[1024,1168]{1,0:T(8,128)(2,1)} %all-gather.2.cloned.1.call-done), kind=kOutput, calls=%fused_computation.6 | convolution fusion | flops 1141407744 | bytes 4325376 | tf_op jit(solution)/shard_map/kti,io->kto/dot_general | solution.py:140
  101.3 2.2 %all-to-all-done.2 = bf16[4,136,144]{2,1,0:T(8,128)(2,1)S(1)} async-done(((bf16[4,136,144]{2,1,0:T(8,128)(2,1)}), bf16[4,136,144]{2,1,0:T(8,128)(2,1)S(1)}, u32[]{:S(2)}, u32[]{:S(2)}) %all-to-all-start.2) | async-done | bytes 156704 | tf_op jit(solution)/shard_map/all_to_all | solution.py:139
  103.6 5.6 %all-to-all-start.1 = ((bf16[4,136,1024]{2,1,0:T(8,128)(2,1)}), bf16[4,136,1024]{2,1,0:T(8,128)(2,1)S(1)}, u32[]{:S(2)}, u32[]{:S(2)}) async-start(bf16[4,136,1024]{2,1,0:T(8,128)(2,1)} %fusion.5), calls=%async_computation.1 | async-start | bytes 2228224 | tf_op jit(solution)/shard_map/all_to_all | solution.py:143
  109.3 1.9 %collective-permute-start.1 = (bf16[128,128]{1,0:T(8,128)(2,1)S(1)}, bf16[128,128]{1,0:T(8,128)(2,1)S(1)}, u32[]{:S(2)}, u32[]{:S(2)}) collective-permute-start(bf16[128,128]{1,0:T(8,128)(2,1)S(1)} %multiply_convert_fusion.6), channel_id=1, source_target_pairs={{4,0},{0,1},{5,2},{1,3},{6,4},{2,5},{7,6},{3,7},{12,8},{8,9},{13,1... | collective-permute-start | bytes 98312 | tf_op jit(solution)/shard_map/ppermute | solution.py:172
  112.5 5.8 %all-to-all-done.1 = bf16[4,136,1024]{2,1,0:T(8,128)(2,1)S(1)} async-done(((bf16[4,136,1024]{2,1,0:T(8,128)(2,1)}), bf16[4,136,1024]{2,1,0:T(8,128)(2,1)S(1)}, u32[]{:S(2)}, u32[]{:S(2)}) %all-to-all-start.1) | async-done | bytes 1114144 | tf_op jit(solution)/shard_map/all_to_all | solution.py:143
  120.1 3.4 %all-to-all-start.3 = ((bf16[4,264,128]{2,1,0:T(8,128)(2,1)}), bf16[4,264,128]{2,1,0:T(8,128)(2,1)S(1)}, u32[]{:S(2)}, u32[]{:S(2)}) async-start(bf16[4,264,128]{2,1,0:T(8,128)(2,1)} %pad_maximum_fusion.1), calls=%async_computation.3 | async-start | bytes 540672 | tf_op jit(solution)/shard_map/all_to_all | solution.py:43
  123.9 8.5 %all-to-all-done.3 = bf16[4,264,128]{2,1,0:T(8,128)(2,1)S(1)} async-done(((bf16[4,264,128]{2,1,0:T(8,128)(2,1)}), bf16[4,264,128]{2,1,0:T(8,128)(2,1)S(1)}, u32[]{:S(2)}, u32[]{:S(2)}) %all-to-all-start.3) | async-done | bytes 270368 | tf_op jit(solution)/shard_map/all_to_all | solution.py:43
  134.4 5.2 %collective-permute-start.3 = (bf16[264,128]{1,0:T(8,128)(2,1)S(1)}, bf16[264,128]{1,0:T(8,128)(2,1)S(1)}, u32[]{:S(2)}, u32[]{:S(2)}) collective-permute-start(bf16[264,128]{1,0:T(8,128)(2,1)S(1)} %maximum_maximum_fusion), channel_id=1, source_target_pairs={{0,32},{32,64},{64,96},{1,33},{33,65},{65,97},{2,34},{34,66},{66,9... | collective-permute-start | bytes 202760 | tf_op jit(solution)/shard_map/ppermute | solution.py:65
  139.6 7.4 %collective-permute-start.4 = (bf16[264,128]{1,0:T(8,128)(2,1)S(1)}, bf16[264,128]{1,0:T(8,128)(2,1)S(1)}, u32[]{:S(2)}, u32[]{:S(2)}) collective-permute-start(bf16[264,128]{1,0:T(8,128)(2,1)S(1)} %maximum_maximum_fusion), channel_id=1, source_target_pairs={{0,64},{32,96},{1,65},{33,97},{2,66},{34,98},{3,67},{35,99},{4,68}... | collective-permute-start | bytes 202760 | tf_op jit(solution)/shard_map/ppermute | solution.py:65
  149.0 6.3 %collective-permute-done.5 = bf16[264,128]{1,0:T(8,128)(2,1)S(1)} collective-permute-done((bf16[264,128]{1,0:T(8,128)(2,1)S(1)}, bf16[264,128]{1,0:T(8,128)(2,1)S(1)}, u32[]{:S(2)}, u32[]{:S(2)}) %collective-permute-start.5) | collective-permute-done | bytes 67616 | tf_op jit(solution)/shard_map/ppermute | solution.py:65
  156.5 3.5 %all-to-all-start.4 = ((bf16[4,256,128]{2,1,0:T(8,128)(2,1)}), bf16[4,256,128]{2,1,0:T(8,128)(2,1)S(1)}, u32[]{:S(2)}, u32[]{:S(2)}) async-start(bf16[4,256,128]{2,1,0:T(8,128)(2,1)} %copy.154), calls=%async_computation.4 | async-start | bytes 524288 | tf_op jit(solution)/shard_map/all_to_all | solution.py:69
  161.7 7.5 %all-to-all-done.4 = bf16[4,256,128]{2,1,0:T(8,128)(2,1)S(1)} async-done(((bf16[4,256,128]{2,1,0:T(8,128)(2,1)}), bf16[4,256,128]{2,1,0:T(8,128)(2,1)S(1)}, u32[]{:S(2)}, u32[]{:S(2)}) %all-to-all-start.4) | async-done | bytes 262176 | tf_op jit(solution)/shard_map/all_to_all | solution.py:69
  (93 shorter events, 15.4 us)
Async XLA Ops:
  7.2 83.1 %all-gather.2.cloned.1.call-start = ((), (), s32[]{:S(2)}) async-start(), calls=%async_computation.5 | async-start | bytes 2785280 | tf_op jit(solution)/shard_map/all_gather | solution.py:126
  61.0 3.8 %collective-permute-start = (bf16[8,4096]{1,0:T(8,128)(2,1)S(1)}, bf16[8,4096]{1,0:T(8,128)(2,1)S(1)}, u32[]{:S(2)}, u32[]{:S(2)}) collective-permute-start(bf16[8,4096]{1,0:T(8,128)(2,1)S(1)} %slice.208), channel_id=1, source_target_pairs={{0,8},{8,16},{16,24},{24,32},{32,40},{40,48},{48,56},{56,64},{64,7... | collective-permute-start | bytes 196616 | tf_op jit(solution)/shard_map/ppermute | solution.py:18
  64.9 8.4 %copy-start.5 = (f32[16]{0:T(128)S(1)}, f32[16]{0:T(128)}, u32[]{:S(2)}) copy-start(f32[16]{0:T(128)} %param.19) | copy-start | bytes 196
  64.9 8.4 %copy-start.3 = (f32[5,128]{1,0:T(8,128)S(1)}, f32[5,128]{1,0:T(8,128)}, u32[]{:S(2)}) copy-start(f32[5,128]{1,0:T(8,128)} %param.17) | copy-start | bytes 7684
  64.9 8.4 %copy-start = (f32[5,1024]{1,0:T(8,128)S(1)}, f32[5,1024]{1,0:T(8,128)}, u32[]{:S(2)}) copy-start(f32[5,1024]{1,0:T(8,128)} %param.16) | copy-start | bytes 61444
  66.0 16.5 %all-to-all-start = ((bf16[4,136,1024]{2,1,0:T(8,128)(2,1)}), bf16[4,136,1024]{2,1,0:T(8,128)(2,1)S(1)}, u32[]{:S(2)}, u32[]{:S(2)}) async-start(bf16[4,136,1024]{2,1,0:T(8,128)(2,1)} %bitcast.104), calls=%async_computation | async-start | bytes 2228224 | tf_op jit(solution)/shard_map/all_to_all | solution.py:133
  92.5 11.1 %all-to-all-start.2 = ((bf16[4,136,144]{2,1,0:T(8,128)(2,1)}), bf16[4,136,144]{2,1,0:T(8,128)(2,1)S(1)}, u32[]{:S(2)}, u32[]{:S(2)}) async-start(bf16[4,136,144]{2,1,0:T(8,128)(2,1)} %convolution_convert_fusion), calls=%async_computation.2 | async-start | bytes 557056 | tf_op jit(solution)/shard_map/all_to_all | solution.py:139
  101.3 10.6 %copy-start.2 = (f32[16]{0:T(128)S(1)}, f32[16]{0:T(128)}, u32[]{:S(2)}) copy-start(f32[16]{0:T(128)} %param.18) | copy-start | bytes 196
  103.6 14.7 %all-to-all-start.1 = ((bf16[4,136,1024]{2,1,0:T(8,128)(2,1)}), bf16[4,136,1024]{2,1,0:T(8,128)(2,1)S(1)}, u32[]{:S(2)}, u32[]{:S(2)}) async-start(bf16[4,136,1024]{2,1,0:T(8,128)(2,1)} %fusion.5), calls=%async_computation.1 | async-start | bytes 2228224 | tf_op jit(solution)/shard_map/all_to_all | solution.py:143
  109.3 9.9 %collective-permute-start.1 = (bf16[128,128]{1,0:T(8,128)(2,1)S(1)}, bf16[128,128]{1,0:T(8,128)(2,1)S(1)}, u32[]{:S(2)}, u32[]{:S(2)}) collective-permute-start(bf16[128,128]{1,0:T(8,128)(2,1)S(1)} %multiply_convert_fusion.6), channel_id=1, source_target_pairs={{4,0},{0,1},{5,2},{1,3},{6,4},{2,5},{7,6},{3,7},{12,8},{8,9},{13,1... | collective-permute-start | bytes 98312 | tf_op jit(solution)/shard_map/ppermute | solution.py:172
  111.2 8.0 %collective-permute-start.2 = (bf16[128,128]{1,0:T(8,128)(2,1)S(1)}, bf16[128,128]{1,0:T(8,128)(2,1)S(1)}, u32[]{:S(2)}, u32[]{:S(2)}) collective-permute-start(bf16[128,128]{1,0:T(8,128)(2,1)S(1)} %multiply_convert_fusion.6), channel_id=1, source_target_pairs={{0,0},{4,1},{1,2},{5,3},{2,4},{6,5},{3,6},{7,7},{8,8},{12,9},{9,10... | collective-permute-start | bytes 98312 | tf_op jit(solution)/shard_map/ppermute | solution.py:171
  120.1 12.2 %all-to-all-start.3 = ((bf16[4,264,128]{2,1,0:T(8,128)(2,1)}), bf16[4,264,128]{2,1,0:T(8,128)(2,1)S(1)}, u32[]{:S(2)}, u32[]{:S(2)}) async-start(bf16[4,264,128]{2,1,0:T(8,128)(2,1)} %pad_maximum_fusion.1), calls=%async_computation.3 | async-start | bytes 540672 | tf_op jit(solution)/shard_map/all_to_all | solution.py:43
  134.1 26.5 %copy-start.1 = (f32[1024]{0:T(1024)S(1)}, f32[1024]{0:T(1024)}, u32[]{:S(2)}) copy-start(f32[1024]{0:T(1024)} %param.21) | copy-start | bytes 12292
  134.4 14.1 %collective-permute-start.3 = (bf16[264,128]{1,0:T(8,128)(2,1)S(1)}, bf16[264,128]{1,0:T(8,128)(2,1)S(1)}, u32[]{:S(2)}, u32[]{:S(2)}) collective-permute-start(bf16[264,128]{1,0:T(8,128)(2,1)S(1)} %maximum_maximum_fusion), channel_id=1, source_target_pairs={{0,32},{32,64},{64,96},{1,33},{33,65},{65,97},{2,34},{34,66},{66,9... | collective-permute-start | bytes 202760 | tf_op jit(solution)/shard_map/ppermute | solution.py:65
  139.6 9.3 %collective-permute-start.4 = (bf16[264,128]{1,0:T(8,128)(2,1)S(1)}, bf16[264,128]{1,0:T(8,128)(2,1)S(1)}, u32[]{:S(2)}, u32[]{:S(2)}) collective-permute-start(bf16[264,128]{1,0:T(8,128)(2,1)S(1)} %maximum_maximum_fusion), channel_id=1, source_target_pairs={{0,64},{32,96},{1,65},{33,97},{2,66},{34,98},{3,67},{35,99},{4,68}... | collective-permute-start | bytes 202760 | tf_op jit(solution)/shard_map/ppermute | solution.py:65
  147.1 8.2 %collective-permute-start.5 = (bf16[264,128]{1,0:T(8,128)(2,1)S(1)}, bf16[264,128]{1,0:T(8,128)(2,1)S(1)}, u32[]{:S(2)}, u32[]{:S(2)}) collective-permute-start(bf16[264,128]{1,0:T(8,128)(2,1)S(1)} %maximum_maximum_fusion), channel_id=1, source_target_pairs={{0,96},{1,97},{2,98},{3,99},{4,100},{5,101},{6,102},{7,103},{8,104... | collective-permute-start | bytes 202760 | tf_op jit(solution)/shard_map/ppermute | solution.py:65
  156.5 12.8 %copy-start.4 = (f32[16]{0:T(128)S(1)}, f32[16]{0:T(128)}, u32[]{:S(2)}) copy-start(f32[16]{0:T(128)} %param.20) | copy-start | bytes 196
  156.5 12.7 %all-to-all-start.4 = ((bf16[4,256,128]{2,1,0:T(8,128)(2,1)}), bf16[4,256,128]{2,1,0:T(8,128)(2,1)S(1)}, u32[]{:S(2)}, u32[]{:S(2)}) async-start(bf16[4,256,128]{2,1,0:T(8,128)(2,1)} %copy.154), calls=%async_computation.4 | async-start | bytes 524288 | tf_op jit(solution)/shard_map/all_to_all | solution.py:69
Sparse Core Ops, SparseCore 0:
  10.7 79.6 all-gather.1

commit v12 on v10

--- a/solution.py
+++ b/solution.py
@@ -137,13 +137,13 @@
     side_partials = jnp.einsum(
         "kti,io->kto", incoming, panel[:, x_end:], preferred_element_type=jnp.float32
     )
-    side_back = lax.all_to_all(side_partials.astype(jnp.bfloat16), "dp", 0, 0)
+    side_back = lax.all_to_all(side_partials, "dp", 0, 0)
     x_partials = jnp.einsum(
         "kti,io->kto", incoming, panel[:, :x_end], preferred_element_type=jnp.float32
     )
-    x_back = lax.all_to_all(x_partials.astype(jnp.bfloat16), "dp", 0, 0)
-    side_ext = jnp.sum(side_back.astype(jnp.float32), 0)
-    x_ext = jnp.sum(x_back.astype(jnp.float32), 0)
+    x_back = lax.all_to_all(x_partials, "dp", 0, 0)
+    side_ext = jnp.sum(side_back, 0)
+    x_ext = jnp.sum(x_back, 0)
     x_cols = x_end
     bc_width = bc_end - x_end
     dt_proj = lax.optimization_barrier(side_ext[rim:, bc_width:].astype(jnp.bfloat16))

time: 178 us -> 187 us (1.051)
  waiting for transfers between devices: 40.5 us -> 47.2 us
    all_to_all x2, waiting for transfers between devices: 8.02 us -> 16.5 us  [the longest x1 12.2 us: shards(): x_back = lax.all_to_all(x_partials, 'dp', 0, 0)]
where the time goes in v12:
time: 187 us; the launch traced here: 183 us
  blocking collectives  64.4 us (34%)
  waiting for transfers between devices  47.2 us (25%)
  starting transfers between devices  29.4 us (16%)
  between operations  14.5 us (8%)
  matrix products  14.3 us (8%)
  local copies, waits for them, and re-layouts  7.42 us (4%)
  other arithmetic  6.03 us (3%)
    psum x2, blocking collectives, shards(): totals = lax.psum(lax.psum(powers, CTX), 'dp')  44.6 us
    all_gather x1, blocking collectives, entering(): lax.all_gather(summary.astype(jnp.bfloat16), 'ch').astype(jnp.float32)  19.8 us
    all_to_all x1, waiting for transfers between devices, shards(): x_back = lax.all_to_all(x_partials, 'dp', 0, 0)  12.2 us
    all_to_all x1, waiting for transfers between devices, shards(): incoming = lax.all_to_all(outgoing, 'dp', 0, 0)  9.16 us
    all_gather x1, waiting for transfers between devices, shards(): panel = lax.all_gather(local_panel, CTX, axis=0, tiled=True)  7.81 us
    all_to_all x1, starting transfers between devices, shards(): incoming = lax.all_to_all(outgoing, 'dp', 0, 0)  7.28 us
    all_to_all x1, waiting for transfers between devices, entering(): incoming = lax.all_to_all(outgoing, 'cl', 0, 0).astype(jnp.float32)  6.57 us
    all_to_all x1, starting transfers between devices, shards(): x_back = lax.all_to_all(x_partials, 'dp', 0, 0)  5.65 us
  transfers between devices with their start and end apart: 9, of which 7 were waited for; matrix products, arithmetic and copies ran while one was open for 9% of the time, Pallas kernels for 0%

profile of v12, /device:TPU:6, one launch (start us, length us, event | category | flops | bytes accessed | tf_op | source)
XLA Modules:
  0.0 183.2 jit_solution(9031749717265466281)
XLA Ops:
  8.0 1.6 pad_maximum_fusion.2
  9.6 1.6 copy.123
  12.1 3.3 %multiply_convert_fusion = bf16[128,64,64]{0,2,1:T(8,128)(2,1)S(1)} fusion(f32[128,64,64]{0,1,2:T(8,128)S(1)} %convolution_bitcast_fusion), kind=kOutput, calls=%fused_computation.4 | convolution fusion | flops 403791872 | bytes 3145728 | tf_op jit(solution)/shard_map/tcb,bd->tcd/dot_general | solution.py:106
  15.8 37.0 %psum.14 = f32[4,512]{1,0:T(4,128)S(1)} all-reduce(f32[4,512]{1,0:T(4,128)S(1)} %pad_maximum_fusion.3), channel_id=1, replica_groups=mesh['dp'=4,'ch'=4,'cl'=4,'mp'=8] {'ch','cl'}, use_global_device_ids=true, to_apply=%region_4.0 | all-reduce | flops 2048 | bytes 16384 | tf_op jit(solution)/shard_map/psum | solution.py:123
  52.8 7.6 %psum.15 = f32[4,512]{1,0:T(4,128)S(1)} all-reduce(f32[4,512]{1,0:T(4,128)S(1)} %psum.14), channel_id=1, replica_groups=mesh['dp'=4,'ch'=4,'cl'=4,'mp'=8] {'dp'}, use_global_device_ids=true, to_apply=%region_5.0 | all-reduce | flops 2048 | bytes 16384 | tf_op jit(solution)/shard_map/psum | solution.py:123
  61.0 1.7 collective-permute-start
  62.7 2.1 %collective-permute-done = bf16[8,4096]{1,0:T(8,128)(2,1)S(1)} collective-permute-done((bf16[8,4096]{1,0:T(8,128)(2,1)S(1)}, bf16[8,4096]{1,0:T(8,128)(2,1)S(1)}, u32[]{:S(2)}, u32[]{:S(2)}) %collective-permute-start) | collective-permute-done | bytes 65568 | tf_op jit(solution)/shard_map/ppermute | solution.py:18
  65.0 1.1 copy.171
  66.1 7.3 %all-to-all-start = ((bf16[4,136,1024]{2,1,0:T(8,128)(2,1)}), bf16[4,136,1024]{2,1,0:T(8,128)(2,1)S(1)}, u32[]{:S(2)}, u32[]{:S(2)}) async-start(bf16[4,136,1024]{2,1,0:T(8,128)(2,1)} %bitcast.106), calls=%async_computation | async-start | bytes 2228224 | tf_op jit(solution)/shard_map/all_to_all | solution.py:134
  73.3 9.2 %all-to-all-done = bf16[4,136,1024]{2,1,0:T(8,128)(2,1)S(1)} async-done(((bf16[4,136,1024]{2,1,0:T(8,128)(2,1)}), bf16[4,136,1024]{2,1,0:T(8,128)(2,1)S(1)}, u32[]{:S(2)}, u32[]{:S(2)}) %all-to-all-start) | async-done | bytes 1114144 | tf_op jit(solution)/shard_map/all_to_all | solution.py:134
  82.5 7.8 %all-gather.2.cloned.1.call-done = bf16[1024,1168]{1,0:T(8,128)(2,1)} async-done(((bf16[64,1168]{1,0:T(8,128)(2,1)}), bf16[1024,1168]{1,0:T(8,128)(2,1)}) %all-gather.2.cloned.1.call-update) | async-done | bytes 2392080 | tf_op jit(solution)/shard_map/all_gather | solution.py:127
  90.3 2.3 %fusion.10 = f32[4,136,144]{2,1,0:T(8,128)} fusion(bf16[4,136,1024]{2,1,0:T(8,128)(2,1)S(1)} %all-to-all-done, bf16[1024,1168]{1,0:T(8,128)(2,1)} %all-gather.2.cloned.1.call-done), kind=kOutput, calls=%fused_computation.20 | convolution fusion | flops 160432128 | bytes 1951744 | tf_op jit(solution)/shard_map/kti,io->kto/dot_general | solution.py:137
  92.6 4.8 %all-to-all-start.2 = ((f32[4,136,144]{2,1,0:T(8,128)}), f32[4,136,144]{2,1,0:T(8,128)S(1)}, u32[]{:S(2)}, u32[]{:S(2)}) async-start(f32[4,136,144]{2,1,0:T(8,128)} %fusion.10), calls=%async_computation.2 | async-start | bytes 1114112 | tf_op jit(solution)/shard_map/all_to_all | solution.py:140
  97.4 4.3 %fusion = f32[4,136,1024]{2,1,0:T(8,128)} fusion(bf16[4,136,1024]{2,1,0:T(8,128)(2,1)S(1)} %all-to-all-done, bf16[1024,1168]{1,0:T(8,128)(2,1)} %all-gather.2.cloned.1.call-done), kind=kOutput, calls=%fused_computation.1 | convolution fusion | flops 1140850688 | bytes 5439488 | tf_op jit(solution)/shard_map/kti,io->kto/dot_general | solution.py:141
  101.7 4.2 %all-to-all-done.2 = f32[4,136,144]{2,1,0:T(8,128)S(1)} async-done(((f32[4,136,144]{2,1,0:T(8,128)}), f32[4,136,144]{2,1,0:T(8,128)S(1)}, u32[]{:S(2)}, u32[]{:S(2)}) %all-to-all-start.2) | async-done | bytes 313376 | tf_op jit(solution)/shard_map/all_to_all | solution.py:140
  105.9 5.7 %all-to-all-start.1 = ((f32[4,136,1024]{2,1,0:T(8,128)}), f32[4,136,1024]{2,1,0:T(8,128)S(1)}, u32[]{:S(2)}, u32[]{:S(2)}) async-start(f32[4,136,1024]{2,1,0:T(8,128)} %fusion), calls=%async_computation.1 | async-start | bytes 4456448 | tf_op jit(solution)/shard_map/all_to_all | solution.py:144
  112.1 1.9 %collective-permute-start.1 = (bf16[128,128]{0,1:T(8,128)(2,1)S(1)}, bf16[128,128]{0,1:T(8,128)(2,1)S(1)}, u32[]{:S(2)}, u32[]{:S(2)}) collective-permute-start(bf16[128,128]{0,1:T(8,128)(2,1)S(1)} %multiply_convert_fusion.6), channel_id=1, source_target_pairs={{4,0},{0,1},{5,2},{1,3},{6,4},{2,5},{7,6},{3,7},{12,8},{8,9},{13,1... | collective-permute-start | bytes 98312 | tf_op jit(solution)/shard_map/ppermute | solution.py:173
  115.2 12.2 %all-to-all-done.1 = f32[4,136,1024]{2,1,0:T(8,128)S(1)} async-done(((f32[4,136,1024]{2,1,0:T(8,128)}), f32[4,136,1024]{2,1,0:T(8,128)S(1)}, u32[]{:S(2)}, u32[]{:S(2)}) %all-to-all-start.1) | async-done | bytes 2228256 | tf_op jit(solution)/shard_map/all_to_all | solution.py:144
  129.3 3.5 %all-to-all-start.3 = ((bf16[4,264,128]{2,1,0:T(8,128)(2,1)}), bf16[4,264,128]{2,1,0:T(8,128)(2,1)S(1)}, u32[]{:S(2)}, u32[]{:S(2)}) async-start(bf16[4,264,128]{2,1,0:T(8,128)(2,1)} %pad_maximum_fusion.1), calls=%async_computation.3 | async-start | bytes 540672 | tf_op jit(solution)/shard_map/all_to_all | solution.py:43
  133.0 6.6 %all-to-all-done.3 = bf16[4,264,128]{2,1,0:T(8,128)(2,1)S(1)} async-done(((bf16[4,264,128]{2,1,0:T(8,128)(2,1)}), bf16[4,264,128]{2,1,0:T(8,128)(2,1)S(1)}, u32[]{:S(2)}, u32[]{:S(2)}) %all-to-all-start.3) | async-done | bytes 270368 | tf_op jit(solution)/shard_map/all_to_all | solution.py:43
  140.2 1.2 convolution_bitcast_fusion.1
  142.0 19.8 %all_gather.8 = bf16[4,264,128]{2,1,0:T(8,128)(2,1)S(1)} all-gather(bf16[1,264,128]{2,1,0:T(8,128)(2,1)S(1)} %copy.143), channel_id=1, replica_groups=mesh['dp'=4,'ch'=4,'cl'=4,'mp'=8] {'ch'}, dimensions={0}, use_global_device_ids=true | all-gather | bytes 337920 | tf_op jit(solution)/shard_map/all_gather | solution.py:60
  164.3 3.9 %all-to-all-start.4 = ((bf16[4,256,128]{2,1,0:T(8,128)(2,1)}), bf16[4,256,128]{2,1,0:T(8,128)(2,1)S(1)}, u32[]{:S(2)}, u32[]{:S(2)}) async-start(bf16[4,256,128]{2,1,0:T(8,128)(2,1)} %copy.144), calls=%async_computation.4 | async-start | bytes 524288 | tf_op jit(solution)/shard_map/all_to_all | solution.py:70
  169.9 5.1 %all-to-all-done.4 = bf16[4,256,128]{2,1,0:T(8,128)(2,1)S(1)} async-done(((bf16[4,256,128]{2,1,0:T(8,128)(2,1)}), bf16[4,256,128]{2,1,0:T(8,128)(2,1)S(1)}, u32[]{:S(2)}, u32[]{:S(2)}) %all-to-all-start.4) | async-done | bytes 262176 | tf_op jit(solution)/shard_map/all_to_all | solution.py:70
  (91 shorter events, 13.0 us)
Async XLA Ops:
  7.2 83.1 %all-gather.2.cloned.1.call-start = ((), (), s32[]{:S(2)}) async-start(), calls=%async_computation.5 | async-start | bytes 2785280 | tf_op jit(solution)/shard_map/all_gather | solution.py:127
  61.0 3.9 %collective-permute-start = (bf16[8,4096]{1,0:T(8,128)(2,1)S(1)}, bf16[8,4096]{1,0:T(8,128)(2,1)S(1)}, u32[]{:S(2)}, u32[]{:S(2)}) collective-permute-start(bf16[8,4096]{1,0:T(8,128)(2,1)S(1)} %slice.197), channel_id=1, source_target_pairs={{0,8},{8,16},{16,24},{24,32},{32,40},{40,48},{48,56},{56,64},{64,7... | collective-permute-start | bytes 196616 | tf_op jit(solution)/shard_map/ppermute | solution.py:18
  64.9 8.4 %copy-start.5 = (f32[16]{0:T(128)S(1)}, f32[16]{0:T(128)}, u32[]{:S(2)}) copy-start(f32[16]{0:T(128)} %param.19) | copy-start | bytes 196
  66.1 16.4 %all-to-all-start = ((bf16[4,136,1024]{2,1,0:T(8,128)(2,1)}), bf16[4,136,1024]{2,1,0:T(8,128)(2,1)S(1)}, u32[]{:S(2)}, u32[]{:S(2)}) async-start(bf16[4,136,1024]{2,1,0:T(8,128)(2,1)} %bitcast.106), calls=%async_computation | async-start | bytes 2228224 | tf_op jit(solution)/shard_map/all_to_all | solution.py:134
  92.6 13.3 %all-to-all-start.2 = ((f32[4,136,144]{2,1,0:T(8,128)}), f32[4,136,144]{2,1,0:T(8,128)S(1)}, u32[]{:S(2)}, u32[]{:S(2)}) async-start(f32[4,136,144]{2,1,0:T(8,128)} %fusion.10), calls=%async_computation.2 | async-start | bytes 1114112 | tf_op jit(solution)/shard_map/all_to_all | solution.py:140
  101.7 9.9 %copy-start.3 = (f32[5,128]{1,0:T(8,128)S(1)}, f32[5,128]{1,0:T(8,128)}, u32[]{:S(2)}) copy-start(f32[5,128]{1,0:T(8,128)} %param.17) | copy-start | bytes 7684
  101.7 9.9 %copy-start = (f32[5,1024]{1,0:T(8,128)S(1)}, f32[5,1024]{1,0:T(8,128)}, u32[]{:S(2)}) copy-start(f32[5,1024]{1,0:T(8,128)} %param.16) | copy-start | bytes 61444
  101.7 13.0 %copy-start.2 = (f32[16]{0:T(128)S(1)}, f32[16]{0:T(128)}, u32[]{:S(2)}) copy-start(f32[16]{0:T(128)} %param.18) | copy-start | bytes 196
  105.9 21.5 %all-to-all-start.1 = ((f32[4,136,1024]{2,1,0:T(8,128)}), f32[4,136,1024]{2,1,0:T(8,128)S(1)}, u32[]{:S(2)}, u32[]{:S(2)}) async-start(f32[4,136,1024]{2,1,0:T(8,128)} %fusion), calls=%async_computation.1 | async-start | bytes 4456448 | tf_op jit(solution)/shard_map/all_to_all | solution.py:144
  112.1 16.2 %collective-permute-start.1 = (bf16[128,128]{0,1:T(8,128)(2,1)S(1)}, bf16[128,128]{0,1:T(8,128)(2,1)S(1)}, u32[]{:S(2)}, u32[]{:S(2)}) collective-permute-start(bf16[128,128]{0,1:T(8,128)(2,1)S(1)} %multiply_convert_fusion.6), channel_id=1, source_target_pairs={{4,0},{0,1},{5,2},{1,3},{6,4},{2,5},{7,6},{3,7},{12,8},{8,9},{13,1... | collective-permute-start | bytes 98312 | tf_op jit(solution)/shard_map/ppermute | solution.py:173
  114.0 14.3 %collective-permute-start.2 = (bf16[128,128]{0,1:T(8,128)(2,1)S(1)}, bf16[128,128]{0,1:T(8,128)(2,1)S(1)}, u32[]{:S(2)}, u32[]{:S(2)}) collective-permute-start(bf16[128,128]{0,1:T(8,128)(2,1)S(1)} %multiply_convert_fusion.6), channel_id=1, source_target_pairs={{0,0},{4,1},{1,2},{5,3},{2,4},{6,5},{3,6},{7,7},{8,8},{12,9},{9,10... | collective-permute-start | bytes 98312 | tf_op jit(solution)/shard_map/ppermute | solution.py:172
  129.3 10.3 %all-to-all-start.3 = ((bf16[4,264,128]{2,1,0:T(8,128)(2,1)}), bf16[4,264,128]{2,1,0:T(8,128)(2,1)S(1)}, u32[]{:S(2)}, u32[]{:S(2)}) async-start(bf16[4,264,128]{2,1,0:T(8,128)(2,1)} %pad_maximum_fusion.1), calls=%async_computation.3 | async-start | bytes 540672 | tf_op jit(solution)/shard_map/all_to_all | solution.py:43
  142.0 26.8 %copy-start.1 = (f32[1024]{0:T(1024)S(1)}, f32[1024]{0:T(1024)}, u32[]{:S(2)}) copy-start(f32[1024]{0:T(1024)} %param.21) | copy-start | bytes 12292
  164.3 10.7 %copy-start.4 = (f32[16]{0:T(128)S(1)}, f32[16]{0:T(128)}, u32[]{:S(2)}) copy-start(f32[16]{0:T(128)} %param.20) | copy-start | bytes 196
  164.3 10.7 %all-to-all-start.4 = ((bf16[4,256,128]{2,1,0:T(8,128)(2,1)}), bf16[4,256,128]{2,1,0:T(8,128)(2,1)S(1)}, u32[]{:S(2)}, u32[]{:S(2)}) async-start(bf16[4,256,128]{2,1,0:T(8,128)(2,1)} %copy.144), calls=%async_computation.4 | async-start | bytes 524288 | tf_op jit(solution)/shard_map/all_to_all | solution.py:70
Sparse Core Ops, SparseCore 0:
  10.7 79.6 all-gather.1

commit v13 on v12

--- a/solution.py
+++ b/solution.py
@@ -137,12 +137,19 @@
     side_partials = jnp.einsum(
         "kti,io->kto", incoming, panel[:, x_end:], preferred_element_type=jnp.float32
     )
-    side_back = lax.all_to_all(side_partials, "dp", 0, 0)
+    place_dp = lax.axis_index("dp")
+    side_ext = lax.dynamic_index_in_dim(side_partials, place_dp, 0, keepdims=False)
+    for shift in range(1, seqs):
+        outgoing_side = lax.dynamic_index_in_dim(
+            side_partials, (place_dp + shift) % seqs, 0, keepdims=False
+        )
+        side_ext = side_ext + lax.ppermute(
+            outgoing_side, "dp", [(k, (k + shift) % seqs) for k in range(seqs)]
+        )
     x_partials = jnp.einsum(
         "kti,io->kto", incoming, panel[:, :x_end], preferred_element_type=jnp.float32
     )
     x_back = lax.all_to_all(x_partials, "dp", 0, 0)
-    side_ext = jnp.sum(side_back, 0)
     x_ext = jnp.sum(x_back, 0)
     x_cols = x_end
     bc_width = bc_end - x_end

time: 187 us -> 194 us (1.037)
  starting transfers between devices: 29.4 us -> 32.1 us
  local copies, waits for them, and re-layouts: 7.42 us -> 9.49 us
  other arithmetic: 6.03 us -> 8.02 us
    ppermute x0 -> x3, waiting for transfers between devices: none -> 13.3 us  [shards(): lax.ppermute(outgoing_side, 'dp', [(k, (k + shift) % seqs) for k in range...]
    all_to_all x1, waiting for transfers between devices: 12.2 us -> 0.01 us  [shards(): x_back = lax.all_to_all(x_partials, 'dp', 0, 0)]
    ppermute x0 -> x3, starting transfers between devices: none -> 8.66 us  [shards(): lax.ppermute(outgoing_side, 'dp', [(k, (k + shift) % seqs) for k in range...]
    all_to_all x1 -> x0, starting transfers between devices: 4.78 us -> none  [shards(): side_back = lax.all_to_all(side_partials, 'dp', 0, 0)]
    all_to_all x1 -> x0, waiting for transfers between devices: 4.23 us -> none  [shards(): side_back = lax.all_to_all(side_partials, 'dp', 0, 0)]
    all_to_all x1, waiting for transfers between devices: 5.05 us -> 7.47 us  [entering(): returned = lax.all_to_all(carried.astype(jnp.bfloat16), 'cl', 0, 0)]
    ppermute x1, waiting for transfers between devices: 0.01 us -> 1.98 us  [shards(): got_b = lax.ppermute(bc_own, 'mp', even_first)]
  transfers between devices with their start and end apart: 9 -> 11, of which waited for: 7 -> 9; matrix products, arithmetic and copies ran while one was open for 9% -> 9% of each run, Pallas kernels for 0% -> 0%
where the time goes in v13:
time: 194 us; the launch traced here: 192 us
  blocking collectives  65.7 us (34%)
  waiting for transfers between devices  48.6 us (25%)
  starting transfers between devices  32.1 us (17%)
  between operations  14.5 us (7%)
  matrix products  13.4 us (7%)
  local copies, waits for them, and re-layouts  9.49 us (5%)
  other arithmetic  8.02 us (4%)
    psum x2, blocking collectives, shards(): totals = lax.psum(lax.psum(powers, CTX), 'dp')  44.6 us
    all_gather x1, blocking collectives, entering(): lax.all_gather(summary.astype(jnp.bfloat16), 'ch').astype(jnp.float32)  21.1 us
    ppermute x3, waiting for transfers between devices, shards(): lax.ppermute(outgoing_side, 'dp', [(k, (k + shift) % seqs) for k in range...  13.3 us
    ppermute x3, starting transfers between devices, shards(): lax.ppermute(outgoing_side, 'dp', [(k, (k + shift) % seqs) for k in range...  8.66 us
    all_to_all x1, waiting for transfers between devices, entering(): incoming = lax.all_to_all(outgoing, 'cl', 0, 0).astype(jnp.float32)  8.49 us
    all_gather x1, waiting for transfers between devices, shards(): panel = lax.all_gather(local_panel, CTX, axis=0, tiled=True)  7.8 us
    all_to_all x1, waiting for transfers between devices, entering(): returned = lax.all_to_all(carried.astype(jnp.bfloat16), 'cl', 0, 0)  7.47 us
    all_to_all x1, waiting for transfers between devices, shards(): incoming = lax.all_to_all(outgoing, 'dp', 0, 0)  7.42 us
  transfers between devices with their start and end apart: 11, of which 9 were waited for; matrix products, arithmetic and copies ran while one was open for 9% of the time, Pallas kernels for 0%

profile of v13, /device:TPU:6, one launch (start us, length us, event | category | flops | bytes accessed | tf_op | source)
XLA Modules:
  0.0 192.0 jit_solution(1761898831308127613)
XLA Ops:
  8.0 1.6 pad_maximum_fusion.2
  9.6 1.6 copy.99
  12.1 3.3 %multiply_convert_fusion = bf16[128,64,64]{0,2,1:T(8,128)(2,1)S(1)} fusion(f32[128,64,64]{0,1,2:T(8,128)S(1)} %convolution_bitcast_fusion), kind=kOutput, calls=%fused_computation.4 | convolution fusion | flops 403791872 | bytes 3145728 | tf_op jit(solution)/shard_map/tcb,bd->tcd/dot_general | solution.py:106
  15.8 37.0 %psum.14 = f32[4,512]{1,0:T(4,128)S(1)} all-reduce(f32[4,512]{1,0:T(4,128)S(1)} %pad_maximum_fusion.3), channel_id=1, replica_groups=mesh['dp'=4,'ch'=4,'cl'=4,'mp'=8] {'ch','cl'}, use_global_device_ids=true, to_apply=%region_4.0 | all-reduce | flops 2048 | bytes 16384 | tf_op jit(solution)/shard_map/psum | solution.py:123
  52.8 7.6 %psum.15 = f32[4,512]{1,0:T(4,128)S(1)} all-reduce(f32[4,512]{1,0:T(4,128)S(1)} %psum.14), channel_id=1, replica_groups=mesh['dp'=4,'ch'=4,'cl'=4,'mp'=8] {'dp'}, use_global_device_ids=true, to_apply=%region_5.0 | all-reduce | flops 2048 | bytes 16384 | tf_op jit(solution)/shard_map/psum | solution.py:123
  61.0 1.7 collective-permute-start
  62.7 2.1 %collective-permute-done = bf16[8,4096]{1,0:T(8,128)(2,1)S(1)} collective-permute-done((bf16[8,4096]{1,0:T(8,128)(2,1)S(1)}, bf16[8,4096]{1,0:T(8,128)(2,1)S(1)}, u32[]{:S(2)}, u32[]{:S(2)}) %collective-permute-start) | collective-permute-done | bytes 65568 | tf_op jit(solution)/shard_map/ppermute | solution.py:18
  66.1 7.3 %all-to-all-start = ((bf16[4,136,1024]{2,1,0:T(8,128)(2,1)}), bf16[4,136,1024]{2,1,0:T(8,128)(2,1)S(1)}, u32[]{:S(2)}, u32[]{:S(2)}) async-start(bf16[4,136,1024]{2,1,0:T(8,128)(2,1)} %bitcast.117), calls=%async_computation | async-start | bytes 2228224 | tf_op jit(solution)/shard_map/all_to_all | solution.py:134
  75.1 7.4 %all-to-all-done = bf16[4,136,1024]{2,1,0:T(8,128)(2,1)S(1)} async-done(((bf16[4,136,1024]{2,1,0:T(8,128)(2,1)}), bf16[4,136,1024]{2,1,0:T(8,128)(2,1)S(1)}, u32[]{:S(2)}, u32[]{:S(2)}) %all-to-all-start) | async-done | bytes 1114144 | tf_op jit(solution)/shard_map/all_to_all | solution.py:134
  82.5 7.8 %all-gather.2.cloned.1.call-done = bf16[1024,1168]{1,0:T(8,128)(2,1)} async-done(((bf16[64,1168]{1,0:T(8,128)(2,1)}), bf16[1024,1168]{1,0:T(8,128)(2,1)}) %all-gather.2.cloned.1.call-update) | async-done | bytes 2392080 | tf_op jit(solution)/shard_map/all_gather | solution.py:127
  90.3 4.3 %fusion = f32[4,136,1024]{2,1,0:T(8,128)} fusion(bf16[4,136,1024]{2,1,0:T(8,128)(2,1)S(1)} %all-to-all-done, bf16[1024,1168]{1,0:T(8,128)(2,1)} %all-gather.2.cloned.1.call-done), kind=kOutput, calls=%fused_computation.1 | convolution fusion | flops 1140850688 | bytes 5439488 | tf_op jit(solution)/shard_map/kti,io->kto/dot_general | solution.py:149
  94.6 4.8 %all-to-all-start.1 = ((f32[4,136,1024]{2,1,0:T(8,128)}), f32[4,136,1024]{2,1,0:T(8,128)S(1)}, u32[]{:S(2)}, u32[]{:S(2)}) async-start(f32[4,136,1024]{2,1,0:T(8,128)} %fusion), calls=%async_computation.1 | async-start | bytes 4456448 | tf_op jit(solution)/shard_map/all_to_all | solution.py:152
  99.4 1.5 fusion.10
  101.0 1.9 %collective-permute-start.1 = (f32[136,144]{0,1:T(8,128)S(1)}, f32[136,144]{0,1:T(8,128)S(1)}, u32[]{:S(2)}, u32[]{:S(2)}) collective-permute-start(f32[136,144]{0,1:T(8,128)S(1)} %bitcast.130), channel_id=1, source_target_pairs={{0,128},{128,256},{256,384},{384,0},{1,129},{129,257},{257,385},{3... | collective-permute-start | bytes 235016 | tf_op jit(solution)/shard_map/ppermute | solution.py:146
  103.1 4.8 %collective-permute-start.2 = (f32[136,144]{0,1:T(8,128)S(1)}, f32[136,144]{0,1:T(8,128)S(1)}, u32[]{:S(2)}, u32[]{:S(2)}) collective-permute-start(f32[136,144]{0,1:T(8,128)S(1)} %bitcast.131), channel_id=1, source_target_pairs={{0,256},{128,384},{256,0},{384,128},{1,257},{129,385},{257,1},{385... | collective-permute-start | bytes 235016 | tf_op jit(solution)/shard_map/ppermute | solution.py:146
  108.0 1.9 %collective-permute-start.3 = (f32[136,144]{0,1:T(8,128)S(1)}, f32[136,144]{0,1:T(8,128)S(1)}, u32[]{:S(2)}, u32[]{:S(2)}) collective-permute-start(f32[136,144]{0,1:T(8,128)S(1)} %bitcast.132), channel_id=1, source_target_pairs={{0,384},{128,0},{256,128},{384,256},{1,385},{129,1},{257,129},{385... | collective-permute-start | bytes 235016 | tf_op jit(solution)/shard_map/ppermute | solution.py:146
  110.1 10.6 %collective-permute-done.1 = f32[136,144]{0,1:T(8,128)S(1)} collective-permute-done((f32[136,144]{0,1:T(8,128)S(1)}, f32[136,144]{0,1:T(8,128)S(1)}, u32[]{:S(2)}, u32[]{:S(2)}) %collective-permute-start.1) | collective-permute-done | bytes 78368 | tf_op jit(solution)/shard_map/ppermute | solution.py:146
  124.3 1.9 %collective-permute-start.4 = (bf16[128,128]{0,1:T(8,128)(2,1)S(1)}, bf16[128,128]{0,1:T(8,128)(2,1)S(1)}, u32[]{:S(2)}, u32[]{:S(2)}) collective-permute-start(bf16[128,128]{0,1:T(8,128)(2,1)S(1)} %multiply_convert_fusion.6), channel_id=1, source_target_pairs={{4,0},{0,1},{5,2},{1,3},{6,4},{2,5},{7,6},{3,7},{12,8},{8,9},{13,1... | collective-permute-start | bytes 98312 | tf_op jit(solution)/shard_map/ppermute | solution.py:180
  129.7 2.0 %collective-permute-done.4 = bf16[128,128]{0,1:T(8,128)(2,1)S(1)} collective-permute-done((bf16[128,128]{0,1:T(8,128)(2,1)S(1)}, bf16[128,128]{0,1:T(8,128)(2,1)S(1)}, u32[]{:S(2)}, u32[]{:S(2)}) %collective-permute-start.4) | collective-permute-done | bytes 32800 | tf_op jit(solution)/shard_map/ppermute | solution.py:180
  132.6 3.4 %all-to-all-start.2 = ((bf16[4,264,128]{2,1,0:T(8,128)(2,1)}), bf16[4,264,128]{2,1,0:T(8,128)(2,1)S(1)}, u32[]{:S(2)}, u32[]{:S(2)}) async-start(bf16[4,264,128]{2,1,0:T(8,128)(2,1)} %pad_maximum_fusion.1), calls=%async_computation.2 | async-start | bytes 540672 | tf_op jit(solution)/shard_map/all_to_all | solution.py:43
  136.4 8.5 %all-to-all-done.2 = bf16[4,264,128]{2,1,0:T(8,128)(2,1)S(1)} async-done(((bf16[4,264,128]{2,1,0:T(8,128)(2,1)}), bf16[4,264,128]{2,1,0:T(8,128)(2,1)S(1)}, u32[]{:S(2)}, u32[]{:S(2)}) %all-to-all-start.2) | async-done | bytes 270368 | tf_op jit(solution)/shard_map/all_to_all | solution.py:43
  147.2 21.1 %all_gather.8 = bf16[4,264,128]{2,1,0:T(8,128)(2,1)S(1)} all-gather(bf16[1,264,128]{2,1,0:T(8,128)(2,1)S(1)} %copy.122), channel_id=1, replica_groups=mesh['dp'=4,'ch'=4,'cl'=4,'mp'=8] {'ch'}, dimensions={0}, use_global_device_ids=true | all-gather | bytes 337920 | tf_op jit(solution)/shard_map/all_gather | solution.py:60
  170.9 3.6 %all-to-all-start.3 = ((bf16[4,256,128]{2,1,0:T(8,128)(2,1)}), bf16[4,256,128]{2,1,0:T(8,128)(2,1)S(1)}, u32[]{:S(2)}, u32[]{:S(2)}) async-start(bf16[4,256,128]{2,1,0:T(8,128)(2,1)} %copy.123), calls=%async_computation.3 | async-start | bytes 524288 | tf_op jit(solution)/shard_map/all_to_all | solution.py:70
  176.3 7.5 %all-to-all-done.3 = bf16[4,256,128]{2,1,0:T(8,128)(2,1)S(1)} async-done(((bf16[4,256,128]{2,1,0:T(8,128)(2,1)}), bf16[4,256,128]{2,1,0:T(8,128)(2,1)S(1)}, u32[]{:S(2)}, u32[]{:S(2)}) %all-to-all-start.3) | async-done | bytes 262176 | tf_op jit(solution)/shard_map/all_to_all | solution.py:70
  (99 shorter events, 22.0 us)
Async XLA Ops:
  7.2 83.1 %all-gather.2.cloned.1.call-start = ((), (), s32[]{:S(2)}) async-start(), calls=%async_computation.4 | async-start | bytes 2785280 | tf_op jit(solution)/shard_map/all_gather | solution.py:127
  61.0 3.9 %collective-permute-start = (bf16[8,4096]{1,0:T(8,128)(2,1)S(1)}, bf16[8,4096]{1,0:T(8,128)(2,1)S(1)}, u32[]{:S(2)}, u32[]{:S(2)}) collective-permute-start(bf16[8,4096]{1,0:T(8,128)(2,1)S(1)} %slice.197), channel_id=1, source_target_pairs={{0,8},{8,16},{16,24},{24,32},{32,40},{40,48},{48,56},{56,64},{64,7... | collective-permute-start | bytes 196616 | tf_op jit(solution)/shard_map/ppermute | solution.py:18
  64.9 8.4 %copy-start.5 = (f32[16]{0:T(128)S(1)}, f32[16]{0:T(128)}, u32[]{:S(2)}) copy-start(f32[16]{0:T(128)} %param.19) | copy-start | bytes 196
  64.9 8.9 %copy-start.3 = (f32[5,128]{1,0:T(8,128)S(1)}, f32[5,128]{1,0:T(8,128)}, u32[]{:S(2)}) copy-start(f32[5,128]{1,0:T(8,128)} %param.17) | copy-start | bytes 7684
  65.0 9.5 %copy-start.1 = (f32[5,1024]{1,0:T(8,128)S(1)}, f32[5,1024]{1,0:T(8,128)}, u32[]{:S(2)}) copy-start(f32[5,1024]{1,0:T(8,128)} %param.16) | copy-start | bytes 61444
  66.1 16.4 %all-to-all-start = ((bf16[4,136,1024]{2,1,0:T(8,128)(2,1)}), bf16[4,136,1024]{2,1,0:T(8,128)(2,1)S(1)}, u32[]{:S(2)}, u32[]{:S(2)}) async-start(bf16[4,136,1024]{2,1,0:T(8,128)(2,1)} %bitcast.117), calls=%async_computation | async-start | bytes 2228224 | tf_op jit(solution)/shard_map/all_to_all | solution.py:134
  94.6 34.2 %all-to-all-start.1 = ((f32[4,136,1024]{2,1,0:T(8,128)}), f32[4,136,1024]{2,1,0:T(8,128)S(1)}, u32[]{:S(2)}, u32[]{:S(2)}) async-start(f32[4,136,1024]{2,1,0:T(8,128)} %fusion), calls=%async_computation.1 | async-start | bytes 4456448 | tf_op jit(solution)/shard_map/all_to_all | solution.py:152
  101.0 19.6 %collective-permute-start.1 = (f32[136,144]{0,1:T(8,128)S(1)}, f32[136,144]{0,1:T(8,128)S(1)}, u32[]{:S(2)}, u32[]{:S(2)}) collective-permute-start(f32[136,144]{0,1:T(8,128)S(1)} %bitcast.130), channel_id=1, source_target_pairs={{0,128},{128,256},{256,384},{384,0},{1,129},{129,257},{257,385},{3... | collective-permute-start | bytes 235016 | tf_op jit(solution)/shard_map/ppermute | solution.py:146
  103.1 18.8 %collective-permute-start.2 = (f32[136,144]{0,1:T(8,128)S(1)}, f32[136,144]{0,1:T(8,128)S(1)}, u32[]{:S(2)}, u32[]{:S(2)}) collective-permute-start(f32[136,144]{0,1:T(8,128)S(1)} %bitcast.131), channel_id=1, source_target_pairs={{0,256},{128,384},{256,0},{384,128},{1,257},{129,385},{257,1},{385... | collective-permute-start | bytes 235016 | tf_op jit(solution)/shard_map/ppermute | solution.py:146
  107.9 21.1 %copy-start = (f32[1,1024]{1,0:T(1,128)S(1)}, f32[1,1024]{1,0:T(1,128)}, u32[]{:S(2)}) copy-start(f32[1,1024]{1,0:T(1,128)} %get-tuple-element.42) | copy-start | bytes 12292
  108.0 15.3 %collective-permute-start.3 = (f32[136,144]{0,1:T(8,128)S(1)}, f32[136,144]{0,1:T(8,128)S(1)}, u32[]{:S(2)}, u32[]{:S(2)}) collective-permute-start(f32[136,144]{0,1:T(8,128)S(1)} %bitcast.132), channel_id=1, source_target_pairs={{0,384},{128,0},{256,128},{384,256},{1,385},{129,1},{257,129},{385... | collective-permute-start | bytes 235016 | tf_op jit(solution)/shard_map/ppermute | solution.py:146
  124.3 7.3 %collective-permute-start.4 = (bf16[128,128]{0,1:T(8,128)(2,1)S(1)}, bf16[128,128]{0,1:T(8,128)(2,1)S(1)}, u32[]{:S(2)}, u32[]{:S(2)}) collective-permute-start(bf16[128,128]{0,1:T(8,128)(2,1)S(1)} %multiply_convert_fusion.6), channel_id=1, source_target_pairs={{4,0},{0,1},{5,2},{1,3},{6,4},{2,5},{7,6},{3,7},{12,8},{8,9},{13,1... | collective-permute-start | bytes 98312 | tf_op jit(solution)/shard_map/ppermute | solution.py:180
  126.3 5.4 %collective-permute-start.5 = (bf16[128,128]{0,1:T(8,128)(2,1)S(1)}, bf16[128,128]{0,1:T(8,128)(2,1)S(1)}, u32[]{:S(2)}, u32[]{:S(2)}) collective-permute-start(bf16[128,128]{0,1:T(8,128)(2,1)S(1)} %multiply_convert_fusion.6), channel_id=1, source_target_pairs={{0,0},{4,1},{1,2},{5,3},{2,4},{6,5},{3,6},{7,7},{8,8},{12,9},{9,10... | collective-permute-start | bytes 98312 | tf_op jit(solution)/shard_map/ppermute | solution.py:179
  132.6 12.2 %all-to-all-start.2 = ((bf16[4,264,128]{2,1,0:T(8,128)(2,1)}), bf16[4,264,128]{2,1,0:T(8,128)(2,1)S(1)}, u32[]{:S(2)}, u32[]{:S(2)}) async-start(bf16[4,264,128]{2,1,0:T(8,128)(2,1)} %pad_maximum_fusion.1), calls=%async_computation.2 | async-start | bytes 540672 | tf_op jit(solution)/shard_map/all_to_all | solution.py:43
  147.2 28.0 %copy-start.2 = (f32[1024]{0:T(1024)S(1)}, f32[1024]{0:T(1024)}, u32[]{:S(2)}) copy-start(f32[1024]{0:T(1024)} %param.21) | copy-start | bytes 12292
  170.9 12.8 %copy-start.4 = (f32[16]{0:T(128)S(1)}, f32[16]{0:T(128)}, u32[]{:S(2)}) copy-start(f32[16]{0:T(128)} %param.20) | copy-start | bytes 196
  170.9 12.8 %all-to-all-start.3 = ((bf16[4,256,128]{2,1,0:T(8,128)(2,1)}), bf16[4,256,128]{2,1,0:T(8,128)(2,1)S(1)}, u32[]{:S(2)}, u32[]{:S(2)}) async-start(bf16[4,256,128]{2,1,0:T(8,128)(2,1)} %copy.123), calls=%async_computation.3 | async-start | bytes 524288 | tf_op jit(solution)/shard_map/all_to_all | solution.py:70
Sparse Core Ops, SparseCore 0:
  10.7 79.6 all-gather.1

commit v14 on v12

--- a/solution.py
+++ b/solution.py
@@ -123,7 +123,22 @@
     totals = lax.psum(lax.psum(powers, CTX), "dp")
     totals, rotated = lax.optimization_barrier((totals, rotated))
     kurtosis = kurtosis_from(totals, row_count)
-    local_panel = jnp.concatenate([x_weight, bc_weight, dt_weight], 1)
+    heads_dev = dt_weight.shape[1]
+    per_group = HEADS // G
+    mp_count = lax.axis_size("mp")
+    owner = [m * heads_dev // per_group for m in range(mp_count)]
+    write_first = [(owner[m] if m % 2 == 0 else G + owner[m], m) for m in range(mp_count)]
+    read_first = [(G + owner[m] if m % 2 == 0 else owner[m], m) for m in range(mp_count)]
+    even = lax.axis_index("mp") % 2 == 0
+
+    def group_pair(value):
+        got_a = lax.ppermute(value, "mp", write_first)
+        got_b = lax.ppermute(value, "mp", read_first)
+        return jnp.where(even, got_a, got_b), jnp.where(even, got_b, got_a)
+
+    write_weight, read_weight = group_pair(bc_weight)
+    write_taps, read_taps = group_pair(conv_bc)
+    local_panel = jnp.concatenate([x_weight, write_weight, read_weight, dt_weight], 1)
     panel = lax.all_gather(local_panel, CTX, axis=0, tiled=True)
     seqs = lax.axis_size("dp")
     share = model_width // seqs
@@ -134,19 +149,12 @@
     incoming = lax.all_to_all(outgoing, "dp", 0, 0)
     x_end = x_weight.shape[1]
     bc_end = x_end + bc_weight.shape[1]
-    side_partials = jnp.einsum(
-        "kti,io->kto", incoming, panel[:, x_end:], preferred_element_type=jnp.float32
-    )
-    side_back = lax.all_to_all(side_partials, "dp", 0, 0)
-    x_partials = jnp.einsum(
-        "kti,io->kto", incoming, panel[:, :x_end], preferred_element_type=jnp.float32
-    )
-    x_back = lax.all_to_all(x_partials, "dp", 0, 0)
-    side_ext = jnp.sum(side_back, 0)
-    x_ext = jnp.sum(x_back, 0)
+    partials = jnp.einsum("kti,io->kto", incoming, panel, preferred_element_type=jnp.float32)
+    both_ext = jnp.sum(lax.all_to_all(partials, "dp", 0, 0), 0)
+    x_end = x_weight.shape[1]
     x_cols = x_end
-    bc_width = bc_end - x_end
-    dt_proj = lax.optimization_barrier(side_ext[rim:, bc_width:].astype(jnp.bfloat16))
+    group_end = x_end + 2 * NS
+    dt_proj = lax.optimization_barrier(both_ext[rim:, group_end:].astype(jnp.bfloat16))
     kernel = conv_x.shape[0] - 1
 
     def causal_conv(rows, taps):
@@ -156,30 +164,12 @@
             total = total + taps[tap_index] * padded[tap_index : tap_index + tok_rows]
         return jax.nn.silu(total).astype(jnp.bfloat16)
 
-    bc_own = causal_conv(side_ext[:, :bc_width], conv_bc)
-    x_conv = causal_conv(x_ext, conv_x)
-    heads_dev = dt_weight.shape[1]
+    x_conv = causal_conv(both_ext[:, :x_end], conv_x)
+    write_here = causal_conv(both_ext[:, x_end : x_end + NS], write_taps).reshape(tok_rows, 1, NS)
+    read_here = causal_conv(both_ext[:, x_end + NS : group_end], read_taps).reshape(tok_rows, 1, NS)
     head_size = x_cols // heads_dev
-    per_group = HEADS // G
     groups_here = max(1, heads_dev // per_group)
     heads_local = heads_dev // groups_here
-    first_group = lax.axis_index("mp") * heads_dev // per_group
-    mp_count = lax.axis_size("mp")
-    if bc_own.shape[1] == NS and mp_count == 2 * G and groups_here == 1:
-        owner = [m * heads_dev // per_group for m in range(mp_count)]
-        odd_first = [(owner[m] if m % 2 == 0 else G + owner[m], m) for m in range(mp_count)]
-        even_first = [(G + owner[m] if m % 2 == 0 else owner[m], m) for m in range(mp_count)]
-        got_a = lax.ppermute(bc_own, "mp", odd_first)
-        got_b = lax.ppermute(bc_own, "mp", even_first)
-        even = lax.axis_index("mp") % 2 == 0
-        write_here = jnp.where(even, got_a, got_b).reshape(tok_rows, 1, NS)
-        read_here = jnp.where(even, got_b, got_a).reshape(tok_rows, 1, NS)
-    else:
-        group_all = lax.all_gather(bc_own, "mp", axis=1, tiled=True)
-        write_all = group_all[:, : G * NS].reshape(tok_rows, G, NS)
-        read_all = group_all[:, G * NS :].reshape(tok_rows, G, NS)
-        write_here = lax.dynamic_slice_in_dim(write_all, first_group, groups_here, 1)
-        read_here = lax.dynamic_slice_in_dim(read_all, first_group, groups_here, 1)
     step_size = jax.nn.softplus(dt_proj.astype(jnp.float32) + dt_bias)
     decay_rate = step_size * jnp.exp(a_log)
     cumulative = jnp.cumsum(decay_rate, 0)

time: 187 us -> 195 us (1.043)
  blocking collectives: 64.4 us -> 77.8 us
  starting transfers between devices: 29.4 us -> 21.7 us
  waiting for transfers between devices: 47.2 us -> 50.4 us
  other arithmetic: 6.03 us -> 8.05 us
    all_to_all x0 -> x1, blocking collectives: none -> 14.4 us  [shards(): incoming = lax.all_to_all(outgoing, 'dp', 0, 0)]
    all_to_all x3 -> x1, starting transfers between devices: 17.7 us -> 4.88 us  [shards(): both_ext = jnp.sum(lax.all_to_all(partials, 'dp', 0, 0), 0)]
    ppermute x2 -> x4, waiting for transfers between devices: 0.01 us -> 6.93 us  [the longest x2 6.92 us: group_pair(): got_b = lax.ppermute(value, 'mp', read_first)]
    all_to_all x3 -> x1, waiting for transfers between devices: 25.6 us -> 18.9 us  [shards(): both_ext = jnp.sum(lax.all_to_all(partials, 'dp', 0, 0), 0)]
    ppermute x2 -> x4, starting transfers between devices: 2.58 us -> 8.09 us  [the longest x2 6.05 us: group_pair(): got_b = lax.ppermute(value, 'mp', read_first)]
    dot_general x2 -> x1, matrix products: 6.62 us -> 5.33 us  [shards(): jnp.einsum('kti,io->kto', incoming, panel, preferred_element_type=jnp.flo...]
  transfers between devices with their start and end apart: 9 -> 9, of which waited for: 7 -> 7; matrix products, arithmetic and copies ran while one was open for 9% -> 5% of each run, Pallas kernels for 0% -> 0%
where the time goes in v14:
time: 195 us; the launch traced here: 192 us
  blocking collectives  77.8 us (40%)
  waiting for transfers between devices  50.4 us (26%)
  starting transfers between devices  21.7 us (11%)
  between operations  14.5 us (7%)
  matrix products  13.1 us (7%)
  other arithmetic  8.05 us (4%)
  local copies, waits for them, and re-layouts  6.25 us (3%)
    psum x2, blocking collectives, shards(): totals = lax.psum(lax.psum(powers, CTX), 'dp')  44.7 us
    all_to_all x1, waiting for transfers between devices, shards(): both_ext = jnp.sum(lax.all_to_all(partials, 'dp', 0, 0), 0)  18.9 us
    all_gather x1, blocking collectives, entering(): lax.all_gather(summary.astype(jnp.bfloat16), 'ch').astype(jnp.float32)  18.7 us
    all_to_all x1, blocking collectives, shards(): incoming = lax.all_to_all(outgoing, 'dp', 0, 0)  14.4 us
    all_gather x1, waiting for transfers between devices, shards(): panel = lax.all_gather(local_panel, CTX, axis=0, tiled=True)  9.03 us
    all_to_all x1, waiting for transfers between devices, entering(): incoming = lax.all_to_all(outgoing, 'cl', 0, 0).astype(jnp.float32)  7.23 us
    ppermute x2, waiting for transfers between devices, group_pair(): got_b = lax.ppermute(value, 'mp', read_first)  6.92 us
    ppermute x2, starting transfers between devices, group_pair(): got_b = lax.ppermute(value, 'mp', read_first)  6.05 us
  transfers between devices with their start and end apart: 9, of which 7 were waited for; matrix products, arithmetic and copies ran while one was open for 5% of the time, Pallas kernels for 0%

profile of v14, /device:TPU:6, one launch (start us, length us, event | category | flops | bytes accessed | tf_op | source)
XLA Modules:
  0.0 191.8 jit_solution(17162700415022455261)
XLA Ops:
  7.2 1.4 collective-permute-start.1
  8.6 4.1 %collective-permute-start.2 = (bf16[64,128]{1,0:T(8,128)(2,1)}, bf16[64,128]{1,0:T(8,128)(2,1)S(1)}, u32[]{:S(2)}, u32[]{:S(2)}) collective-permute-start(bf16[64,128]{1,0:T(8,128)(2,1)} %param.14), channel_id=1, source_target_pairs={{4,0},{0,1},{5,2},{1,3},{6,4},{2,5},{7,6},{3,7},{12,8},{8,9},{13,1... | collective-permute-start | bytes 49160 | tf_op jit(solution)/shard_map/ppermute | solution.py:136
  13.5 2.6 %collective-permute-done.2 = bf16[64,128]{1,0:T(8,128)(2,1)S(1)} collective-permute-done((bf16[64,128]{1,0:T(8,128)(2,1)}, bf16[64,128]{1,0:T(8,128)(2,1)S(1)}, u32[]{:S(2)}, u32[]{:S(2)}) %collective-permute-start.2) | collective-permute-done | bytes 16416 | tf_op jit(solution)/shard_map/ppermute | solution.py:136
  16.2 1.6 pad_maximum_fusion.2
  17.8 1.6 copy.100
  20.3 3.3 %multiply_convert_fusion = bf16[128,64,64]{0,2,1:T(8,128)(2,1)S(1)} fusion(f32[128,64,64]{0,1,2:T(8,128)S(1)} %convolution_bitcast_fusion), kind=kOutput, calls=%fused_computation.4 | convolution fusion | flops 403791872 | bytes 3145728 | tf_op jit(solution)/shard_map/tcb,bd->tcd/dot_general | solution.py:106
  24.0 37.2 %psum.14 = f32[4,512]{1,0:T(4,128)S(1)} all-reduce(f32[4,512]{1,0:T(4,128)S(1)} %pad_maximum_fusion.3), channel_id=1, replica_groups=mesh['dp'=4,'ch'=4,'cl'=4,'mp'=8] {'ch','cl'}, use_global_device_ids=true, to_apply=%region_4.0 | all-reduce | flops 2048 | bytes 16384 | tf_op jit(solution)/shard_map/psum | solution.py:123
  61.1 7.6 %psum.15 = f32[4,512]{1,0:T(4,128)S(1)} all-reduce(f32[4,512]{1,0:T(4,128)S(1)} %psum.14), channel_id=1, replica_groups=mesh['dp'=4,'ch'=4,'cl'=4,'mp'=8] {'dp'}, use_global_device_ids=true, to_apply=%region_5.0 | all-reduce | flops 2048 | bytes 16384 | tf_op jit(solution)/shard_map/psum | solution.py:123
  69.3 1.6 collective-permute-start
  70.9 3.1 %collective-permute-done = bf16[8,4096]{1,0:T(8,128)(2,1)S(1)} collective-permute-done((bf16[8,4096]{1,0:T(8,128)(2,1)S(1)}, bf16[8,4096]{1,0:T(8,128)(2,1)S(1)}, u32[]{:S(2)}, u32[]{:S(2)}) %collective-permute-start) | collective-permute-done | bytes 65568 | tf_op jit(solution)/shard_map/ppermute | solution.py:18
  74.2 14.4 %all_to_all.20 = bf16[4,136,1024]{2,1,0:T(8,128)(2,1)S(1)} all-to-all(bf16[4,136,1024]{2,1,0:T(8,128)(2,1)S(1)} %bitcast.119), channel_id=1, replica_groups=mesh['dp'=4,'ch'=4,'cl'=4,'mp'=8] {'dp'}, dimensions={0} | all-to-all | bytes 2228224 | tf_op jit(solution)/shard_map/all_to_all | solution.py:149
  88.6 9.0 %all-gather.2.cloned.1.call-done = bf16[1024,1296]{1,0:T(8,128)(2,1)} async-done(((bf16[64,1296]{1,0:T(8,128)(2,1)}), bf16[1024,1296]{1,0:T(8,128)(2,1)}) %all-gather.2.cloned.1.call-update) | async-done | bytes 2654224 | tf_op jit(solution)/shard_map/all_gather | solution.py:142
  97.7 5.3 %fusion = f32[4,136,1296]{2,1,0:T(8,128)} fusion(bf16[4,136,1024]{2,1,0:T(8,128)(2,1)S(1)} %all_to_all.20, bf16[1024,1296]{1,0:T(8,128)(2,1)} %all-gather.2.cloned.1.call-done), kind=kOutput, calls=%fused_computation | convolution fusion | flops 1443889152 | bytes 6588416 | tf_op jit(solution)/shard_map/kti,io->kto/dot_general | solution.py:152
  103.0 4.9 %all-to-all-start.1 = ((f32[4,136,1296]{2,1,0:T(8,128)}), f32[4,136,1296]{2,1,0:T(8,128)S(1)}, u32[]{:S(2)}, u32[]{:S(2)}) async-start(f32[4,136,1296]{2,1,0:T(8,128)} %fusion), calls=%async_computation.1 | async-start | bytes 6127616 | tf_op jit(solution)/shard_map/all_to_all | solution.py:153
  107.9 1.9 collective-permute-start.3
  110.6 4.3 %collective-permute-done.3 = f32[5,128]{1,0:T(8,128)S(1)} collective-permute-done((f32[5,128]{1,0:T(8,128)S(1)}, f32[5,128]{1,0:T(8,128)S(1)}, u32[]{:S(2)}, u32[]{:S(2)}) %collective-permute-start.3) | collective-permute-done | bytes 2592 | tf_op jit(solution)/shard_map/ppermute | solution.py:136
  114.9 18.9 %all-to-all-done.1 = f32[4,136,1296]{2,1,0:T(8,128)S(1)} async-done(((f32[4,136,1296]{2,1,0:T(8,128)}), f32[4,136,1296]{2,1,0:T(8,128)S(1)}, u32[]{:S(2)}, u32[]{:S(2)}) %all-to-all-start.1) | async-done | bytes 2820128 | tf_op jit(solution)/shard_map/all_to_all | solution.py:153
  134.9 1.2 multiply_convert_fusion.4
  137.4 3.4 %all-to-all-start.2 = ((bf16[4,264,128]{2,1,0:T(8,128)(2,1)}), bf16[4,264,128]{2,1,0:T(8,128)(2,1)S(1)}, u32[]{:S(2)}, u32[]{:S(2)}) async-start(bf16[4,264,128]{2,1,0:T(8,128)(2,1)} %pad_maximum_fusion.1), calls=%async_computation.2 | async-start | bytes 540672 | tf_op jit(solution)/shard_map/all_to_all | solution.py:43
  141.8 7.2 %all-to-all-done.2 = bf16[4,264,128]{2,1,0:T(8,128)(2,1)S(1)} async-done(((bf16[4,264,128]{2,1,0:T(8,128)(2,1)}), bf16[4,264,128]{2,1,0:T(8,128)(2,1)S(1)}, u32[]{:S(2)}, u32[]{:S(2)}) %all-to-all-start.2) | async-done | bytes 270368 | tf_op jit(solution)/shard_map/all_to_all | solution.py:43
  149.6 1.2 convolution_bitcast_fusion.1
  151.4 18.7 %all_gather.8 = bf16[4,264,128]{2,1,0:T(8,128)(2,1)S(1)} all-gather(bf16[1,264,128]{2,1,0:T(8,128)(2,1)S(1)} %copy.118), channel_id=1, replica_groups=mesh['dp'=4,'ch'=4,'cl'=4,'mp'=8] {'ch'}, dimensions={0}, use_global_device_ids=true | all-gather | bytes 337920 | tf_op jit(solution)/shard_map/all_gather | solution.py:60
  172.7 3.6 %all-to-all-start.3 = ((bf16[4,256,128]{2,1,0:T(8,128)(2,1)}), bf16[4,256,128]{2,1,0:T(8,128)(2,1)S(1)}, u32[]{:S(2)}, u32[]{:S(2)}) async-start(bf16[4,256,128]{2,1,0:T(8,128)(2,1)} %copy.119), calls=%async_computation.3 | async-start | bytes 524288 | tf_op jit(solution)/shard_map/all_to_all | solution.py:70
  177.9 5.2 %all-to-all-done.3 = bf16[4,256,128]{2,1,0:T(8,128)(2,1)S(1)} async-done(((bf16[4,256,128]{2,1,0:T(8,128)(2,1)}), bf16[4,256,128]{2,1,0:T(8,128)(2,1)S(1)}, u32[]{:S(2)}, u32[]{:S(2)}) %all-to-all-start.3) | async-done | bytes 262176 | tf_op jit(solution)/shard_map/all_to_all | solution.py:70
  (90 shorter events, 13.8 us)
Async XLA Ops:
  7.2 90.5 %all-gather.2.cloned.1.call-start = ((), (), s32[]{:S(2)}) async-start(), calls=%async_computation.4 | async-start | bytes 3063808 | tf_op jit(solution)/shard_map/all_gather | solution.py:142
  7.2 6.3 %collective-permute-start.1 = (bf16[64,128]{1,0:T(8,128)(2,1)}, bf16[64,128]{1,0:T(8,128)(2,1)S(1)}, u32[]{:S(2)}, u32[]{:S(2)}) collective-permute-start(bf16[64,128]{1,0:T(8,128)(2,1)} %param.14), channel_id=1, source_target_pairs={{0,0},{4,1},{1,2},{5,3},{2,4},{6,5},{3,6},{7,7},{8,8},{12,9},{9,10... | collective-permute-start | bytes 49160 | tf_op jit(solution)/shard_map/ppermute | solution.py:135
  8.6 7.6 %collective-permute-start.2 = (bf16[64,128]{1,0:T(8,128)(2,1)}, bf16[64,128]{1,0:T(8,128)(2,1)S(1)}, u32[]{:S(2)}, u32[]{:S(2)}) collective-permute-start(bf16[64,128]{1,0:T(8,128)(2,1)} %param.14), channel_id=1, source_target_pairs={{4,0},{0,1},{5,2},{1,3},{6,4},{2,5},{7,6},{3,7},{12,8},{8,9},{13,1... | collective-permute-start | bytes 49160 | tf_op jit(solution)/shard_map/ppermute | solution.py:136
  69.3 4.8 %collective-permute-start = (bf16[8,4096]{1,0:T(8,128)(2,1)S(1)}, bf16[8,4096]{1,0:T(8,128)(2,1)S(1)}, u32[]{:S(2)}, u32[]{:S(2)}) collective-permute-start(bf16[8,4096]{1,0:T(8,128)(2,1)S(1)} %slice.242), channel_id=1, source_target_pairs={{0,8},{8,16},{16,24},{24,32},{32,40},{40,48},{48,56},{56,64},{64,7... | collective-permute-start | bytes 196616 | tf_op jit(solution)/shard_map/ppermute | solution.py:18
  103.0 4.9 %copy-start.3 = (f32[5,128]{1,0:T(8,128)S(1)}, f32[5,128]{1,0:T(8,128)}, u32[]{:S(2)}) copy-start(f32[5,128]{1,0:T(8,128)} %param.17) | copy-start | bytes 7684
  103.0 7.5 %copy-start = (f32[5,1024]{1,0:T(8,128)S(1)}, f32[5,1024]{1,0:T(8,128)}, u32[]{:S(2)}) copy-start(f32[5,1024]{1,0:T(8,128)} %param.16) | copy-start | bytes 61444
  103.0 7.6 %copy-start.4 = (f32[16]{0:T(128)S(1)}, f32[16]{0:T(128)}, u32[]{:S(2)}) copy-start(f32[16]{0:T(128)} %param.19) | copy-start | bytes 196
  103.0 30.8 %all-to-all-start.1 = ((f32[4,136,1296]{2,1,0:T(8,128)}), f32[4,136,1296]{2,1,0:T(8,128)S(1)}, u32[]{:S(2)}, u32[]{:S(2)}) async-start(f32[4,136,1296]{2,1,0:T(8,128)} %fusion), calls=%async_computation.1 | async-start | bytes 6127616 | tf_op jit(solution)/shard_map/all_to_all | solution.py:153
  107.9 7.0 %collective-permute-start.3 = (f32[5,128]{1,0:T(8,128)S(1)}, f32[5,128]{1,0:T(8,128)S(1)}, u32[]{:S(2)}, u32[]{:S(2)}) collective-permute-start(f32[5,128]{1,0:T(8,128)S(1)} %copy-done.3), channel_id=1, source_target_pairs={{4,0},{0,1},{5,2},{1,3},{6,4},{2,5},{7,6},{3,7},{12,8},{8,9},{13,1... | collective-permute-start | bytes 7688 | tf_op jit(solution)/shard_map/ppermute | solution.py:136
  109.8 5.1 %collective-permute-start.4 = (f32[5,128]{1,0:T(8,128)S(1)}, f32[5,128]{1,0:T(8,128)S(1)}, u32[]{:S(2)}, u32[]{:S(2)}) collective-permute-start(f32[5,128]{1,0:T(8,128)S(1)} %copy-done.3), channel_id=1, source_target_pairs={{0,0},{4,1},{1,2},{5,3},{2,4},{6,5},{3,6},{7,7},{8,8},{12,9},{9,10... | collective-permute-start | bytes 7688 | tf_op jit(solution)/shard_map/ppermute | solution.py:135
  114.9 19.4 %copy-start.2 = (f32[16]{0:T(128)S(1)}, f32[16]{0:T(128)}, u32[]{:S(2)}) copy-start(f32[16]{0:T(128)} %param.18) | copy-start | bytes 196
  134.3 6.7 %copy-start.1 = (f32[1024]{0:T(1024)S(1)}, f32[1024]{0:T(1024)}, u32[]{:S(2)}) copy-start(f32[1024]{0:T(1024)} %param.21) | copy-start | bytes 12292
  137.4 11.6 %all-to-all-start.2 = ((bf16[4,264,128]{2,1,0:T(8,128)(2,1)}), bf16[4,264,128]{2,1,0:T(8,128)(2,1)S(1)}, u32[]{:S(2)}, u32[]{:S(2)}) async-start(bf16[4,264,128]{2,1,0:T(8,128)(2,1)} %pad_maximum_fusion.1), calls=%async_computation.2 | async-start | bytes 540672 | tf_op jit(solution)/shard_map/all_to_all | solution.py:43
  171.6 11.7 %copy-start.5 = (f32[16]{0:T(128)S(1)}, f32[16]{0:T(128)}, u32[]{:S(2)}) copy-start(f32[16]{0:T(128)} %param.20) | copy-start | bytes 196
  172.7 10.4 %all-to-all-start.3 = ((bf16[4,256,128]{2,1,0:T(8,128)(2,1)}), bf16[4,256,128]{2,1,0:T(8,128)(2,1)S(1)}, u32[]{:S(2)}, u32[]{:S(2)}) async-start(bf16[4,256,128]{2,1,0:T(8,128)(2,1)} %copy.119), calls=%async_computation.3 | async-start | bytes 524288 | tf_op jit(solution)/shard_map/all_to_all | solution.py:70
Sparse Core Ops, SparseCore 0:
  17.9 79.7 all-gather.1

commit v15 on v12

--- a/solution.py
+++ b/solution.py
@@ -226,7 +226,7 @@
 
 def solution(mesh):
     grid = mesh.devices
-    quad = 4 if grid.shape[1] % 4 == 0 else 1
+    quad = 8 if grid.shape[1] % 8 == 0 else 1
     split = jax.sharding.Mesh(
         grid.reshape(grid.shape[0], grid.shape[1] // quad, quad, grid.shape[2]),
         ("dp", "ch", "cl", "mp"),

time: 187 us -> 197 us (1.053)
  the two profiles are of different devices: /device:TPU:6 before, /device:TPU:24 now
where the time goes in v15:
time: 197 us; the launch traced here: 196 us
  waiting for transfers between devices  63.7 us (32%)
  blocking collectives  61.6 us (31%)
  starting transfers between devices  30 us (15%)
  between operations  14.5 us (7%)
  matrix products  13.7 us (7%)
  local copies, waits for them, and re-layouts  7.25 us (4%)
  other arithmetic  5.79 us (3%)
    psum x2, blocking collectives, shards(): totals = lax.psum(lax.psum(powers, CTX), 'dp')  47.8 us
    all_gather x1, blocking collectives, entering(): lax.all_gather(summary.astype(jnp.bfloat16), 'ch').astype(jnp.float32)  13.8 us
    all_to_all x1, waiting for transfers between devices, entering(): incoming = lax.all_to_all(outgoing, 'cl', 0, 0).astype(jnp.float32)  13.7 us
    all_to_all x1, waiting for transfers between devices, shards(): x_back = lax.all_to_all(x_partials, 'dp', 0, 0)  12.1 us
    all_to_all x1, waiting for transfers between devices, entering(): returned = lax.all_to_all(carried.astype(jnp.bfloat16), 'cl', 0, 0)  11.3 us
    all_to_all x1, waiting for transfers between devices, shards(): incoming = lax.all_to_all(outgoing, 'dp', 0, 0)  11.2 us
    all_gather x1, waiting for transfers between devices, shards(): panel = lax.all_gather(local_panel, CTX, axis=0, tiled=True)  6.51 us
    all_to_all x1, waiting for transfers between devices, shards(): side_back = lax.all_to_all(side_partials, 'dp', 0, 0)  6.4 us
  transfers between devices with their start and end apart: 9, of which 7 were waited for; matrix products, arithmetic and copies ran while one was open for 8% of the time, Pallas kernels for 0%

profile of v15, /device:TPU:24, one launch (start us, length us, event | category | flops | bytes accessed | tf_op | source)
XLA Modules:
  0.0 196.4 jit_solution(12487934375544864749)
XLA Ops:
  8.0 1.6 pad_maximum_fusion.2
  9.6 1.6 copy.129
  12.1 3.3 %multiply_convert_fusion = bf16[128,64,64]{0,2,1:T(8,128)(2,1)S(1)} fusion(f32[128,64,64]{0,1,2:T(8,128)S(1)} %convolution_bitcast_fusion), kind=kOutput, calls=%fused_computation.4 | convolution fusion | flops 403791872 | bytes 3145728 | tf_op jit(solution)/shard_map/tcb,bd->tcd/dot_general | solution.py:106
  15.8 37.1 %psum.14 = f32[4,512]{1,0:T(4,128)S(1)} all-reduce(f32[4,512]{1,0:T(4,128)S(1)} %pad_maximum_fusion.3), channel_id=1, replica_groups=mesh['dp'=4,'ch'=2,'cl'=8,'mp'=8] {'ch','cl'}, use_global_device_ids=true, to_apply=%region_4.0 | all-reduce | flops 2048 | bytes 16384 | tf_op jit(solution)/shard_map/psum | solution.py:123
  53.0 10.6 %psum.15 = f32[4,512]{1,0:T(4,128)S(1)} all-reduce(f32[4,512]{1,0:T(4,128)S(1)} %psum.14), channel_id=1, replica_groups=mesh['dp'=4,'ch'=2,'cl'=8,'mp'=8] {'dp'}, use_global_device_ids=true, to_apply=%region_5.0 | all-reduce | flops 2048 | bytes 16384 | tf_op jit(solution)/shard_map/psum | solution.py:123
  64.2 1.6 collective-permute-start
  65.7 2.4 %collective-permute-done = bf16[8,4096]{1,0:T(8,128)(2,1)S(1)} collective-permute-done((bf16[8,4096]{1,0:T(8,128)(2,1)S(1)}, bf16[8,4096]{1,0:T(8,128)(2,1)S(1)}, u32[]{:S(2)}, u32[]{:S(2)}) %collective-permute-start) | collective-permute-done | bytes 65568 | tf_op jit(solution)/shard_map/ppermute | solution.py:18
  68.3 1.1 copy.176
  69.4 3.5 %all-to-all-start = ((bf16[4,136,1024]{2,1,0:T(8,128)(2,1)}), bf16[4,136,1024]{2,1,0:T(8,128)(2,1)S(1)}, u32[]{:S(2)}, u32[]{:S(2)}) async-start(bf16[4,136,1024]{2,1,0:T(8,128)(2,1)} %bitcast.105), calls=%async_computation | async-start | bytes 2228224 | tf_op jit(solution)/shard_map/all_to_all | solution.py:134
  72.9 11.2 %all-to-all-done = bf16[4,136,1024]{2,1,0:T(8,128)(2,1)S(1)} async-done(((bf16[4,136,1024]{2,1,0:T(8,128)(2,1)}), bf16[4,136,1024]{2,1,0:T(8,128)(2,1)S(1)}, u32[]{:S(2)}, u32[]{:S(2)}) %all-to-all-start) | async-done | bytes 1114144 | tf_op jit(solution)/shard_map/all_to_all | solution.py:134
  84.1 6.5 %all-gather.2.cloned.1.call-done = bf16[1024,1168]{1,0:T(8,128)(2,1)} async-done(((bf16[64,1168]{1,0:T(8,128)(2,1)}), bf16[1024,1168]{1,0:T(8,128)(2,1)}) %all-gather.2.cloned.1.call-update) | async-done | bytes 2392080 | tf_op jit(solution)/shard_map/all_gather | solution.py:127
  90.6 2.3 %fusion.10 = f32[4,136,144]{2,1,0:T(8,128)} fusion(bf16[4,136,1024]{2,1,0:T(8,128)(2,1)S(1)} %all-to-all-done, bf16[1024,1168]{1,0:T(8,128)(2,1)} %all-gather.2.cloned.1.call-done), kind=kOutput, calls=%fused_computation.20 | convolution fusion | flops 160432128 | bytes 1951744 | tf_op jit(solution)/shard_map/kti,io->kto/dot_general | solution.py:137
  92.9 4.1 %all-to-all-start.2 = ((f32[4,136,144]{2,1,0:T(8,128)}), f32[4,136,144]{2,1,0:T(8,128)S(1)}, u32[]{:S(2)}, u32[]{:S(2)}) async-start(f32[4,136,144]{2,1,0:T(8,128)} %fusion.10), calls=%async_computation.2 | async-start | bytes 1114112 | tf_op jit(solution)/shard_map/all_to_all | solution.py:140
  97.1 4.3 %fusion = f32[4,136,1024]{2,1,0:T(8,128)} fusion(bf16[4,136,1024]{2,1,0:T(8,128)(2,1)S(1)} %all-to-all-done, bf16[1024,1168]{1,0:T(8,128)(2,1)} %all-gather.2.cloned.1.call-done), kind=kOutput, calls=%fused_computation.1 | convolution fusion | flops 1140850688 | bytes 5439488 | tf_op jit(solution)/shard_map/kti,io->kto/dot_general | solution.py:141
  101.4 6.4 %all-to-all-done.2 = f32[4,136,144]{2,1,0:T(8,128)S(1)} async-done(((f32[4,136,144]{2,1,0:T(8,128)}), f32[4,136,144]{2,1,0:T(8,128)S(1)}, u32[]{:S(2)}, u32[]{:S(2)}) %all-to-all-start.2) | async-done | bytes 313376 | tf_op jit(solution)/shard_map/all_to_all | solution.py:140
  107.8 3.6 %all-to-all-start.1 = ((f32[4,136,1024]{2,1,0:T(8,128)}), f32[4,136,1024]{2,1,0:T(8,128)S(1)}, u32[]{:S(2)}, u32[]{:S(2)}) async-start(f32[4,136,1024]{2,1,0:T(8,128)} %fusion), calls=%async_computation.1 | async-start | bytes 4456448 | tf_op jit(solution)/shard_map/all_to_all | solution.py:144
  111.9 2.7 %collective-permute-start.1 = (bf16[128,128]{0,1:T(8,128)(2,1)S(1)}, bf16[128,128]{0,1:T(8,128)(2,1)S(1)}, u32[]{:S(2)}, u32[]{:S(2)}) collective-permute-start(bf16[128,128]{0,1:T(8,128)(2,1)S(1)} %multiply_convert_fusion.6), channel_id=1, source_target_pairs={{4,0},{0,1},{5,2},{1,3},{6,4},{2,5},{7,6},{3,7},{12,8},{8,9},{13,1... | collective-permute-start | bytes 98312 | tf_op jit(solution)/shard_map/ppermute | solution.py:173
  114.6 1.9 collective-permute-start.2
  117.1 12.1 %all-to-all-done.1 = f32[4,136,1024]{2,1,0:T(8,128)S(1)} async-done(((f32[4,136,1024]{2,1,0:T(8,128)}), f32[4,136,1024]{2,1,0:T(8,128)S(1)}, u32[]{:S(2)}, u32[]{:S(2)}) %all-to-all-start.1) | async-done | bytes 2228256 | tf_op jit(solution)/shard_map/all_to_all | solution.py:144
  131.0 6.2 %all-to-all-start.3 = ((bf16[8,136,128]{2,1,0:T(8,128)(2,1)}), bf16[8,136,128]{2,1,0:T(8,128)(2,1)S(1)}, u32[]{:S(2)}, u32[]{:S(2)}) async-start(bf16[8,136,128]{2,1,0:T(8,128)(2,1)} %pad_maximum_fusion.1), calls=%async_computation.3 | async-start | bytes 557056 | tf_op jit(solution)/shard_map/all_to_all | solution.py:43
  137.5 13.7 %all-to-all-done.3 = bf16[8,136,128]{2,1,0:T(8,128)(2,1)S(1)} async-done(((bf16[8,136,128]{2,1,0:T(8,128)(2,1)}), bf16[8,136,128]{2,1,0:T(8,128)(2,1)S(1)}, u32[]{:S(2)}, u32[]{:S(2)}) %all-to-all-start.3) | async-done | bytes 278560 | tf_op jit(solution)/shard_map/all_to_all | solution.py:43
  153.2 13.8 %all_gather.8 = bf16[2,136,128]{2,1,0:T(8,128)(2,1)S(1)} all-gather(bf16[1,136,128]{2,1,0:T(8,128)(2,1)S(1)} %copy.150), channel_id=1, replica_groups=mesh['dp'=4,'ch'=2,'cl'=8,'mp'=8] {'ch'}, dimensions={0}, use_global_device_ids=true | all-gather | bytes 104448 | tf_op jit(solution)/shard_map/all_gather | solution.py:60
  168.9 6.3 %all-to-all-start.4 = ((bf16[8,128,128]{2,1,0:T(8,128)(2,1)}), bf16[8,128,128]{2,1,0:T(8,128)(2,1)S(1)}, u32[]{:S(2)}, u32[]{:S(2)}) async-start(bf16[8,128,128]{2,1,0:T(8,128)(2,1)} %copy.151), calls=%async_computation.4 | async-start | bytes 524288 | tf_op jit(solution)/shard_map/all_to_all | solution.py:70
  176.9 11.3 %all-to-all-done.4 = bf16[8,128,128]{2,1,0:T(8,128)(2,1)S(1)} async-done(((bf16[8,128,128]{2,1,0:T(8,128)(2,1)}), bf16[8,128,128]{2,1,0:T(8,128)(2,1)S(1)}, u32[]{:S(2)}, u32[]{:S(2)}) %all-to-all-start.4) | async-done | bytes 262176 | tf_op jit(solution)/shard_map/all_to_all | solution.py:70
  (90 shorter events, 12.5 us)
Async XLA Ops:
  7.2 83.5 %all-gather.2.cloned.1.call-start = ((), (), s32[]{:S(2)}) async-start(), calls=%async_computation.5 | async-start | bytes 2785280 | tf_op jit(solution)/shard_map/all_gather | solution.py:127
  64.2 4.0 %collective-permute-start = (bf16[8,4096]{1,0:T(8,128)(2,1)S(1)}, bf16[8,4096]{1,0:T(8,128)(2,1)S(1)}, u32[]{:S(2)}, u32[]{:S(2)}) collective-permute-start(bf16[8,4096]{1,0:T(8,128)(2,1)S(1)} %slice.197), channel_id=1, source_target_pairs={{0,8},{8,16},{16,24},{24,32},{32,40},{40,48},{48,56},{56,64},{64,7... | collective-permute-start | bytes 196616 | tf_op jit(solution)/shard_map/ppermute | solution.py:18
  68.3 4.6 %copy-start.5 = (f32[16]{0:T(128)S(1)}, f32[16]{0:T(128)}, u32[]{:S(2)}) copy-start(f32[16]{0:T(128)} %param.19) | copy-start | bytes 196
  69.4 14.7 %all-to-all-start = ((bf16[4,136,1024]{2,1,0:T(8,128)(2,1)}), bf16[4,136,1024]{2,1,0:T(8,128)(2,1)S(1)}, u32[]{:S(2)}, u32[]{:S(2)}) async-start(bf16[4,136,1024]{2,1,0:T(8,128)(2,1)} %bitcast.105), calls=%async_computation | async-start | bytes 2228224 | tf_op jit(solution)/shard_map/all_to_all | solution.py:134
  92.9 14.8 %all-to-all-start.2 = ((f32[4,136,144]{2,1,0:T(8,128)}), f32[4,136,144]{2,1,0:T(8,128)S(1)}, u32[]{:S(2)}, u32[]{:S(2)}) async-start(f32[4,136,144]{2,1,0:T(8,128)} %fusion.10), calls=%async_computation.2 | async-start | bytes 1114112 | tf_op jit(solution)/shard_map/all_to_all | solution.py:140
  101.3 10.0 %copy-start.3 = (f32[5,128]{1,0:T(8,128)S(1)}, f32[5,128]{1,0:T(8,128)}, u32[]{:S(2)}) copy-start(f32[5,128]{1,0:T(8,128)} %param.17) | copy-start | bytes 7684
  101.4 10.1 %copy-start = (f32[5,1024]{1,0:T(8,128)S(1)}, f32[5,1024]{1,0:T(8,128)}, u32[]{:S(2)}) copy-start(f32[5,1024]{1,0:T(8,128)} %param.16) | copy-start | bytes 61444
  101.4 15.2 %copy-start.2 = (f32[16]{0:T(128)S(1)}, f32[16]{0:T(128)}, u32[]{:S(2)}) copy-start(f32[16]{0:T(128)} %param.18) | copy-start | bytes 196
  107.8 21.4 %all-to-all-start.1 = ((f32[4,136,1024]{2,1,0:T(8,128)}), f32[4,136,1024]{2,1,0:T(8,128)S(1)}, u32[]{:S(2)}, u32[]{:S(2)}) async-start(f32[4,136,1024]{2,1,0:T(8,128)} %fusion), calls=%async_computation.1 | async-start | bytes 4456448 | tf_op jit(solution)/shard_map/all_to_all | solution.py:144
  111.9 18.1 %collective-permute-start.1 = (bf16[128,128]{0,1:T(8,128)(2,1)S(1)}, bf16[128,128]{0,1:T(8,128)(2,1)S(1)}, u32[]{:S(2)}, u32[]{:S(2)}) collective-permute-start(bf16[128,128]{0,1:T(8,128)(2,1)S(1)} %multiply_convert_fusion.6), channel_id=1, source_target_pairs={{4,0},{0,1},{5,2},{1,3},{6,4},{2,5},{7,6},{3,7},{12,8},{8,9},{13,1... | collective-permute-start | bytes 98312 | tf_op jit(solution)/shard_map/ppermute | solution.py:173
  114.6 15.4 %collective-permute-start.2 = (bf16[128,128]{0,1:T(8,128)(2,1)S(1)}, bf16[128,128]{0,1:T(8,128)(2,1)S(1)}, u32[]{:S(2)}, u32[]{:S(2)}) collective-permute-start(bf16[128,128]{0,1:T(8,128)(2,1)S(1)} %multiply_convert_fusion.6), channel_id=1, source_target_pairs={{0,0},{4,1},{1,2},{5,3},{2,4},{6,5},{3,6},{7,7},{8,8},{12,9},{9,10... | collective-permute-start | bytes 98312 | tf_op jit(solution)/shard_map/ppermute | solution.py:172
  131.0 20.2 %all-to-all-start.3 = ((bf16[8,136,128]{2,1,0:T(8,128)(2,1)}), bf16[8,136,128]{2,1,0:T(8,128)(2,1)S(1)}, u32[]{:S(2)}, u32[]{:S(2)}) async-start(bf16[8,136,128]{2,1,0:T(8,128)(2,1)} %pad_maximum_fusion.1), calls=%async_computation.3 | async-start | bytes 557056 | tf_op jit(solution)/shard_map/all_to_all | solution.py:43
  151.9 23.3 %copy-start.1 = (f32[1024]{0:T(1024)S(1)}, f32[1024]{0:T(1024)}, u32[]{:S(2)}) copy-start(f32[1024]{0:T(1024)} %param.21) | copy-start | bytes 12292
  168.9 19.4 %copy-start.4 = (f32[16]{0:T(128)S(1)}, f32[16]{0:T(128)}, u32[]{:S(2)}) copy-start(f32[16]{0:T(128)} %param.20) | copy-start | bytes 196
  168.9 19.4 %all-to-all-start.4 = ((bf16[8,128,128]{2,1,0:T(8,128)(2,1)}), bf16[8,128,128]{2,1,0:T(8,128)(2,1)S(1)}, u32[]{:S(2)}, u32[]{:S(2)}) async-start(bf16[8,128,128]{2,1,0:T(8,128)(2,1)} %copy.151), calls=%async_computation.4 | async-start | bytes 524288 | tf_op jit(solution)/shard_map/all_to_all | solution.py:70
Sparse Core Ops, SparseCore 0:
  10.7 79.9 all-gather.1

commit v16 on v12

--- a/solution.py
+++ b/solution.py
@@ -137,7 +137,9 @@
     side_partials = jnp.einsum(
         "kti,io->kto", incoming, panel[:, x_end:], preferred_element_type=jnp.float32
     )
-    side_back = lax.all_to_all(side_partials, "dp", 0, 0)
+    side_shape = side_partials.shape
+    dense = side_partials.reshape(side_shape[0], -1, 128)
+    side_back = lax.all_to_all(dense, "dp", 0, 0).reshape(side_shape)
     x_partials = jnp.einsum(
         "kti,io->kto", incoming, panel[:, :x_end], preferred_element_type=jnp.float32
     )

time: 187 us -> 186 us (level)
    all_to_all x1, waiting for transfers between devices: 4.23 us -> 2.35 us  [shards(): side_back = lax.all_to_all(dense, 'dp', 0, 0).reshape(side_shape)]
where the time goes in v16:
time: 186 us; the launch traced here: 183 us
  blocking collectives  64.5 us (35%)
  waiting for transfers between devices  46.9 us (25%)
  starting transfers between devices  29 us (16%)
  between operations  14.5 us (8%)
  matrix products  13.4 us (7%)
  local copies, waits for them, and re-layouts  8.64 us (5%)
  other arithmetic  5.89 us (3%)
    psum x2, blocking collectives, shards(): totals = lax.psum(lax.psum(powers, CTX), 'dp')  44.6 us
    all_gather x1, blocking collectives, entering(): lax.all_gather(summary.astype(jnp.bfloat16), 'ch').astype(jnp.float32)  19.9 us
    all_to_all x1, waiting for transfers between devices, shards(): x_back = lax.all_to_all(x_partials, 'dp', 0, 0)  12.4 us
    all_to_all x1, waiting for transfers between devices, shards(): incoming = lax.all_to_all(outgoing, 'dp', 0, 0)  9.16 us
    all_to_all x1, waiting for transfers between devices, entering(): incoming = lax.all_to_all(outgoing, 'cl', 0, 0).astype(jnp.float32)  7.95 us
    all_gather x1, waiting for transfers between devices, shards(): panel = lax.all_gather(local_panel, CTX, axis=0, tiled=True)  7.81 us
    all_to_all x1, starting transfers between devices, shards(): incoming = lax.all_to_all(outgoing, 'dp', 0, 0)  7.28 us
    all_to_all x1, starting transfers between devices, shards(): x_back = lax.all_to_all(x_partials, 'dp', 0, 0)  5.67 us
  transfers between devices with their start and end apart: 9, of which 7 were waited for; matrix products, arithmetic and copies ran while one was open for 9% of the time, Pallas kernels for 0%

profile of v16, /device:TPU:6, one launch (start us, length us, event | category | flops | bytes accessed | tf_op | source)
XLA Modules:
  0.0 182.9 jit_solution(3156502679975944739)
XLA Ops:
  8.0 1.6 pad_maximum_fusion.2
  9.6 1.6 copy.123
  12.1 3.3 %multiply_convert_fusion = bf16[128,64,64]{0,2,1:T(8,128)(2,1)S(1)} fusion(f32[128,64,64]{0,1,2:T(8,128)S(1)} %convolution_bitcast_fusion), kind=kOutput, calls=%fused_computation.4 | convolution fusion | flops 403791872 | bytes 3145728 | tf_op jit(solution)/shard_map/tcb,bd->tcd/dot_general | solution.py:106
  15.8 37.0 %psum.14 = f32[4,512]{1,0:T(4,128)S(1)} all-reduce(f32[4,512]{1,0:T(4,128)S(1)} %pad_maximum_fusion.3), channel_id=1, replica_groups=mesh['dp'=4,'ch'=4,'cl'=4,'mp'=8] {'ch','cl'}, use_global_device_ids=true, to_apply=%region_4.0 | all-reduce | flops 2048 | bytes 16384 | tf_op jit(solution)/shard_map/psum | solution.py:123
  52.8 7.6 %psum.15 = f32[4,512]{1,0:T(4,128)S(1)} all-reduce(f32[4,512]{1,0:T(4,128)S(1)} %psum.14), channel_id=1, replica_groups=mesh['dp'=4,'ch'=4,'cl'=4,'mp'=8] {'dp'}, use_global_device_ids=true, to_apply=%region_5.0 | all-reduce | flops 2048 | bytes 16384 | tf_op jit(solution)/shard_map/psum | solution.py:123
  61.0 1.7 collective-permute-start
  62.7 2.1 %collective-permute-done = bf16[8,4096]{1,0:T(8,128)(2,1)S(1)} collective-permute-done((bf16[8,4096]{1,0:T(8,128)(2,1)S(1)}, bf16[8,4096]{1,0:T(8,128)(2,1)S(1)}, u32[]{:S(2)}, u32[]{:S(2)}) %collective-permute-start) | collective-permute-done | bytes 65568 | tf_op jit(solution)/shard_map/ppermute | solution.py:18
  66.1 7.3 %all-to-all-start = ((bf16[4,136,1024]{2,1,0:T(8,128)(2,1)}), bf16[4,136,1024]{2,1,0:T(8,128)(2,1)S(1)}, u32[]{:S(2)}, u32[]{:S(2)}) async-start(bf16[4,136,1024]{2,1,0:T(8,128)(2,1)} %bitcast.106), calls=%async_computation | async-start | bytes 2228224 | tf_op jit(solution)/shard_map/all_to_all | solution.py:134
  73.3 9.2 %all-to-all-done = bf16[4,136,1024]{2,1,0:T(8,128)(2,1)S(1)} async-done(((bf16[4,136,1024]{2,1,0:T(8,128)(2,1)}), bf16[4,136,1024]{2,1,0:T(8,128)(2,1)S(1)}, u32[]{:S(2)}, u32[]{:S(2)}) %all-to-all-start) | async-done | bytes 1114144 | tf_op jit(solution)/shard_map/all_to_all | solution.py:134
  82.5 7.8 %all-gather.2.cloned.1.call-done = bf16[1024,1168]{1,0:T(8,128)(2,1)} async-done(((bf16[64,1168]{1,0:T(8,128)(2,1)}), bf16[1024,1168]{1,0:T(8,128)(2,1)}) %all-gather.2.cloned.1.call-update) | async-done | bytes 2392080 | tf_op jit(solution)/shard_map/all_gather | solution.py:127
  90.3 1.5 fusion.10
  91.8 1.1 reshape.280
  93.0 4.8 %all-to-all-start.2 = ((f32[4,153,128]{2,1,0:T(8,128)}), f32[4,153,128]{2,1,0:T(8,128)S(1)}, u32[]{:S(2)}, u32[]{:S(2)}) async-start(f32[4,153,128]{2,1,0:T(8,128)} %reshape.280), calls=%async_computation.2 | async-start | bytes 655360 | tf_op jit(solution)/shard_map/all_to_all | solution.py:142
  97.8 4.3 %fusion = f32[4,136,1024]{2,1,0:T(8,128)} fusion(bf16[4,136,1024]{2,1,0:T(8,128)(2,1)S(1)} %all-to-all-done, bf16[1024,1168]{1,0:T(8,128)(2,1)} %all-gather.2.cloned.1.call-done), kind=kOutput, calls=%fused_computation.1 | convolution fusion | flops 1140850688 | bytes 5439488 | tf_op jit(solution)/shard_map/kti,io->kto/dot_general | solution.py:143
  102.1 2.4 %all-to-all-done.2 = f32[4,153,128]{2,1,0:T(8,128)S(1)} async-done(((f32[4,153,128]{2,1,0:T(8,128)}), f32[4,153,128]{2,1,0:T(8,128)S(1)}, u32[]{:S(2)}, u32[]{:S(2)}) %all-to-all-start.2) | async-done | bytes 313376 | tf_op jit(solution)/shard_map/all_to_all | solution.py:142
  104.4 5.7 %all-to-all-start.1 = ((f32[4,136,1024]{2,1,0:T(8,128)}), f32[4,136,1024]{2,1,0:T(8,128)S(1)}, u32[]{:S(2)}, u32[]{:S(2)}) async-start(f32[4,136,1024]{2,1,0:T(8,128)} %fusion), calls=%async_computation.1 | async-start | bytes 4456448 | tf_op jit(solution)/shard_map/all_to_all | solution.py:146
  110.4 1.9 %collective-permute-start.1 = (bf16[128,128]{1,0:T(8,128)(2,1)S(1)}, bf16[128,128]{1,0:T(8,128)(2,1)S(1)}, u32[]{:S(2)}, u32[]{:S(2)}) collective-permute-start(bf16[128,128]{1,0:T(8,128)(2,1)S(1)} %multiply_convert_fusion.6), channel_id=1, source_target_pairs={{4,0},{0,1},{5,2},{1,3},{6,4},{2,5},{7,6},{3,7},{12,8},{8,9},{13,1... | collective-permute-start | bytes 98312 | tf_op jit(solution)/shard_map/ppermute | solution.py:175
  113.6 12.4 %all-to-all-done.1 = f32[4,136,1024]{2,1,0:T(8,128)S(1)} async-done(((f32[4,136,1024]{2,1,0:T(8,128)}), f32[4,136,1024]{2,1,0:T(8,128)S(1)}, u32[]{:S(2)}, u32[]{:S(2)}) %all-to-all-start.1) | async-done | bytes 2228256 | tf_op jit(solution)/shard_map/all_to_all | solution.py:146
  127.9 3.4 %all-to-all-start.3 = ((bf16[4,264,128]{2,1,0:T(8,128)(2,1)}), bf16[4,264,128]{2,1,0:T(8,128)(2,1)S(1)}, u32[]{:S(2)}, u32[]{:S(2)}) async-start(bf16[4,264,128]{2,1,0:T(8,128)(2,1)} %pad_maximum_fusion.1), calls=%async_computation.3 | async-start | bytes 540672 | tf_op jit(solution)/shard_map/all_to_all | solution.py:43
  131.6 8.0 %all-to-all-done.3 = bf16[4,264,128]{2,1,0:T(8,128)(2,1)S(1)} async-done(((bf16[4,264,128]{2,1,0:T(8,128)(2,1)}), bf16[4,264,128]{2,1,0:T(8,128)(2,1)S(1)}, u32[]{:S(2)}, u32[]{:S(2)}) %all-to-all-start.3) | async-done | bytes 270368 | tf_op jit(solution)/shard_map/all_to_all | solution.py:43
  140.2 1.2 convolution_bitcast_fusion.1
  141.9 19.9 %all_gather.8 = bf16[4,264,128]{2,1,0:T(8,128)(2,1)S(1)} all-gather(bf16[1,264,128]{2,1,0:T(8,128)(2,1)S(1)} %copy.142), channel_id=1, replica_groups=mesh['dp'=4,'ch'=4,'cl'=4,'mp'=8] {'ch'}, dimensions={0}, use_global_device_ids=true | all-gather | bytes 337920 | tf_op jit(solution)/shard_map/all_gather | solution.py:60
  164.4 3.5 %all-to-all-start.4 = ((bf16[4,256,128]{2,1,0:T(8,128)(2,1)}), bf16[4,256,128]{2,1,0:T(8,128)(2,1)S(1)}, u32[]{:S(2)}, u32[]{:S(2)}) async-start(bf16[4,256,128]{2,1,0:T(8,128)(2,1)} %copy.143), calls=%async_computation.4 | async-start | bytes 524288 | tf_op jit(solution)/shard_map/all_to_all | solution.py:70
  169.7 5.1 %all-to-all-done.4 = bf16[4,256,128]{2,1,0:T(8,128)(2,1)S(1)} async-done(((bf16[4,256,128]{2,1,0:T(8,128)(2,1)}), bf16[4,256,128]{2,1,0:T(8,128)(2,1)S(1)}, u32[]{:S(2)}, u32[]{:S(2)}) %all-to-all-start.4) | async-done | bytes 262176 | tf_op jit(solution)/shard_map/all_to_all | solution.py:70
  (93 shorter events, 14.0 us)
Async XLA Ops:
  7.2 83.1 %all-gather.2.cloned.1.call-start = ((), (), s32[]{:S(2)}) async-start(), calls=%async_computation.5 | async-start | bytes 2785280 | tf_op jit(solution)/shard_map/all_gather | solution.py:127
  61.0 3.9 %collective-permute-start = (bf16[8,4096]{1,0:T(8,128)(2,1)S(1)}, bf16[8,4096]{1,0:T(8,128)(2,1)S(1)}, u32[]{:S(2)}, u32[]{:S(2)}) collective-permute-start(bf16[8,4096]{1,0:T(8,128)(2,1)S(1)} %slice.197), channel_id=1, source_target_pairs={{0,8},{8,16},{16,24},{24,32},{32,40},{40,48},{48,56},{56,64},{64,7... | collective-permute-start | bytes 196616 | tf_op jit(solution)/shard_map/ppermute | solution.py:18
  64.9 8.4 %copy-start.5 = (f32[16]{0:T(128)S(1)}, f32[16]{0:T(128)}, u32[]{:S(2)}) copy-start(f32[16]{0:T(128)} %param.19) | copy-start | bytes 196
  66.1 16.4 %all-to-all-start = ((bf16[4,136,1024]{2,1,0:T(8,128)(2,1)}), bf16[4,136,1024]{2,1,0:T(8,128)(2,1)S(1)}, u32[]{:S(2)}, u32[]{:S(2)}) async-start(bf16[4,136,1024]{2,1,0:T(8,128)(2,1)} %bitcast.106), calls=%async_computation | async-start | bytes 2228224 | tf_op jit(solution)/shard_map/all_to_all | solution.py:134
  93.0 11.4 %all-to-all-start.2 = ((f32[4,153,128]{2,1,0:T(8,128)}), f32[4,153,128]{2,1,0:T(8,128)S(1)}, u32[]{:S(2)}, u32[]{:S(2)}) async-start(f32[4,153,128]{2,1,0:T(8,128)} %reshape.280), calls=%async_computation.2 | async-start | bytes 655360 | tf_op jit(solution)/shard_map/all_to_all | solution.py:142
  102.0 8.0 %copy-start.3 = (f32[5,128]{1,0:T(8,128)S(1)}, f32[5,128]{1,0:T(8,128)}, u32[]{:S(2)}) copy-start(f32[5,128]{1,0:T(8,128)} %param.17) | copy-start | bytes 7684
  102.0 8.0 %copy-start = (f32[5,1024]{1,0:T(8,128)S(1)}, f32[5,1024]{1,0:T(8,128)}, u32[]{:S(2)}) copy-start(f32[5,1024]{1,0:T(8,128)} %param.16) | copy-start | bytes 61444
  102.0 11.0 %copy-start.2 = (f32[16]{0:T(128)S(1)}, f32[16]{0:T(128)}, u32[]{:S(2)}) copy-start(f32[16]{0:T(128)} %param.18) | copy-start | bytes 196
  104.4 21.7 %all-to-all-start.1 = ((f32[4,136,1024]{2,1,0:T(8,128)}), f32[4,136,1024]{2,1,0:T(8,128)S(1)}, u32[]{:S(2)}, u32[]{:S(2)}) async-start(f32[4,136,1024]{2,1,0:T(8,128)} %fusion), calls=%async_computation.1 | async-start | bytes 4456448 | tf_op jit(solution)/shard_map/all_to_all | solution.py:146
  110.4 16.5 %collective-permute-start.1 = (bf16[128,128]{1,0:T(8,128)(2,1)S(1)}, bf16[128,128]{1,0:T(8,128)(2,1)S(1)}, u32[]{:S(2)}, u32[]{:S(2)}) collective-permute-start(bf16[128,128]{1,0:T(8,128)(2,1)S(1)} %multiply_convert_fusion.6), channel_id=1, source_target_pairs={{4,0},{0,1},{5,2},{1,3},{6,4},{2,5},{7,6},{3,7},{12,8},{8,9},{13,1... | collective-permute-start | bytes 98312 | tf_op jit(solution)/shard_map/ppermute | solution.py:175
  112.3 14.6 %collective-permute-start.2 = (bf16[128,128]{1,0:T(8,128)(2,1)S(1)}, bf16[128,128]{1,0:T(8,128)(2,1)S(1)}, u32[]{:S(2)}, u32[]{:S(2)}) collective-permute-start(bf16[128,128]{1,0:T(8,128)(2,1)S(1)} %multiply_convert_fusion.6), channel_id=1, source_target_pairs={{0,0},{4,1},{1,2},{5,3},{2,4},{6,5},{3,6},{7,7},{8,8},{12,9},{9,10... | collective-permute-start | bytes 98312 | tf_op jit(solution)/shard_map/ppermute | solution.py:174
  127.9 11.7 %all-to-all-start.3 = ((bf16[4,264,128]{2,1,0:T(8,128)(2,1)}), bf16[4,264,128]{2,1,0:T(8,128)(2,1)S(1)}, u32[]{:S(2)}, u32[]{:S(2)}) async-start(bf16[4,264,128]{2,1,0:T(8,128)(2,1)} %pad_maximum_fusion.1), calls=%async_computation.3 | async-start | bytes 540672 | tf_op jit(solution)/shard_map/all_to_all | solution.py:43
  141.9 26.7 %copy-start.1 = (f32[1024]{0:T(1024)S(1)}, f32[1024]{0:T(1024)}, u32[]{:S(2)}) copy-start(f32[1024]{0:T(1024)} %param.21) | copy-start | bytes 12292
  164.4 10.3 %copy-start.4 = (f32[16]{0:T(128)S(1)}, f32[16]{0:T(128)}, u32[]{:S(2)}) copy-start(f32[16]{0:T(128)} %param.20) | copy-start | bytes 196
  164.4 10.3 %all-to-all-start.4 = ((bf16[4,256,128]{2,1,0:T(8,128)(2,1)}), bf16[4,256,128]{2,1,0:T(8,128)(2,1)S(1)}, u32[]{:S(2)}, u32[]{:S(2)}) async-start(bf16[4,256,128]{2,1,0:T(8,128)(2,1)} %copy.143), calls=%async_computation.4 | async-start | bytes 524288 | tf_op jit(solution)/shard_map/all_to_all | solution.py:70
Sparse Core Ops, SparseCore 0:
  10.7 79.6 all-gather.1

commit v17 on v16

--- a/solution.py
+++ b/solution.py
@@ -138,8 +138,17 @@
         "kti,io->kto", incoming, panel[:, x_end:], preferred_element_type=jnp.float32
     )
     side_shape = side_partials.shape
-    dense = side_partials.reshape(side_shape[0], -1, 128)
-    side_back = lax.all_to_all(dense, "dp", 0, 0).reshape(side_shape)
+    lead_cols = side_shape[2] - side_shape[2] % 128
+    tail_rows = side_partials[:, :, lead_cols:].reshape(side_shape[0], -1, 128)
+    dense = jnp.concatenate([side_partials[:, :, :lead_cols], tail_rows], 1)
+    arrived = lax.all_to_all(dense, "dp", 0, 0)
+    side_back = jnp.concatenate(
+        [
+            arrived[:, : side_shape[1]],
+            arrived[:, side_shape[1] :].reshape(side_shape[0], side_shape[1], -1),
+        ],
+        2,
+    )
     x_partials = jnp.einsum(
         "kti,io->kto", incoming, panel[:, :x_end], preferred_element_type=jnp.float32
     )

time: 186 us -> 186 us (level)
  no operation moved by 1% of the time
where the time goes in v17:
time: 186 us; the launch traced here: 183 us
  blocking collectives  66 us (35%)
  waiting for transfers between devices  45.2 us (24%)
  starting transfers between devices  29 us (16%)
  between operations  14.5 us (8%)
  matrix products  13.5 us (7%)
  local copies, waits for them, and re-layouts  7.75 us (4%)
  other arithmetic  6.8 us (4%)
    psum x2, blocking collectives, shards(): totals = lax.psum(lax.psum(powers, CTX), 'dp')  44.6 us
    all_gather x1, blocking collectives, entering(): lax.all_gather(summary.astype(jnp.bfloat16), 'ch').astype(jnp.float32)  21.4 us
    all_to_all x1, waiting for transfers between devices, shards(): x_back = lax.all_to_all(x_partials, 'dp', 0, 0)  12.2 us
    all_to_all x1, waiting for transfers between devices, shards(): incoming = lax.all_to_all(outgoing, 'dp', 0, 0)  9.16 us
    all_gather x1, waiting for transfers between devices, shards(): panel = lax.all_gather(local_panel, CTX, axis=0, tiled=True)  7.81 us
    all_to_all x1, starting transfers between devices, shards(): incoming = lax.all_to_all(outgoing, 'dp', 0, 0)  7.28 us
    all_to_all x1, waiting for transfers between devices, entering(): incoming = lax.all_to_all(outgoing, 'cl', 0, 0).astype(jnp.float32)  6.53 us
    all_to_all x1, starting transfers between devices, shards(): x_back = lax.all_to_all(x_partials, 'dp', 0, 0)  5.67 us
  transfers between devices with their start and end apart: 9, of which 7 were waited for; matrix products, arithmetic and copies ran while one was open for 9% of the time, Pallas kernels for 0%

profile of v17, /device:TPU:6, one launch (start us, length us, event | category | flops | bytes accessed | tf_op | source)
XLA Modules:
  0.0 182.8 jit_solution(8465596909689969975)
XLA Ops:
  8.0 1.6 pad_maximum_fusion.3
  9.6 1.6 copy.123
  12.1 3.3 %multiply_convert_fusion = bf16[128,64,64]{0,2,1:T(8,128)(2,1)S(1)} fusion(f32[128,64,64]{0,1,2:T(8,128)S(1)} %convolution_bitcast_fusion), kind=kOutput, calls=%fused_computation.4 | convolution fusion | flops 403791872 | bytes 3145728 | tf_op jit(solution)/shard_map/tcb,bd->tcd/dot_general | solution.py:106
  15.8 37.0 %psum.14 = f32[4,512]{1,0:T(4,128)S(1)} all-reduce(f32[4,512]{1,0:T(4,128)S(1)} %pad_maximum_fusion.4), channel_id=1, replica_groups=mesh['dp'=4,'ch'=4,'cl'=4,'mp'=8] {'ch','cl'}, use_global_device_ids=true, to_apply=%region_4.0 | all-reduce | flops 2048 | bytes 16384 | tf_op jit(solution)/shard_map/psum | solution.py:123
  52.8 7.6 %psum.15 = f32[4,512]{1,0:T(4,128)S(1)} all-reduce(f32[4,512]{1,0:T(4,128)S(1)} %psum.14), channel_id=1, replica_groups=mesh['dp'=4,'ch'=4,'cl'=4,'mp'=8] {'dp'}, use_global_device_ids=true, to_apply=%region_5.0 | all-reduce | flops 2048 | bytes 16384 | tf_op jit(solution)/shard_map/psum | solution.py:123
  61.0 1.7 collective-permute-start
  62.7 2.1 %collective-permute-done = bf16[8,4096]{1,0:T(8,128)(2,1)S(1)} collective-permute-done((bf16[8,4096]{1,0:T(8,128)(2,1)S(1)}, bf16[8,4096]{1,0:T(8,128)(2,1)S(1)}, u32[]{:S(2)}, u32[]{:S(2)}) %collective-permute-start) | collective-permute-done | bytes 65568 | tf_op jit(solution)/shard_map/ppermute | solution.py:18
  65.0 1.1 copy.171
  66.1 7.3 %all-to-all-start = ((bf16[4,136,1024]{2,1,0:T(8,128)(2,1)}), bf16[4,136,1024]{2,1,0:T(8,128)(2,1)S(1)}, u32[]{:S(2)}, u32[]{:S(2)}) async-start(bf16[4,136,1024]{2,1,0:T(8,128)(2,1)} %bitcast.106), calls=%async_computation | async-start | bytes 2228224 | tf_op jit(solution)/shard_map/all_to_all | solution.py:134
  73.3 9.2 %all-to-all-done = bf16[4,136,1024]{2,1,0:T(8,128)(2,1)S(1)} async-done(((bf16[4,136,1024]{2,1,0:T(8,128)(2,1)}), bf16[4,136,1024]{2,1,0:T(8,128)(2,1)S(1)}, u32[]{:S(2)}, u32[]{:S(2)}) %all-to-all-start) | async-done | bytes 1114144 | tf_op jit(solution)/shard_map/all_to_all | solution.py:134
  82.5 7.8 %all-gather.2.cloned.1.call-done = bf16[1024,1168]{1,0:T(8,128)(2,1)} async-done(((bf16[64,1168]{1,0:T(8,128)(2,1)}), bf16[1024,1168]{1,0:T(8,128)(2,1)}) %all-gather.2.cloned.1.call-update) | async-done | bytes 2392080 | tf_op jit(solution)/shard_map/all_gather | solution.py:127
  90.3 1.5 fusion.10
  92.8 4.8 %all-to-all-start.2 = ((f32[4,153,128]{2,1,0:T(8,128)}), f32[4,153,128]{2,1,0:T(8,128)S(1)}, u32[]{:S(2)}, u32[]{:S(2)}) async-start(f32[4,153,128]{2,1,0:T(8,128)} %pad_maximum_fusion.1), calls=%async_computation.2 | async-start | bytes 655360 | tf_op jit(solution)/shard_map/all_to_all | solution.py:144
  97.6 4.3 %fusion = f32[4,136,1024]{2,1,0:T(8,128)} fusion(bf16[4,136,1024]{2,1,0:T(8,128)(2,1)S(1)} %all-to-all-done, bf16[1024,1168]{1,0:T(8,128)(2,1)} %all-gather.2.cloned.1.call-done), kind=kOutput, calls=%fused_computation.1 | convolution fusion | flops 1140850688 | bytes 5439488 | tf_op jit(solution)/shard_map/kti,io->kto/dot_general | solution.py:152
  101.9 2.4 %all-to-all-done.2 = f32[4,153,128]{2,1,0:T(8,128)S(1)} async-done(((f32[4,153,128]{2,1,0:T(8,128)}), f32[4,153,128]{2,1,0:T(8,128)S(1)}, u32[]{:S(2)}, u32[]{:S(2)}) %all-to-all-start.2) | async-done | bytes 313376 | tf_op jit(solution)/shard_map/all_to_all | solution.py:144
  104.2 5.7 %all-to-all-start.1 = ((f32[4,136,1024]{2,1,0:T(8,128)}), f32[4,136,1024]{2,1,0:T(8,128)S(1)}, u32[]{:S(2)}, u32[]{:S(2)}) async-start(f32[4,136,1024]{2,1,0:T(8,128)} %fusion), calls=%async_computation.1 | async-start | bytes 4456448 | tf_op jit(solution)/shard_map/all_to_all | solution.py:155
  110.5 1.9 %collective-permute-start.1 = (bf16[128,128]{0,1:T(8,128)(2,1)S(1)}, bf16[128,128]{0,1:T(8,128)(2,1)S(1)}, u32[]{:S(2)}, u32[]{:S(2)}) collective-permute-start(bf16[128,128]{0,1:T(8,128)(2,1)S(1)} %multiply_convert_fusion.6), channel_id=1, source_target_pairs={{4,0},{0,1},{5,2},{1,3},{6,4},{2,5},{7,6},{3,7},{12,8},{8,9},{13,1... | collective-permute-start | bytes 98312 | tf_op jit(solution)/shard_map/ppermute | solution.py:184
  113.7 12.2 %all-to-all-done.1 = f32[4,136,1024]{2,1,0:T(8,128)S(1)} async-done(((f32[4,136,1024]{2,1,0:T(8,128)}), f32[4,136,1024]{2,1,0:T(8,128)S(1)}, u32[]{:S(2)}, u32[]{:S(2)}) %all-to-all-start.1) | async-done | bytes 2228256 | tf_op jit(solution)/shard_map/all_to_all | solution.py:155
  127.7 3.4 %all-to-all-start.3 = ((bf16[4,264,128]{2,1,0:T(8,128)(2,1)}), bf16[4,264,128]{2,1,0:T(8,128)(2,1)S(1)}, u32[]{:S(2)}, u32[]{:S(2)}) async-start(bf16[4,264,128]{2,1,0:T(8,128)(2,1)} %pad_maximum_fusion.2), calls=%async_computation.3 | async-start | bytes 540672 | tf_op jit(solution)/shard_map/all_to_all | solution.py:43
  131.4 6.5 %all-to-all-done.3 = bf16[4,264,128]{2,1,0:T(8,128)(2,1)S(1)} async-done(((bf16[4,264,128]{2,1,0:T(8,128)(2,1)}), bf16[4,264,128]{2,1,0:T(8,128)(2,1)S(1)}, u32[]{:S(2)}, u32[]{:S(2)}) %all-to-all-start.3) | async-done | bytes 270368 | tf_op jit(solution)/shard_map/all_to_all | solution.py:43
  138.6 1.2 convolution_bitcast_fusion.1
  140.3 21.4 %all_gather.8 = bf16[4,264,128]{2,1,0:T(8,128)(2,1)S(1)} all-gather(bf16[1,264,128]{2,1,0:T(8,128)(2,1)S(1)} %copy.143), channel_id=1, replica_groups=mesh['dp'=4,'ch'=4,'cl'=4,'mp'=8] {'ch'}, dimensions={0}, use_global_device_ids=true | all-gather | bytes 337920 | tf_op jit(solution)/shard_map/all_gather | solution.py:60
  164.3 3.5 %all-to-all-start.4 = ((bf16[4,256,128]{2,1,0:T(8,128)(2,1)}), bf16[4,256,128]{2,1,0:T(8,128)(2,1)S(1)}, u32[]{:S(2)}, u32[]{:S(2)}) async-start(bf16[4,256,128]{2,1,0:T(8,128)(2,1)} %copy.144), calls=%async_computation.4 | async-start | bytes 524288 | tf_op jit(solution)/shard_map/all_to_all | solution.py:70
  169.5 5.0 %all-to-all-done.4 = bf16[4,256,128]{2,1,0:T(8,128)(2,1)S(1)} async-done(((bf16[4,256,128]{2,1,0:T(8,128)(2,1)}), bf16[4,256,128]{2,1,0:T(8,128)(2,1)S(1)}, u32[]{:S(2)}, u32[]{:S(2)}) %all-to-all-start.4) | async-done | bytes 262176 | tf_op jit(solution)/shard_map/all_to_all | solution.py:70
  (98 shorter events, 14.2 us)
Async XLA Ops:
  7.2 83.1 %all-gather.2.cloned.1.call-start = ((), (), s32[]{:S(2)}) async-start(), calls=%async_computation.5 | async-start | bytes 2785280 | tf_op jit(solution)/shard_map/all_gather | solution.py:127
  61.0 3.9 %collective-permute-start = (bf16[8,4096]{1,0:T(8,128)(2,1)S(1)}, bf16[8,4096]{1,0:T(8,128)(2,1)S(1)}, u32[]{:S(2)}, u32[]{:S(2)}) collective-permute-start(bf16[8,4096]{1,0:T(8,128)(2,1)S(1)} %slice.213), channel_id=1, source_target_pairs={{0,8},{8,16},{16,24},{24,32},{32,40},{40,48},{48,56},{56,64},{64,7... | collective-permute-start | bytes 196616 | tf_op jit(solution)/shard_map/ppermute | solution.py:18
  64.9 8.4 %copy-start.5 = (f32[16]{0:T(128)S(1)}, f32[16]{0:T(128)}, u32[]{:S(2)}) copy-start(f32[16]{0:T(128)} %param.19) | copy-start | bytes 196
  66.1 16.4 %all-to-all-start = ((bf16[4,136,1024]{2,1,0:T(8,128)(2,1)}), bf16[4,136,1024]{2,1,0:T(8,128)(2,1)S(1)}, u32[]{:S(2)}, u32[]{:S(2)}) async-start(bf16[4,136,1024]{2,1,0:T(8,128)(2,1)} %bitcast.106), calls=%async_computation | async-start | bytes 2228224 | tf_op jit(solution)/shard_map/all_to_all | solution.py:134
  92.8 11.4 %all-to-all-start.2 = ((f32[4,153,128]{2,1,0:T(8,128)}), f32[4,153,128]{2,1,0:T(8,128)S(1)}, u32[]{:S(2)}, u32[]{:S(2)}) async-start(f32[4,153,128]{2,1,0:T(8,128)} %pad_maximum_fusion.1), calls=%async_computation.2 | async-start | bytes 655360 | tf_op jit(solution)/shard_map/all_to_all | solution.py:144
  101.9 8.0 %copy-start.3 = (f32[5,128]{1,0:T(8,128)S(1)}, f32[5,128]{1,0:T(8,128)}, u32[]{:S(2)}) copy-start(f32[5,128]{1,0:T(8,128)} %param.17) | copy-start | bytes 7684
  101.9 8.0 %copy-start = (f32[5,1024]{1,0:T(8,128)S(1)}, f32[5,1024]{1,0:T(8,128)}, u32[]{:S(2)}) copy-start(f32[5,1024]{1,0:T(8,128)} %param.16) | copy-start | bytes 61444
  101.9 11.3 %copy-start.2 = (f32[16]{0:T(128)S(1)}, f32[16]{0:T(128)}, u32[]{:S(2)}) copy-start(f32[16]{0:T(128)} %param.18) | copy-start | bytes 196
  104.2 21.7 %all-to-all-start.1 = ((f32[4,136,1024]{2,1,0:T(8,128)}), f32[4,136,1024]{2,1,0:T(8,128)S(1)}, u32[]{:S(2)}, u32[]{:S(2)}) async-start(f32[4,136,1024]{2,1,0:T(8,128)} %fusion), calls=%async_computation.1 | async-start | bytes 4456448 | tf_op jit(solution)/shard_map/all_to_all | solution.py:155
  110.5 16.1 %collective-permute-start.1 = (bf16[128,128]{0,1:T(8,128)(2,1)S(1)}, bf16[128,128]{0,1:T(8,128)(2,1)S(1)}, u32[]{:S(2)}, u32[]{:S(2)}) collective-permute-start(bf16[128,128]{0,1:T(8,128)(2,1)S(1)} %multiply_convert_fusion.6), channel_id=1, source_target_pairs={{4,0},{0,1},{5,2},{1,3},{6,4},{2,5},{7,6},{3,7},{12,8},{8,9},{13,1... | collective-permute-start | bytes 98312 | tf_op jit(solution)/shard_map/ppermute | solution.py:184
  112.5 14.2 %collective-permute-start.2 = (bf16[128,128]{0,1:T(8,128)(2,1)S(1)}, bf16[128,128]{0,1:T(8,128)(2,1)S(1)}, u32[]{:S(2)}, u32[]{:S(2)}) collective-permute-start(bf16[128,128]{0,1:T(8,128)(2,1)S(1)} %multiply_convert_fusion.6), channel_id=1, source_target_pairs={{0,0},{4,1},{1,2},{5,3},{2,4},{6,5},{3,6},{7,7},{8,8},{12,9},{9,10... | collective-permute-start | bytes 98312 | tf_op jit(solution)/shard_map/ppermute | solution.py:183
  127.7 10.3 %all-to-all-start.3 = ((bf16[4,264,128]{2,1,0:T(8,128)(2,1)}), bf16[4,264,128]{2,1,0:T(8,128)(2,1)S(1)}, u32[]{:S(2)}, u32[]{:S(2)}) async-start(bf16[4,264,128]{2,1,0:T(8,128)(2,1)} %pad_maximum_fusion.2), calls=%async_computation.3 | async-start | bytes 540672 | tf_op jit(solution)/shard_map/all_to_all | solution.py:43
  140.3 28.1 %copy-start.1 = (f32[1024]{0:T(1024)S(1)}, f32[1024]{0:T(1024)}, u32[]{:S(2)}) copy-start(f32[1024]{0:T(1024)} %param.21) | copy-start | bytes 12292
  164.3 10.3 %copy-start.4 = (f32[16]{0:T(128)S(1)}, f32[16]{0:T(128)}, u32[]{:S(2)}) copy-start(f32[16]{0:T(128)} %param.20) | copy-start | bytes 196
  164.3 10.3 %all-to-all-start.4 = ((bf16[4,256,128]{2,1,0:T(8,128)(2,1)}), bf16[4,256,128]{2,1,0:T(8,128)(2,1)S(1)}, u32[]{:S(2)}, u32[]{:S(2)}) async-start(bf16[4,256,128]{2,1,0:T(8,128)(2,1)} %copy.144), calls=%async_computation.4 | async-start | bytes 524288 | tf_op jit(solution)/shard_map/all_to_all | solution.py:70
Sparse Core Ops, SparseCore 0:
  10.7 79.6 all-gather.1
